TPU v7x, 128 devices: a whole 4x4x4 slice. The times are simulated.
128 devices in a mesh: src: 8 (over z, core), dst: 16 (over x, y).
Axes of the slice: x: 4, y: 4, z: 4, core: 2. Of those that a mesh axis runs over, the one named last changes fastest.
Arguments:
- slab_blocks: bfloat16 [1536, 64, 4096], P(('src', 'dst')), may hold values from -6 to 6
- owner_column: int32 [1536, 1], P(('src', 'dst')), may hold values from 0 to 15; in each aligned block of 12 rows (0 to 11, 12 to 23, ...) at most 3 rows name the same one
- block_row: int32 [1536], P(('src', 'dst')), may hold values from 0 to 3
- block_col: int32 [1536], P(('src', 'dst')), may hold values from 0 to 63
- factor_dst: bfloat16 [65536, 256], P('dst'), may hold values from -0.015136719 to 0.04248047
- factor_slab: bfloat16 [64, 256], replicated, may hold values from -0.0625 to 0.125
- factor_old: float32 [2048, 256], P(('src', 'dst')), may hold values from -6 to 6
Outputs:
- factor_new: float32 [2048, 256], P(('src', 'dst'))
Inputs may be any that keep to these rules, and one draw needn't show every extreme that they name: `owner_column`: among one device's 12 blocks, at most 3 name the same owner, a bound that some block reaches.
All inputs are finite; a program needn't handle non-finite values.
Results may differ from a plain program's by a relative error of at most 0.0024.
Values may be sent and summed in bfloat16 or wider, within the bound.
No kernel may reach another device: no remote copies, remote signals or barrier semaphores. Data moves between devices by JAX's collectives and lax.ppermute only.
A program may use at most 192 MiB of HBM per device.

v0:
```python
import jax
import jax.numpy as jnp
from jax import lax
from jax.sharding import PartitionSpec as P

RIDGE = 0.1


def block_terms(blocks, left, factor_slab):
    slab = factor_slab.astype(jnp.float32)
    edge = left.shape[1]
    width = left.shape[2]
    total = blocks.shape[0]

    def one_pair(pair):
        tiles, rows_left = pair
        khatri = rows_left.astype(jnp.float32)[:, :, None, :] * slab[None, None, :, :]
        khatri = khatri.reshape(rows_left.shape[0], edge * slab.shape[0], width).astype(
            jnp.bfloat16
        )
        return jnp.einsum("gak,gkr->gar", tiles, khatri, preferred_element_type=jnp.float32)

    grouped = (
        blocks.reshape(total // 2, 2, blocks.shape[1], blocks.shape[2]),
        left.reshape(total // 2, 2, edge, width),
    )
    return lax.map(one_pair, grouped).reshape(total, edge, width)


def shards(slab_blocks, owner_column, block_row, block_col, factor_dst, factor_slab, factor_old):
    peers = lax.axis_size("dst")
    count = slab_blocks.shape[0]
    edge = slab_blocks.shape[1]
    width = factor_dst.shape[1]
    depth = max(2, 4 * count // peers)
    owners = owner_column[:, 0]
    order = jnp.arange(count, dtype=jnp.int32)
    same = (owners[:, None] == owners[None, :]) & (order[None, :] < order[:, None])
    places = owners * depth + jnp.sum(same.astype(jnp.int32), axis=1)
    slot_ids = jnp.arange(peers * depth, dtype=jnp.int32)
    match = places[None, :] == slot_ids[:, None]
    sources = jnp.sum(jnp.where(match, order[None, :], 0), axis=1) + jnp.where(
        jnp.any(match, axis=1), 0, count
    )
    tiles_dst = factor_dst.reshape(factor_dst.shape[0] // edge, edge, width)
    zero_index = jnp.zeros((1,), jnp.int32)
    col_padded = jnp.concatenate([block_col, zero_index])
    padded = jnp.concatenate(
        [slab_blocks, jnp.zeros((1, edge, slab_blocks.shape[2]), slab_blocks.dtype)]
    )
    row_padded = jnp.concatenate([block_row, zero_index])
    outgoing = padded[sources].reshape(peers, depth, edge, slab_blocks.shape[2])
    labels = jnp.stack([row_padded[sources], col_padded[sources]], axis=1).reshape(peers, depth, 2)
    arrived, arrived_labels = (
        lax.all_to_all(outgoing, "dst", split_axis=0, concat_axis=0, tiled=True),
        lax.all_to_all(labels, "dst", split_axis=0, concat_axis=0, tiled=True),
    )
    arrived_labels = arrived_labels.reshape(peers * depth, 2)
    left = tiles_dst[arrived_labels[:, 1]]
    terms = block_terms(
        arrived.reshape(peers * depth, edge, slab_blocks.shape[2]), left, factor_slab
    )
    targets = arrived_labels[:, 0]
    blocks_src = factor_old.shape[0] * peers // edge
    onehot = (targets[:, None] == jnp.arange(blocks_src, dtype=jnp.int32)[None, :]).astype(
        jnp.float32
    )
    partial_sum = jnp.einsum("sb,sar->bar", onehot, terms, precision=lax.Precision.HIGHEST)
    partial_sum = partial_sum.reshape(blocks_src * edge, width)
    summed_rows = lax.psum_scatter(partial_sum, "dst", scatter_dimension=0, tiled=True)
    local_gram = jnp.dot(factor_dst.T, factor_dst, preferred_element_type=jnp.float32)
    gram_left = lax.psum(local_gram, "dst")
    gram_right = jnp.dot(factor_slab.T, factor_slab, preferred_element_type=jnp.float32)
    gram = gram_left * gram_right + RIDGE * jnp.eye(width, dtype=jnp.float32)
    lower = jnp.linalg.cholesky(gram)
    target = summed_rows + RIDGE * factor_old
    return jax.scipy.linalg.cho_solve((lower, True), target.T).T


def solution(mesh):
    placed = (
        P(("src", "dst"), None, None),
        P(("src", "dst"), None),
        P(("src", "dst")),
        P(("src", "dst")),
        P("dst", None),
        P(),
        P(("src", "dst"), None),
    )
    return jax.shard_map(
        shards, mesh=mesh, in_specs=placed, out_specs=P(("src", "dst"), None), check_vma=False
    )
```

profile of v0, /device:TPU:0, one launch (start us, length us, event | category | flops | bytes accessed | tf_op | source)
XLA Modules:
  0.0 750.0 jit_solution(8270128834084861796)
XLA Ops:
  6.5 1.0 convert_reduce_fusion
  11.5 7.1 all-to-all-start
  18.7 6.5 concatenate.18
  25.2 12.6 %gather_fusion.2 = bf16[48,64,4096]{2,1,0:T(8,128)(2,1)} fusion(bf16[13,64,4096]{2,1,0:T(8,128)(2,1)} %concatenate.18, s32[1024]{0:T(1024)S(1)} %pad_clamp_fusion.1), kind=kCustom, calls=%fused_computation.2 | custom fusion | bytes 50331840 | tf_op jit(solution)/shard_map/gather | solution.py:52
  37.8 7.3 all-to-all-start.1
  45.1 1.7 fusion.27
  47.2 1.9 gather_fusion.3
  49.1 426.2 %all-reduce.4.cloned.1.call-done = f32[256,256]{0,1:T(8,128)} async-done(((f32[256,256]{0,1:T(8,128)}), f32[256,256]{0,1:T(8,128)}) %all-reduce.4.cloned.1.call-update) | async-done | bytes 262160 | tf_op jit(solution)/shard_map/psum | solution.py:72
  475.3 1.2 fusion.7
  476.7 11.7 %cholesky.49 = f32[128,128]{1,0:T(8,128)S(1)} custom-call(f32[128,128]{1,0:T(8,128)S(1)} %cholesky.115), custom_call_target="Cholesky" | custom-call | tf_op jit(solution)/shard_map/jit(cholesky)/cholesky | solution.py:75
  488.6 9.8 %custom-call.18 = f32[1,128,128]{1,2,0:T(8,128)S(1)} custom-call(f32[1,128,128]{2,1,0:T(8,128)S(1)} %get-tuple-element.78), custom_call_target="InvertDiagBlocksLowerTriangular" | custom-call | tf_op jit(solution)/shard_map/jit(cholesky)/cholesky | solution.py:75
  499.0 11.7 %cholesky.103 = f32[128,128]{1,0:T(8,128)S(1)} custom-call(f32[128,128]{1,0:T(8,128)S(1)} %convolution_subtract_fusion), custom_call_target="Cholesky" | custom-call | tf_op jit(solution)/shard_map/jit(cholesky)/cholesky | solution.py:75
  512.8 113.2 %while.11 = (s32[]{:T(128)}, f32[24,2,64,256]{3,2,1,0:T(8,128)}, bf16[24,2,64,4096]{3,2,1,0:T(8,128)(2,1)}, bf16[24,2,64,256]{3,2,1,0:T(8,128)(2,1)}, f32[64,256]{1,0:T(8,128)S(1)}, /*index=5*/s32[]{:T(128)}) while((s32[]{:T(128)}, f32[24,2,64,256]{3,2,1,0:T(8,128)}, bf16[24,2,64,4096]{3,2,1,0:T(8,128)(2,1)}, ...), condition=%wide.region_9.10_spmd, body=%wide.region_8.9_spmd.sunk | while | flops 272662528 | bytes 18351176 | solution.py:27
  513.0 0.9 bitcast_convert_fusion.2
  515.1 2.7 fusion.48
  519.8 2.7 fusion.48
  522.4 0.8 bitcast_convert_fusion.2
  524.5 2.7 fusion.48
  529.2 2.7 fusion.48
  531.8 0.8 bitcast_convert_fusion.2
  533.9 2.7 fusion.48
  538.6 2.7 fusion.48
  543.3 2.7 fusion.48
  546.0 0.8 bitcast_convert_fusion.2
  548.0 2.7 fusion.48
  552.7 2.7 fusion.48
  557.4 2.7 fusion.48
  560.1 0.8 bitcast_convert_fusion.2
  562.1 2.7 fusion.48
  566.8 2.7 fusion.48
  571.6 2.7 fusion.48
  576.3 2.7 fusion.48
  581.0 2.7 fusion.48
  585.7 2.7 fusion.48
  590.4 2.7 fusion.48
  595.1 2.7 fusion.48
  599.8 2.7 fusion.48
  604.5 2.7 fusion.48
  609.2 2.7 fusion.48
  613.9 2.7 fusion.48
  618.6 2.7 fusion.48
  623.3 2.7 fusion.48
  626.0 4.8 fusion.5
  631.6 4.0 while.12
  632.2 1.3 dynamic-slice.7
  634.3 1.3 dynamic-slice.7
  635.7 19.7 %custom-call.19 = f32[2,128,128]{1,2,0:T(8,128)S(1)} custom-call(f32[2,128,128]{2,1,0:T(8,128)S(1)} %get-tuple-element.40), custom_call_target="InvertDiagBlocksLowerTriangular" | custom-call | tf_op jit(solution)/shard_map/jit(_cho_solve)/triangular_solve | solution.py:77
  655.4 85.3 %reduce-scatter.2.cloned.1.call-done = f32[16,256]{1,0:T(8,128)} async-done(((f32[256,256]{1,0:T(8,128)}), f32[16,256]{1,0:T(8,128)}) %reduce-scatter.2.cloned.1.call-update) | async-done | bytes 16400 | tf_op jit(solution)/shard_map/reduce_scatter | solution.py:70
  (134 shorter events, 54.9 us)
Async XLA Ops:
  6.5 38.6 %copy-start = (bf16[4096,256]{1,0:T(8,128)(2,1)S(1)}, bf16[4096,256]{1,0:T(8,128)(2,1)}, u32[]{:S(2)}) copy-start(bf16[4096,256]{1,0:T(8,128)(2,1)} %param.13) | copy-start | bytes 6291460
  11.5 26.3 %all-to-all-start = ((s32[16,3,2]{1,2,0:T(2,128)}), s32[16,3,2]{1,2,0:T(2,128)S(1)}, u32[]{:S(2)}, u32[]{:S(2)}) async-start(s32[16,3,2]{1,2,0:T(2,128)} %copy.45), calls=%async_computation | async-start | bytes 32768 | tf_op jit(solution)/shard_map/all_to_all | solution.py:56
  37.8 475.0 %all-to-all-start.1 = ((bf16[16,3,64,4096]{3,2,1,0:T(8,128)(2,1)}), bf16[16,3,64,4096]{3,2,1,0:T(8,128)(2,1)}, u32[]{:S(2)}, u32[]{:S(2)}) async-start(bf16[16,3,64,4096]{3,2,1,0:T(8,128)(2,1)} %bitcast.93), calls=%async_computation.1 | async-start | bytes 50331648 | tf_op jit(solution)/shard_map/all_to_all | solution.py:55
  45.1 2.0 copy-start.2
  45.1 430.3 %all-reduce.4.cloned.1.call-start = ((), (), s32[]{:S(2)}) async-start(), calls=%async_computation.3 | async-start | bytes 524288 | tf_op jit(solution)/shard_map/psum | solution.py:72
  46.8 693.9 %reduce-scatter.2.cloned.1.call-start = ((), (), s32[]{:S(2)}) async-start(), calls=%async_computation.4 | async-start | bytes 278528 | tf_op jit(solution)/shard_map/reduce_scatter | solution.py:70
  626.0 117.2 %copy-start.1 = (bf16[4096,256]{1,0:T(8,128)(2,1)S(1)}, bf16[4096,256]{1,0:T(8,128)(2,1)}, u32[]{:S(2)}) copy-start(bf16[4096,256]{1,0:T(8,128)(2,1)} %param.13) | copy-start | bytes 6291460
  626.0 114.7 %copy-start.3 = (f32[16,256]{1,0:T(8,128)S(1)}, f32[16,256]{1,0:T(8,128)}, u32[]{:S(2)}) copy-start(f32[16,256]{1,0:T(8,128)} %param.15) | copy-start | bytes 49156
Sparse Core Ops, SparseCore 0:
  49.0 426.2 all-reduce.3
  631.7 108.9 reduce-scatter.1
where the time goes:
time: 753 us; the launch traced here: 750 us
  waiting for transfers between devices  512 us (68%)
  other arithmetic  94.1 us (12%)
  matrix products  73.5 us (10%)
  local copies, waits for them, and re-layouts  40.6 us (5%)
  between operations  14.9 us (2%)
  starting transfers between devices  14.7 us (2%)
    psum x1, waiting for transfers between devices, shards(): gram_left = lax.psum(local_gram, 'dst')  426 us
    reduce_scatter x1, waiting for transfers between devices, shards(): lax.psum_scatter(partial_sum, 'dst', scatter_dimension=0, tiled=True)  85.3 us
    dot_general x24, matrix products, one_pair(): jnp.einsum('gak,gkr->gar', tiles, khatri, preferred_element_type=jnp.floa...  64.2 us
    another operation x6, other arithmetic, shards(): lower = jnp.linalg.cholesky(gram)  34 us
    convert_element_type x24, other arithmetic, one_pair(): rows_left.astype(jnp.float32)[:, :, None, :] * slab[None, None, :, :]  20.4 us
    another operation x3, other arithmetic, shards(): return jax.scipy.linalg.cho_solve((lower, True), target.T).T  19.7 us
    convert_element_type x24, other arithmetic, one_pair(): khatri.reshape(rows_left.shape[0], edge * slab.shape[0], width)  16 us
  transfers between devices with their start and end apart: 4, of which 2 were waited for; matrix products, arithmetic and copies ran while one was open for 11% of the time, Pallas kernels for 0%

commit v1 on v0

v1 whole, which is shorter than its diff:
```python
import functools

import jax
import jax.numpy as jnp
from jax import lax
from jax.experimental import pallas as pl
from jax.experimental.pallas import tpu as pltpu
from jax.sharding import PartitionSpec as P

RIDGE = 0.1


def mttkrp_kernel(rows_ref, places_ref, x_ref, left_ref, slab_ref, out_ref, kr_ref):
    step = pl.program_id(0)

    @pl.when(step == 0)
    def _():
        out_ref[...] = jnp.zeros_like(out_ref)

    left = left_ref[0].astype(jnp.float32)
    slab = slab_ref[...].astype(jnp.float32)
    edge = left.shape[0]
    bins = slab.shape[0]
    for b in range(edge):
        kr_ref[pl.ds(b * bins, bins), :] = (left[b : b + 1, :] * slab).astype(kr_ref.dtype)
    prod = jnp.dot(x_ref[0], kr_ref[...], preferred_element_type=jnp.float32)
    row = rows_ref[step]
    out_ref[row] = out_ref[row] + prod


def block_products(slab_blocks, received, places, block_row, factor_slab, row_blocks):
    count, edge, depth_k = slab_blocks.shape
    width = received.shape[2]
    grid_spec = pltpu.PrefetchScalarGridSpec(
        num_scalar_prefetch=2,
        grid=(count,),
        in_specs=[
            pl.BlockSpec((1, edge, depth_k), lambda i, rows, pl_: (i, 0, 0)),
            pl.BlockSpec((1, received.shape[1], width), lambda i, rows, pl_: (pl_[i], 0, 0)),
            pl.BlockSpec(factor_slab.shape, lambda i, rows, pl_: (0, 0)),
        ],
        out_specs=pl.BlockSpec((row_blocks, edge, width), lambda i, rows, pl_: (0, 0, 0)),
        scratch_shapes=[pltpu.VMEM((depth_k, width), jnp.bfloat16)],
    )
    flops = 2 * count * edge * depth_k * width
    return pl.pallas_call(
        mttkrp_kernel,
        grid_spec=grid_spec,
        out_shape=jax.ShapeDtypeStruct((row_blocks, edge, width), jnp.float32),
        compiler_params=pltpu.CompilerParams(
            dimension_semantics=("arbitrary",), vmem_limit_bytes=48 * 1024 * 1024
        ),
        cost_estimate=pl.CostEstimate(
            flops=flops,
            bytes_accessed=slab_blocks.size * 2 + count * edge * width * 2 + row_blocks * edge * width * 4,
            transcendentals=0,
        ),
    )(block_row, places, slab_blocks, received, factor_slab)


def shards(slab_blocks, owner_column, block_row, block_col, factor_dst, factor_slab, factor_old):
    peers = lax.axis_size("dst")
    count = slab_blocks.shape[0]
    edge = slab_blocks.shape[1]
    width = factor_dst.shape[1]
    depth = max(2, 4 * count // peers)
    owners = owner_column[:, 0]
    order = jnp.arange(count, dtype=jnp.int32)
    same = (owners[:, None] == owners[None, :]) & (order[None, :] < order[:, None])
    places = owners * depth + jnp.sum(same.astype(jnp.int32), axis=1)
    slot_ids = jnp.arange(peers * depth, dtype=jnp.int32)
    match = places[None, :] == slot_ids[:, None]
    requests = jnp.sum(jnp.where(match, block_col[None, :], 0), axis=1).reshape(peers, depth)
    asked = lax.all_to_all(requests, "dst", split_axis=0, concat_axis=0, tiled=True)
    tiles_dst = factor_dst.reshape(factor_dst.shape[0] // edge, edge, width)
    outgoing = tiles_dst[asked.reshape(peers * depth)].reshape(peers, depth, edge, width)
    received = lax.all_to_all(outgoing, "dst", split_axis=0, concat_axis=0, tiled=True)
    received = received.reshape(peers * depth, edge, width)

    row_blocks = factor_old.shape[0] * peers // edge
    partial_sum = block_products(slab_blocks, received, places, block_row, factor_slab, row_blocks)
    partial_sum = partial_sum.reshape(row_blocks * edge, width)
    summed_rows = lax.psum_scatter(partial_sum, "dst", scatter_dimension=0, tiled=True)

    local_gram = jnp.dot(factor_dst.T, factor_dst, preferred_element_type=jnp.float32)
    gram_left = lax.psum(local_gram, "dst")
    gram_right = jnp.dot(factor_slab.T, factor_slab, preferred_element_type=jnp.float32)
    gram = gram_left * gram_right + RIDGE * jnp.eye(width, dtype=jnp.float32)
    lower = jnp.linalg.cholesky(gram)
    target = summed_rows + RIDGE * factor_old
    return jax.scipy.linalg.cho_solve((lower, True), target.T).T


def solution(mesh):
    placed = (
        P(("src", "dst"), None, None),
        P(("src", "dst"), None),
        P(("src", "dst")),
        P(("src", "dst")),
        P("dst", None),
        P(),
        P(("src", "dst"), None),
    )
    return jax.shard_map(
        shards, mesh=mesh, in_specs=placed, out_specs=P(("src", "dst"), None), check_vma=False
    )
```

time: 753 us -> 251 us (0.33)
  waiting for transfers between devices: 512 us -> 142 us
  matrix products: 73.5 us -> 4.43 us
  other arithmetic: 94.1 us -> 58.2 us
  local copies, waits for them, and re-layouts: 40.6 us -> 7.66 us
  Pallas kernels: 0 us -> 11.3 us
    psum x1, waiting for transfers between devices: 426 us -> 86.8 us  [shards(): gram_left = lax.psum(local_gram, 'dst')]
    dot_general x25 -> x0, matrix products: 69 us -> none  [the longest x24 64.2 us: one_pair(): jnp.einsum('gak,gkr->gar', tiles, khatri, preferred_element_type=jnp.floa...]
    convert_element_type x49 -> x0, other arithmetic: 36.4 us -> none  [the longest x24 20.4 us: one_pair(): rows_left.astype(jnp.float32)[:, :, None, :] * slab[None, None, :, :]]
    reduce_scatter x1, waiting for transfers between devices: 85.3 us -> 49.1 us  [shards(): lax.psum_scatter(partial_sum, 'dst', scatter_dimension=0, tiled=True)]
    gather x4 -> x1, local copies, waits for them, and re-layouts: 16 us -> 1.86 us  [shards(): tiles_dst[asked.reshape(peers * depth)].reshape(peers, depth, edge, width)]
    mul x24 -> x0, local copies, waits for them, and re-layouts: 11.9 us -> none  [one_pair(): rows_left.astype(jnp.float32)[:, :, None, :] * slab[None, None, :, :]]
    pallas_call x0 -> x1, Pallas kernels: none -> 11.3 us  [block_products(): pl.pallas_call(mttkrp_kernel, grid_spec=grid_spec, out_shape=jax.ShapeDty...]
  transfers between devices with their start and end apart: 4 -> 4, of which waited for: 2 -> 3; matrix products, arithmetic and copies ran while one was open for 11% -> 26% of each run, Pallas kernels for 0% -> 0%
where the time goes in v1:
time: 251 us; the launch traced here: 250 us
  waiting for transfers between devices  142 us (57%)
  other arithmetic  58.2 us (23%)
  between operations  14.8 us (6%)
  starting transfers between devices  11.7 us (5%)
  Pallas kernels  11.3 us (5%)
  local copies, waits for them, and re-layouts  7.66 us (3%)
  matrix products  4.43 us (2%)
    psum x1, waiting for transfers between devices, shards(): gram_left = lax.psum(local_gram, 'dst')  86.8 us
    reduce_scatter x1, waiting for transfers between devices, shards(): lax.psum_scatter(partial_sum, 'dst', scatter_dimension=0, tiled=True)  49.1 us
    another operation x6, other arithmetic, shards(): lower = jnp.linalg.cholesky(gram)  34 us
    another operation x3, other arithmetic, shards(): return jax.scipy.linalg.cho_solve((lower, True), target.T).T  19.7 us
    pallas_call x1, Pallas kernels, block_products(): pl.pallas_call(mttkrp_kernel, grid_spec=grid_spec, out_shape=jax.ShapeDty...  11.3 us
    all_to_all x1, starting transfers between devices, shards(): lax.all_to_all(requests, 'dst', split_axis=0, concat_axis=0, tiled=True)  7.15 us
    all_to_all x1, waiting for transfers between devices, shards(): lax.all_to_all(requests, 'dst', split_axis=0, concat_axis=0, tiled=True)  5.77 us
  transfers between devices with their start and end apart: 4, of which 3 were waited for; matrix products, arithmetic and copies ran while one was open for 26% of the time, Pallas kernels for 0%

profile of v1, /device:TPU:0, one launch (start us, length us, event | category | flops | bytes accessed | tf_op | source)
XLA Modules:
  0.0 249.9 jit_solution(5527501111026514173)
XLA Ops:
  6.5 1.0 convert_reduce_fusion
  7.5 0.7 multiply_add_fusion.places_ref
  8.2 0.7 select_reduce_fusion.2
  8.9 0.7 all_to_all.9
  9.6 7.1 %all-to-all-start = ((s32[16,1,3]{2,1,0:T(1,128)}), s32[16,1,3]{2,1,0:T(1,128)S(1)}, u32[]{:S(2)}, u32[]{:S(2)}) async-start(s32[16,1,3]{2,1,0:T(1,128)} %bitcast.6), calls=%async_computation | async-start | bytes 16384 | tf_op jit(solution)/shard_map/all_to_all | solution.py:74
  16.8 0.0 all-reduce.3.cloned.1.call-start
  16.8 1.6 fusion.15
  18.5 0.0 all-reduce.3.cloned.1.call-update
  18.5 5.8 %all-to-all-done = s32[16,1,3]{2,1,0:T(1,128)S(1)} async-done(((s32[16,1,3]{2,1,0:T(1,128)}), s32[16,1,3]{2,1,0:T(1,128)S(1)}, u32[]{:S(2)}, u32[]{:S(2)}) %all-to-all-start) | async-done | bytes 224 | tf_op jit(solution)/shard_map/all_to_all | solution.py:74
  24.3 0.5 broadcast.172
  24.8 0.7 reduce.15
  25.5 0.1 reshape.84
  25.6 1.9 gather_fusion
  27.5 4.5 %all-to-all-start.1 = ((bf16[16,3,64,256]{3,2,1,0:T(8,128)(2,1)}), bf16[16,3,64,256]{3,2,1,0:T(8,128)(2,1)}, u32[]{:S(2)}, u32[]{:S(2)}) async-start(bf16[16,3,64,256]{3,2,1,0:T(8,128)(2,1)} %bitcast.52), calls=%async_computation.1 | async-start | bytes 3145728 | tf_op jit(solution)/shard_map/all_to_all | solution.py:77
  32.0 0.0 copy-start.2
  32.0 0.0 reduce-scatter.2.cloned.1.call-start
  32.1 86.8 %all-reduce.3.cloned.1.call-done = f32[256,256]{0,1:T(8,128)} async-done(((f32[256,256]{0,1:T(8,128)}), f32[256,256]{0,1:T(8,128)}) %all-reduce.3.cloned.1.call-update) | async-done | bytes 262160 | tf_op jit(solution)/shard_map/psum | solution.py:86
  118.8 1.2 fusion
  120.0 0.1 copy.32
  120.2 11.7 %cholesky.49 = f32[128,128]{1,0:T(8,128)S(1)} custom-call(f32[128,128]{1,0:T(8,128)S(1)} %cholesky.115), custom_call_target="Cholesky" | custom-call | tf_op jit(solution)/shard_map/jit(cholesky)/cholesky | solution.py:89
  131.9 0.1 copy.33
  132.0 9.8 %custom-call.18 = f32[1,128,128]{1,2,0:T(8,128)S(1)} custom-call(f32[1,128,128]{2,1,0:T(8,128)S(1)} %get-tuple-element.40), custom_call_target="InvertDiagBlocksLowerTriangular" | custom-call | tf_op jit(solution)/shard_map/jit(cholesky)/cholesky | solution.py:89
  141.9 0.2 fusion.2
  142.1 0.1 copy.34
  142.2 0.3 convolution_subtract_fusion
  142.4 11.7 %cholesky.103 = f32[128,128]{1,0:T(8,128)S(1)} custom-call(f32[128,128]{1,0:T(8,128)S(1)} %convolution_subtract_fusion), custom_call_target="Cholesky" | custom-call | tf_op jit(solution)/shard_map/jit(cholesky)/cholesky | solution.py:89
  154.2 0.1 copy.35
  154.3 0.6 compare_reduce_fusion
  156.3 11.3 %shard_map.73 = f32[4,64,256]{2,1,0:T(8,128)} custom-call(s32[12]{0:T(128)S(1)} %copy-done.2, s32[12]{0:T(128)S(1)} %multiply_add_fusion.places_ref, bf16[12,64,4096]{2,1,0:T(8,128)(2,1)} %x_ref.1, bf16[48,64,256]{2,1,0:T(8,128)(2,1)} %bitcast.9.left_ref, bf16[64,256]{1,0:T(8,128)(2,1)S(1)} %copy-done.1), custom_call_target="tpu_custom_call" | custom-call | flops 1610612736 | bytes 6946816 | tf_op jit(solution)/shard_map/pallas_call | solution.py:46
  167.6 0.0 reduce-scatter.2.cloned.1.call-update
  167.6 0.1 triangular_solve.69
  167.7 4.0 %while.1 = (s32[]{:T(128)}, f32[256,256]{0,1:T(8,128)S(1)}, s32[2,2]{1,0:T(2,128)S(1)}, f32[2,128,128]{2,1,0:T(8,128)S(1)}, s32[]{:T(128)}) while((s32[]{:T(128)}, f32[256,256]{0,1:T(8,128)S(1)}, s32[2,2]{1,0:T(2,128)S(1)}, f32[2,128,128]{2,1,0:T(8,128)S(1)}, s32[]{:T(128)}) %tuple.25), condition=%wide.while_cond, body=%wide.while_body.sunk | while | flops 2 | bytes 393329 | solution.py:91
  167.7 0.6 fusion.28
  168.3 1.3 dynamic-slice.7
  169.6 0.1 copy.42
  169.7 0.6 fusion.28
  170.3 1.3 dynamic-slice.7
  171.6 0.1 copy.42
  171.7 19.7 %custom-call.19 = f32[2,128,128]{1,2,0:T(8,128)S(1)} custom-call(f32[2,128,128]{2,1,0:T(8,128)S(1)} %get-tuple-element.12), custom_call_target="InvertDiagBlocksLowerTriangular" | custom-call | tf_op jit(solution)/shard_map/jit(_cho_solve)/triangular_solve | solution.py:91
  191.4 49.1 %reduce-scatter.2.cloned.1.call-done = f32[16,256]{1,0:T(8,128)} async-done(((f32[256,256]{1,0:T(8,128)}), f32[16,256]{1,0:T(8,128)}) %reduce-scatter.2.cloned.1.call-update) | async-done | bytes 16400 | tf_op jit(solution)/shard_map/reduce_scatter | solution.py:83
  240.5 0.7 add_bitcast_fusion
  241.3 0.2 fusion.6
  241.4 0.2 convolution_subtract_fusion.2
  241.6 0.2 fusion.8
  241.8 0.2 fusion.7
  242.0 0.2 convolution_subtract_fusion.1
  242.2 0.2 fusion.5
  242.4 0.7 maximum_bitcast_fusion
  (24 shorter events, 0.3 us)
Async XLA Ops:
  6.5 10.3 %copy-start = (bf16[4096,256]{1,0:T(8,128)(2,1)S(1)}, bf16[4096,256]{1,0:T(8,128)(2,1)}, u32[]{:S(2)}) copy-start(bf16[4096,256]{1,0:T(8,128)(2,1)} %param.11) | copy-start | bytes 6291460
  9.6 14.7 %all-to-all-start = ((s32[16,1,3]{2,1,0:T(1,128)}), s32[16,1,3]{2,1,0:T(1,128)S(1)}, u32[]{:S(2)}, u32[]{:S(2)}) async-start(s32[16,1,3]{2,1,0:T(1,128)} %bitcast.6), calls=%async_computation | async-start | bytes 16384 | tf_op jit(solution)/shard_map/all_to_all | solution.py:74
  16.8 102.0 %all-reduce.3.cloned.1.call-start = ((), (), s32[]{:S(2)}) async-start(), calls=%async_computation.3 | async-start | bytes 524288 | tf_op jit(solution)/shard_map/psum | solution.py:86
  27.5 91.3 %copy-start.1 = (bf16[64,256]{1,0:T(8,128)(2,1)S(1)}, bf16[64,256]{1,0:T(8,128)(2,1)}, u32[]{:S(2)}) copy-start(bf16[64,256]{1,0:T(8,128)(2,1)} %slab_ref.1) | copy-start | bytes 98308
  27.5 128.8 %all-to-all-start.1 = ((bf16[16,3,64,256]{3,2,1,0:T(8,128)(2,1)}), bf16[16,3,64,256]{3,2,1,0:T(8,128)(2,1)}, u32[]{:S(2)}, u32[]{:S(2)}) async-start(bf16[16,3,64,256]{3,2,1,0:T(8,128)(2,1)} %bitcast.52), calls=%async_computation.1 | async-start | bytes 3145728 | tf_op jit(solution)/shard_map/all_to_all | solution.py:77
  32.0 124.3 %copy-start.2 = (s32[12]{0:T(128)S(1)}, s32[12]{0:T(128)}, u32[]{:S(2)}) copy-start(s32[12]{0:T(128)} %rows_ref.1) | copy-start | bytes 148
  32.0 208.5 %reduce-scatter.2.cloned.1.call-start = ((), (), s32[]{:S(2)}) async-start(), calls=%async_computation.4 | async-start | bytes 278528 | tf_op jit(solution)/shard_map/reduce_scatter | solution.py:83
  167.6 72.9 %copy-start.3 = (f32[16,256]{1,0:T(8,128)S(1)}, f32[16,256]{1,0:T(8,128)}, u32[]{:S(2)}) copy-start(f32[16,256]{1,0:T(8,128)} %param.13) | copy-start | bytes 49156
Sparse Core Ops, SparseCore 0:
  20.8 97.9 all-reduce.2
  167.7 72.7 reduce-scatter.1

commit v2 on v1

--- a/solution.py
+++ b/solution.py
@@ -58,6 +58,12 @@
     )(block_row, places, slab_blocks, received, factor_slab)
 
 
+def scatter_sum(rows, peers):
+    pieces = rows.reshape(peers, rows.shape[0] // peers, rows.shape[1])
+    arrived = lax.all_to_all(pieces, "dst", split_axis=0, concat_axis=0, tiled=True)
+    return jnp.sum(arrived, axis=0)
+
+
 def shards(slab_blocks, owner_column, block_row, block_col, factor_dst, factor_slab, factor_old):
     peers = lax.axis_size("dst")
     count = slab_blocks.shape[0]
@@ -80,10 +86,11 @@
     row_blocks = factor_old.shape[0] * peers // edge
     partial_sum = block_products(slab_blocks, received, places, block_row, factor_slab, row_blocks)
     partial_sum = partial_sum.reshape(row_blocks * edge, width)
-    summed_rows = lax.psum_scatter(partial_sum, "dst", scatter_dimension=0, tiled=True)
+    summed_rows = scatter_sum(partial_sum, peers)
 
     local_gram = jnp.dot(factor_dst.T, factor_dst, preferred_element_type=jnp.float32)
-    gram_left = lax.psum(local_gram, "dst")
+    gram_rows = scatter_sum(local_gram, peers)
+    gram_left = lax.all_gather(gram_rows, "dst", axis=0, tiled=True)
     gram_right = jnp.dot(factor_slab.T, factor_slab, preferred_element_type=jnp.float32)
     gram = gram_left * gram_right + RIDGE * jnp.eye(width, dtype=jnp.float32)
     lower = jnp.linalg.cholesky(gram)

time: 251 us -> 149 us (0.59)
  waiting for transfers between devices: 142 us -> 11.3 us
  blocking collectives: 0 us -> 35.4 us
  between operations: 14.8 us -> 1.55 us
  starting transfers between devices: 11.7 us -> 19.7 us
    psum x1 -> x0, waiting for transfers between devices: 86.8 us -> none  [shards(): gram_left = lax.psum(local_gram, 'dst')]
    reduce_scatter x1 -> x0, waiting for transfers between devices: 49.1 us -> none  [shards(): lax.psum_scatter(partial_sum, 'dst', scatter_dimension=0, tiled=True)]
    all_gather x0 -> x1, blocking collectives: none -> 35.4 us  [shards(): gram_left = lax.all_gather(gram_rows, 'dst', axis=0, tiled=True)]
    all_to_all x0 -> x2, starting transfers between devices: none -> 8 us  [scatter_sum(): lax.all_to_all(pieces, 'dst', split_axis=0, concat_axis=0, tiled=True)]
    all_to_all x0 -> x2, waiting for transfers between devices: none -> 5.28 us  [scatter_sum(): lax.all_to_all(pieces, 'dst', split_axis=0, concat_axis=0, tiled=True)]
  transfers between devices with their start and end apart: 4 -> 4, of which waited for: 3 -> 2; matrix products, arithmetic and copies ran while one was open for 26% -> 43% of each run, Pallas kernels for 0% -> 0%
where the time goes in v2:
time: 149 us; the launch traced here: 148 us
  other arithmetic  57.5 us (39%)
  blocking collectives  35.4 us (24%)
  starting transfers between devices  19.7 us (13%)
  waiting for transfers between devices  11.3 us (8%)
  Pallas kernels  11.2 us (8%)
  local copies, waits for them, and re-layouts  7.82 us (5%)
  matrix products  3.28 us (2%)
  between operations  1.55 us (1%)
    all_gather x1, blocking collectives, shards(): gram_left = lax.all_gather(gram_rows, 'dst', axis=0, tiled=True)  35.4 us
    another operation x6, other arithmetic, shards(): lower = jnp.linalg.cholesky(gram)  34 us
    another operation x3, other arithmetic, shards(): return jax.scipy.linalg.cho_solve((lower, True), target.T).T  19.7 us
    pallas_call x1, Pallas kernels, block_products(): pl.pallas_call(mttkrp_kernel, grid_spec=grid_spec, out_shape=jax.ShapeDty...  11.2 us
    all_to_all x2, starting transfers between devices, scatter_sum(): lax.all_to_all(pieces, 'dst', split_axis=0, concat_axis=0, tiled=True)  8 us
    all_to_all x1, starting transfers between devices, shards(): lax.all_to_all(requests, 'dst', split_axis=0, concat_axis=0, tiled=True)  7.15 us
    all_to_all x1, waiting for transfers between devices, shards(): lax.all_to_all(requests, 'dst', split_axis=0, concat_axis=0, tiled=True)  6.05 us
    all_to_all x2, waiting for transfers between devices, scatter_sum(): lax.all_to_all(pieces, 'dst', split_axis=0, concat_axis=0, tiled=True)  5.28 us
  transfers between devices with their start and end apart: 4, of which 2 were waited for; matrix products, arithmetic and copies ran while one was open for 43% of the time, Pallas kernels for 0%

profile of v2, /device:TPU:0, one launch (start us, length us, event | category | flops | bytes accessed | tf_op | source)
XLA Modules:
  0.0 147.8 jit_solution(10427498722356715343)
XLA Ops:
  0.0 1.0 convert_reduce_fusion
  1.0 0.7 multiply_add_fusion.places_ref
  1.7 0.7 select_reduce_fusion.2
  2.4 0.7 all_to_all.16
  3.1 7.1 %all-to-all-start.1 = ((s32[16,1,3]{2,1,0:T(1,128)}), s32[16,1,3]{2,1,0:T(1,128)S(1)}, u32[]{:S(2)}, u32[]{:S(2)}) async-start(s32[16,1,3]{2,1,0:T(1,128)} %bitcast.7), calls=%async_computation.1 | async-start | bytes 16384 | tf_op jit(solution)/shard_map/all_to_all | solution.py:80
  10.3 1.4 fusion.15
  11.7 6.1 %all-to-all-done.1 = s32[16,1,3]{2,1,0:T(1,128)S(1)} async-done(((s32[16,1,3]{2,1,0:T(1,128)}), s32[16,1,3]{2,1,0:T(1,128)S(1)}, u32[]{:S(2)}, u32[]{:S(2)}) %all-to-all-start.1) | async-done | bytes 224 | tf_op jit(solution)/shard_map/all_to_all | solution.py:80
  17.8 3.5 %all-to-all-start = ((f32[16,16,256]{2,1,0:T(8,128)}), f32[16,16,256]{2,1,0:T(8,128)S(1)}, u32[]{:S(2)}, u32[]{:S(2)}) async-start(f32[16,16,256]{2,1,0:T(8,128)} %bitcast), calls=%async_computation | async-start | bytes 524288 | tf_op jit(solution)/shard_map/all_to_all | solution.py:63
  21.3 0.5 broadcast.172
  21.8 0.7 reduce.15
  22.5 0.1 reshape.85
  22.6 1.9 %gather_fusion = bf16[48,64,256]{2,1,0:T(8,128)(2,1)} fusion(bf16[64,64,256]{2,1,0:T(8,128)(2,1)S(1)} %bitcast.52, s32[1024]{0:T(1024)S(1)} %pad_clamp_fusion), kind=kCustom, calls=%fused_computation | custom fusion | bytes 3145920 | tf_op jit(solution)/shard_map/gather | solution.py:82
  24.5 5.3 %all-to-all-done = f32[16,16,256]{2,1,0:T(8,128)S(1)} async-done(((f32[16,16,256]{2,1,0:T(8,128)}), f32[16,16,256]{2,1,0:T(8,128)S(1)}, u32[]{:S(2)}, u32[]{:S(2)}) %all-to-all-start) | async-done | bytes 262176 | tf_op jit(solution)/shard_map/all_to_all | solution.py:63
  29.8 4.5 %all-to-all-start.2 = ((bf16[16,3,64,256]{3,2,1,0:T(8,128)(2,1)}), bf16[16,3,64,256]{3,2,1,0:T(8,128)(2,1)}, u32[]{:S(2)}, u32[]{:S(2)}) async-start(bf16[16,3,64,256]{3,2,1,0:T(8,128)(2,1)} %bitcast.53), calls=%async_computation.2 | async-start | bytes 3145728 | tf_op jit(solution)/shard_map/all_to_all | solution.py:83
  34.3 35.4 %all_gather.3 = f32[256,256]{1,0:T(8,128)S(1)} all-gather(f32[16,256]{1,0:T(8,128)S(1)} %reduce_sum.36), channel_id=1, replica_groups=mesh['src'=8,'dst'=16] {'dst'}, dimensions={0}, use_global_device_ids=true | all-gather | bytes 278528 | tf_op jit(solution)/shard_map/all_gather | solution.py:93
  69.7 0.1 copy.28
  69.9 0.0 copy-start.2
  69.9 0.2 fusion
  70.1 0.1 copy.30
  70.3 11.7 %cholesky.49 = f32[128,128]{1,0:T(8,128)S(1)} custom-call(f32[128,128]{1,0:T(8,128)S(1)} %cholesky.115), custom_call_target="Cholesky" | custom-call | tf_op jit(solution)/shard_map/jit(cholesky)/cholesky | solution.py:96
  82.1 0.1 copy.31
  82.2 9.8 %custom-call.18 = f32[1,128,128]{1,2,0:T(8,128)S(1)} custom-call(f32[1,128,128]{2,1,0:T(8,128)S(1)} %get-tuple-element.40), custom_call_target="InvertDiagBlocksLowerTriangular" | custom-call | tf_op jit(solution)/shard_map/jit(cholesky)/cholesky | solution.py:96
  92.0 0.2 fusion.2
  92.2 0.1 copy.32
  92.3 0.3 convolution_subtract_fusion
  92.6 11.7 %cholesky.103 = f32[128,128]{1,0:T(8,128)S(1)} custom-call(f32[128,128]{1,0:T(8,128)S(1)} %convolution_subtract_fusion), custom_call_target="Cholesky" | custom-call | tf_op jit(solution)/shard_map/jit(cholesky)/cholesky | solution.py:96
  104.3 0.1 copy.33
  104.5 0.7 compare_reduce_fusion
  106.5 0.0 all-to-all-done.2
  106.5 11.2 %shard_map.73 = f32[4,64,256]{2,1,0:T(8,128)} custom-call(s32[12]{0:T(128)S(1)} %copy-done.2, s32[12]{0:T(128)S(1)} %multiply_add_fusion.places_ref, bf16[12,64,4096]{2,1,0:T(8,128)(2,1)} %x_ref.1, bf16[48,64,256]{2,1,0:T(8,128)(2,1)} %bitcast.10.left_ref, bf16[64,256]{1,0:T(8,128)(2,1)S(1)} %copy-done.1), custom_call_target="tpu_custom_call" | custom-call | flops 1610612736 | bytes 6946816 | tf_op jit(solution)/shard_map/pallas_call | solution.py:46
  117.7 4.5 %all-to-all-start.3 = ((f32[16,16,256]{2,1,0:T(8,128)}), f32[16,16,256]{2,1,0:T(8,128)S(1)}, u32[]{:S(2)}, u32[]{:S(2)}) async-start(f32[16,16,256]{2,1,0:T(8,128)} %bitcast.11), calls=%async_computation.3 | async-start | bytes 524288 | tf_op jit(solution)/shard_map/all_to_all | solution.py:63
  122.1 0.1 triangular_solve.69
  122.2 4.1 %while.1 = (s32[]{:T(128)}, f32[256,256]{0,1:T(8,128)S(1)}, s32[2,2]{1,0:T(2,128)S(1)}, f32[2,128,128]{2,1,0:T(8,128)S(1)}, s32[]{:T(128)}) while((s32[]{:T(128)}, f32[256,256]{0,1:T(8,128)S(1)}, s32[2,2]{1,0:T(2,128)S(1)}, f32[2,128,128]{2,1,0:T(8,128)S(1)}, s32[]{:T(128)}) %tuple.25), condition=%wide.while_cond, body=%wide.while_body.sunk | while | flops 2 | bytes 393329 | solution.py:98
  122.2 0.6 fusion.28
  122.8 1.3 dynamic-slice.7
  124.1 0.1 copy.39
  124.3 0.6 fusion.28
  124.8 1.3 dynamic-slice.7
  126.2 0.1 copy.39
  126.3 19.7 %custom-call.19 = f32[2,128,128]{1,2,0:T(8,128)S(1)} custom-call(f32[2,128,128]{2,1,0:T(8,128)S(1)} %get-tuple-element.12), custom_call_target="InvertDiagBlocksLowerTriangular" | custom-call | tf_op jit(solution)/shard_map/jit(_cho_solve)/triangular_solve | solution.py:98
  146.0 0.0 all-to-all-done.3
  146.0 0.2 fusion.6
  146.2 0.2 convolution_subtract_fusion.2
  146.4 0.2 fusion.8
  146.5 0.2 fusion.7
  146.7 0.2 convolution_subtract_fusion.1
  146.9 0.2 fusion.5
  147.2 0.7 maximum_bitcast_fusion
  (26 shorter events, 0.3 us)
Async XLA Ops:
  0.0 10.3 %copy-start = (bf16[4096,256]{1,0:T(8,128)(2,1)S(1)}, bf16[4096,256]{1,0:T(8,128)(2,1)}, u32[]{:S(2)}) copy-start(bf16[4096,256]{1,0:T(8,128)(2,1)} %param.11) | copy-start | bytes 6291460
  3.1 14.7 %all-to-all-start.1 = ((s32[16,1,3]{2,1,0:T(1,128)}), s32[16,1,3]{2,1,0:T(1,128)S(1)}, u32[]{:S(2)}, u32[]{:S(2)}) async-start(s32[16,1,3]{2,1,0:T(1,128)} %bitcast.7), calls=%async_computation.1 | async-start | bytes 16384 | tf_op jit(solution)/shard_map/all_to_all | solution.py:80
  17.8 12.0 %all-to-all-start = ((f32[16,16,256]{2,1,0:T(8,128)}), f32[16,16,256]{2,1,0:T(8,128)S(1)}, u32[]{:S(2)}, u32[]{:S(2)}) async-start(f32[16,16,256]{2,1,0:T(8,128)} %bitcast), calls=%async_computation | async-start | bytes 524288 | tf_op jit(solution)/shard_map/all_to_all | solution.py:63
  29.7 40.1 %copy-start.1 = (bf16[64,256]{1,0:T(8,128)(2,1)S(1)}, bf16[64,256]{1,0:T(8,128)(2,1)}, u32[]{:S(2)}) copy-start(bf16[64,256]{1,0:T(8,128)(2,1)} %slab_ref.1) | copy-start | bytes 98308
  29.8 76.7 %all-to-all-start.2 = ((bf16[16,3,64,256]{3,2,1,0:T(8,128)(2,1)}), bf16[16,3,64,256]{3,2,1,0:T(8,128)(2,1)}, u32[]{:S(2)}, u32[]{:S(2)}) async-start(bf16[16,3,64,256]{3,2,1,0:T(8,128)(2,1)} %bitcast.53), calls=%async_computation.2 | async-start | bytes 3145728 | tf_op jit(solution)/shard_map/all_to_all | solution.py:83
  69.9 36.6 %copy-start.2 = (s32[12]{0:T(128)S(1)}, s32[12]{0:T(128)}, u32[]{:S(2)}) copy-start(s32[12]{0:T(128)} %rows_ref.1) | copy-start | bytes 148
  117.7 28.4 %copy-start.3 = (f32[16,256]{1,0:T(8,128)S(1)}, f32[16,256]{1,0:T(8,128)}, u32[]{:S(2)}) copy-start(f32[16,256]{1,0:T(8,128)} %param.13) | copy-start | bytes 49156
  117.7 28.3 %all-to-all-start.3 = ((f32[16,16,256]{2,1,0:T(8,128)}), f32[16,16,256]{2,1,0:T(8,128)S(1)}, u32[]{:S(2)}, u32[]{:S(2)}) async-start(f32[16,16,256]{2,1,0:T(8,128)} %bitcast.11), calls=%async_computation.3 | async-start | bytes 524288 | tf_op jit(solution)/shard_map/all_to_all | solution.py:63

commit v3 on v2

--- a/solution.py
+++ b/solution.py
@@ -77,7 +77,16 @@
     slot_ids = jnp.arange(peers * depth, dtype=jnp.int32)
     match = places[None, :] == slot_ids[:, None]
     requests = jnp.sum(jnp.where(match, block_col[None, :], 0), axis=1).reshape(peers, depth)
-    asked = lax.all_to_all(requests, "dst", split_axis=0, concat_axis=0, tiled=True)
+    local_gram = jnp.dot(factor_dst.T, factor_dst, preferred_element_type=jnp.float32)
+    chunk = local_gram.shape[0] // peers
+    asked_row = jnp.zeros((peers, 1, width), jnp.float32).at[:, 0, :depth].set(requests.astype(jnp.float32))
+    first = jnp.concatenate([local_gram.reshape(peers, chunk, width), asked_row], axis=1)
+    first = lax.all_to_all(first, "dst", split_axis=0, concat_axis=0, tiled=True)
+    gram_rows = jnp.sum(first[:, :chunk, :], axis=0)
+    asked = first[:, chunk, :depth].astype(jnp.int32)
+    spread = jnp.broadcast_to(gram_rows[None], (peers, chunk, width))
+    gram_left = lax.all_to_all(spread, "dst", split_axis=0, concat_axis=0, tiled=True)
+    gram_left = gram_left.reshape(peers * chunk, width)
     tiles_dst = factor_dst.reshape(factor_dst.shape[0] // edge, edge, width)
     outgoing = tiles_dst[asked.reshape(peers * depth)].reshape(peers, depth, edge, width)
     received = lax.all_to_all(outgoing, "dst", split_axis=0, concat_axis=0, tiled=True)
@@ -88,9 +97,6 @@
     partial_sum = partial_sum.reshape(row_blocks * edge, width)
     summed_rows = scatter_sum(partial_sum, peers)
 
-    local_gram = jnp.dot(factor_dst.T, factor_dst, preferred_element_type=jnp.float32)
-    gram_rows = scatter_sum(local_gram, peers)
-    gram_left = lax.all_gather(gram_rows, "dst", axis=0, tiled=True)
     gram_right = jnp.dot(factor_slab.T, factor_slab, preferred_element_type=jnp.float32)
     gram = gram_left * gram_right + RIDGE * jnp.eye(width, dtype=jnp.float32)
     lower = jnp.linalg.cholesky(gram)

time: 149 us -> 120 us (0.81)
  blocking collectives: 35.4 us -> 0 us
  waiting for transfers between devices: 11.3 us -> 16.4 us
  starting transfers between devices: 19.7 us -> 22.5 us
    all_gather x1 -> x0, blocking collectives: 35.4 us -> none  [shards(): gram_left = lax.all_gather(gram_rows, 'dst', axis=0, tiled=True)]
    all_to_all x1 -> x2, waiting for transfers between devices: 6.05 us -> 16.4 us  [the longest x1 9.8 us: shards(): lax.all_to_all(first, 'dst', split_axis=0, concat_axis=0, tiled=True)]
    all_to_all x2 -> x1, waiting for transfers between devices: 5.28 us -> 0.01 us  [scatter_sum(): lax.all_to_all(pieces, 'dst', split_axis=0, concat_axis=0, tiled=True)]
    all_to_all x1 -> x2, starting transfers between devices: 7.15 us -> 10.9 us  [the longest x1 7.15 us: shards(): lax.all_to_all(first, 'dst', split_axis=0, concat_axis=0, tiled=True)]
    all_to_all x2 -> x1, starting transfers between devices: 8 us -> 7.24 us  [scatter_sum(): lax.all_to_all(pieces, 'dst', split_axis=0, concat_axis=0, tiled=True)]
  transfers between devices with their start and end apart: 4 -> 4, of which waited for: 2 -> 2; matrix products, arithmetic and copies ran while one was open for 43% -> 51% of each run, Pallas kernels for 0% -> 0%
where the time goes in v3:
time: 120 us; the launch traced here: 119 us
  other arithmetic  57.6 us (48%)
  starting transfers between devices  22.5 us (19%)
  waiting for transfers between devices  16.4 us (14%)
  Pallas kernels  11.2 us (9%)
  local copies, waits for them, and re-layouts  7.63 us (6%)
  matrix products  2.59 us (2%)
  between operations  1.46 us (1%)
    another operation x6, other arithmetic, shards(): lower = jnp.linalg.cholesky(gram)  34 us
    another operation x3, other arithmetic, shards(): return jax.scipy.linalg.cho_solve((lower, True), target.T).T  19.7 us
    pallas_call x1, Pallas kernels, block_products(): pl.pallas_call(mttkrp_kernel, grid_spec=grid_spec, out_shape=jax.ShapeDty...  11.2 us
    all_to_all x1, waiting for transfers between devices, shards(): lax.all_to_all(first, 'dst', split_axis=0, concat_axis=0, tiled=True)  9.8 us
    all_to_all x1, starting transfers between devices, scatter_sum(): lax.all_to_all(pieces, 'dst', split_axis=0, concat_axis=0, tiled=True)  7.24 us
    all_to_all x1, starting transfers between devices, shards(): lax.all_to_all(first, 'dst', split_axis=0, concat_axis=0, tiled=True)  7.15 us
    all_to_all x1, waiting for transfers between devices, shards(): lax.all_to_all(spread, 'dst', split_axis=0, concat_axis=0, tiled=True)  6.58 us
    all_to_all x1, starting transfers between devices, shards(): lax.all_to_all(outgoing, 'dst', split_axis=0, concat_axis=0, tiled=True)  4.39 us
  transfers between devices with their start and end apart: 4, of which 2 were waited for; matrix products, arithmetic and copies ran while one was open for 51% of the time, Pallas kernels for 0%

profile of v3, /device:TPU:0, one launch (start us, length us, event | category | flops | bytes accessed | tf_op | source)
XLA Modules:
  0.0 119.4 jit_solution(11653285353238054804)
XLA Ops:
  0.0 1.0 convert_reduce_fusion
  1.0 0.7 multiply_add_fusion.places_ref
  1.7 0.7 select_reduce_fusion.2
  2.4 0.1 convert_element_type.31
  2.5 0.0 copy-done
  2.5 0.7 fusion.16
  3.3 0.8 select_maximum_fusion
  4.0 7.1 %all-to-all-start = ((f32[16,17,256]{2,1,0:T(8,128)}), f32[16,17,256]{2,1,0:T(8,128)S(1)}, u32[]{:S(2)}, u32[]{:S(2)}) async-start(f32[16,17,256]{2,1,0:T(8,128)} %select_maximum_fusion), calls=%async_computation | async-start | bytes 786432 | tf_op jit(solution)/shard_map/all_to_all | solution.py:84
  11.2 9.8 %all-to-all-done = f32[16,17,256]{2,1,0:T(8,128)S(1)} async-done(((f32[16,17,256]{2,1,0:T(8,128)}), f32[16,17,256]{2,1,0:T(8,128)S(1)}, u32[]{:S(2)}, u32[]{:S(2)}) %all-to-all-start) | async-done | bytes 278560 | tf_op jit(solution)/shard_map/all_to_all | solution.py:84
  21.0 0.1 convert_element_type.33
  21.1 0.7 broadcast_in_dim.17
  21.9 3.7 %all-to-all-start.1 = ((f32[16,16,256]{2,1,0:T(8,128)}), f32[16,16,256]{2,1,0:T(8,128)S(1)}, u32[]{:S(2)}, u32[]{:S(2)}) async-start(f32[16,16,256]{2,1,0:T(8,128)} %broadcast_in_dim.17), calls=%async_computation.1 | async-start | bytes 524288 | tf_op jit(solution)/shard_map/all_to_all | solution.py:88
  25.6 1.9 %gather_fusion = bf16[48,64,256]{2,1,0:T(8,128)(2,1)} fusion(bf16[64,64,256]{2,1,0:T(8,128)(2,1)S(1)} %bitcast.53, s32[1024]{0:T(1024)S(1)} %pad_clamp_fusion), kind=kCustom, calls=%fused_computation | custom fusion | bytes 3145920 | tf_op jit(solution)/shard_map/gather | solution.py:91
  27.5 6.6 %all-to-all-done.1 = f32[16,16,256]{2,1,0:T(8,128)S(1)} async-done(((f32[16,16,256]{2,1,0:T(8,128)}), f32[16,16,256]{2,1,0:T(8,128)S(1)}, u32[]{:S(2)}, u32[]{:S(2)}) %all-to-all-start.1) | async-done | bytes 262176 | tf_op jit(solution)/shard_map/all_to_all | solution.py:88
  34.1 4.4 %all-to-all-start.2 = ((bf16[16,3,64,256]{3,2,1,0:T(8,128)(2,1)}), bf16[16,3,64,256]{3,2,1,0:T(8,128)(2,1)}, u32[]{:S(2)}, u32[]{:S(2)}) async-start(bf16[16,3,64,256]{3,2,1,0:T(8,128)(2,1)} %bitcast.54), calls=%async_computation.2 | async-start | bytes 3145728 | tf_op jit(solution)/shard_map/all_to_all | solution.py:92
  38.5 0.1 copy.32
  38.6 0.0 copy-start.2
  38.6 0.2 fusion
  38.8 0.1 copy.34
  39.0 11.7 %cholesky.49 = f32[128,128]{1,0:T(8,128)S(1)} custom-call(f32[128,128]{1,0:T(8,128)S(1)} %cholesky.115), custom_call_target="Cholesky" | custom-call | tf_op jit(solution)/shard_map/jit(cholesky)/cholesky | solution.py:102
  50.8 0.1 copy.35
  50.9 9.8 %custom-call.18 = f32[1,128,128]{1,2,0:T(8,128)S(1)} custom-call(f32[1,128,128]{2,1,0:T(8,128)S(1)} %get-tuple-element.52), custom_call_target="InvertDiagBlocksLowerTriangular" | custom-call | tf_op jit(solution)/shard_map/jit(cholesky)/cholesky | solution.py:102
  60.7 0.2 fusion.2
  60.9 0.1 copy.36
  61.0 0.3 convolution_subtract_fusion
  61.3 11.7 %cholesky.103 = f32[128,128]{1,0:T(8,128)S(1)} custom-call(f32[128,128]{1,0:T(8,128)S(1)} %convolution_subtract_fusion), custom_call_target="Cholesky" | custom-call | tf_op jit(solution)/shard_map/jit(cholesky)/cholesky | solution.py:102
  73.0 0.1 copy.37
  73.1 0.7 compare_reduce_fusion
  75.1 0.0 all-to-all-done.2
  75.1 11.2 %shard_map.73 = f32[4,64,256]{2,1,0:T(8,128)} custom-call(s32[12]{0:T(128)S(1)} %copy-done.2, s32[12]{0:T(128)S(1)} %multiply_add_fusion.places_ref, bf16[12,64,4096]{2,1,0:T(8,128)(2,1)} %x_ref.1, bf16[48,64,256]{2,1,0:T(8,128)(2,1)} %bitcast.10.left_ref, bf16[64,256]{1,0:T(8,128)(2,1)S(1)} %copy-done.1), custom_call_target="tpu_custom_call" | custom-call | flops 1610612736 | bytes 6946816 | tf_op jit(solution)/shard_map/pallas_call | solution.py:46
  86.3 7.2 %all-to-all-start.3 = ((f32[16,16,256]{2,1,0:T(8,128)}), f32[16,16,256]{2,1,0:T(8,128)S(1)}, u32[]{:S(2)}, u32[]{:S(2)}) async-start(f32[16,16,256]{2,1,0:T(8,128)} %bitcast.11), calls=%async_computation.3 | async-start | bytes 524288 | tf_op jit(solution)/shard_map/all_to_all | solution.py:63
  93.5 0.1 triangular_solve.69
  93.6 4.3 %while.2 = (s32[]{:T(128)}, f32[256,256]{0,1:T(8,128)S(1)}, s32[2,2]{1,0:T(2,128)S(1)}, f32[2,128,128]{2,1,0:T(8,128)S(1)}, s32[]{:T(128)}) while((s32[]{:T(128)}, f32[256,256]{0,1:T(8,128)S(1)}, s32[2,2]{1,0:T(2,128)S(1)}, f32[2,128,128]{2,1,0:T(8,128)S(1)}, s32[]{:T(128)}) %tuple.29), condition=%wide.while_cond.1, body=%wide.while_body.1.sunk | while | flops 2 | bytes 393329 | solution.py:104
  93.6 0.7 fusion.29
  94.3 1.3 %dynamic-slice.14 = f32[128,128]{0,1:T(8,128)S(1)} dynamic-slice(f32[256,256]{0,1:T(8,128)S(1)} %get-tuple-element.95, s32[]{:T(128)} %bitcast.51, s32[]{:T(128)} %bitcast.52), dynamic_slice_sizes={128,128} | dynamic-slice | bytes 131076 | tf_op jit(solution)/shard_map/jit(_cho_solve)/triangular_solve
  95.6 0.1 copy.43
  95.7 0.7 fusion.29
  96.4 1.3 %dynamic-slice.14 = f32[128,128]{0,1:T(8,128)S(1)} dynamic-slice(f32[256,256]{0,1:T(8,128)S(1)} %get-tuple-element.95, s32[]{:T(128)} %bitcast.51, s32[]{:T(128)} %bitcast.52), dynamic_slice_sizes={128,128} | dynamic-slice | bytes 131076 | tf_op jit(solution)/shard_map/jit(_cho_solve)/triangular_solve
  97.7 0.1 copy.43
  97.9 19.7 %custom-call.19 = f32[2,128,128]{1,2,0:T(8,128)S(1)} custom-call(f32[2,128,128]{2,1,0:T(8,128)S(1)} %get-tuple-element.24), custom_call_target="InvertDiagBlocksLowerTriangular" | custom-call | tf_op jit(solution)/shard_map/jit(_cho_solve)/triangular_solve | solution.py:104
  117.6 0.0 all-to-all-done.3
  117.6 0.2 fusion.6
  117.8 0.2 convolution_subtract_fusion.2
  117.9 0.2 fusion.8
  118.1 0.2 fusion.7
  118.3 0.2 convolution_subtract_fusion.1
  118.5 0.2 fusion.5
  118.8 0.7 maximum_bitcast_fusion
  (27 shorter events, 0.3 us)
Async XLA Ops:
  0.0 2.5 %copy-start = (bf16[4096,256]{1,0:T(8,128)(2,1)S(1)}, bf16[4096,256]{1,0:T(8,128)(2,1)}, u32[]{:S(2)}) copy-start(bf16[4096,256]{1,0:T(8,128)(2,1)} %param.13) | copy-start | bytes 6291460
  4.0 17.0 %all-to-all-start = ((f32[16,17,256]{2,1,0:T(8,128)}), f32[16,17,256]{2,1,0:T(8,128)S(1)}, u32[]{:S(2)}, u32[]{:S(2)}) async-start(f32[16,17,256]{2,1,0:T(8,128)} %select_maximum_fusion), calls=%async_computation | async-start | bytes 786432 | tf_op jit(solution)/shard_map/all_to_all | solution.py:84
  21.9 12.2 %all-to-all-start.1 = ((f32[16,16,256]{2,1,0:T(8,128)}), f32[16,16,256]{2,1,0:T(8,128)S(1)}, u32[]{:S(2)}, u32[]{:S(2)}) async-start(f32[16,16,256]{2,1,0:T(8,128)} %broadcast_in_dim.17), calls=%async_computation.1 | async-start | bytes 524288 | tf_op jit(solution)/shard_map/all_to_all | solution.py:88
  27.5 11.1 %copy-start.1 = (bf16[64,256]{1,0:T(8,128)(2,1)S(1)}, bf16[64,256]{1,0:T(8,128)(2,1)}, u32[]{:S(2)}) copy-start(bf16[64,256]{1,0:T(8,128)(2,1)} %slab_ref.1) | copy-start | bytes 98308
  34.1 41.0 %all-to-all-start.2 = ((bf16[16,3,64,256]{3,2,1,0:T(8,128)(2,1)}), bf16[16,3,64,256]{3,2,1,0:T(8,128)(2,1)}, u32[]{:S(2)}, u32[]{:S(2)}) async-start(bf16[16,3,64,256]{3,2,1,0:T(8,128)(2,1)} %bitcast.54), calls=%async_computation.2 | async-start | bytes 3145728 | tf_op jit(solution)/shard_map/all_to_all | solution.py:92
  38.6 36.5 %copy-start.2 = (s32[12]{0:T(128)S(1)}, s32[12]{0:T(128)}, u32[]{:S(2)}) copy-start(s32[12]{0:T(128)} %rows_ref.1) | copy-start | bytes 148
  86.3 31.3 %copy-start.3 = (f32[16,256]{1,0:T(8,128)S(1)}, f32[16,256]{1,0:T(8,128)}, u32[]{:S(2)}) copy-start(f32[16,256]{1,0:T(8,128)} %param.15) | copy-start | bytes 49156
  86.3 31.3 %all-to-all-start.3 = ((f32[16,16,256]{2,1,0:T(8,128)}), f32[16,16,256]{2,1,0:T(8,128)S(1)}, u32[]{:S(2)}, u32[]{:S(2)}) async-start(f32[16,16,256]{2,1,0:T(8,128)} %bitcast.11), calls=%async_computation.3 | async-start | bytes 524288 | tf_op jit(solution)/shard_map/all_to_all | solution.py:63

commit v4 on v3

--- a/solution.py
+++ b/solution.py
@@ -64,6 +64,25 @@
     return jnp.sum(arrived, axis=0)
 
 
+def ridge_inverse(gram):
+    eye = jnp.eye(gram.shape[0], dtype=jnp.float32)
+    start = eye / jnp.max(jnp.sum(jnp.abs(gram), axis=1))
+
+    def going(state):
+        steps, _, norm = state
+        return (norm >= 1e-3) & (steps < 64)
+
+    def step(state):
+        steps, inverse, _ = state
+        residual = eye - jnp.dot(gram, inverse, precision=lax.Precision.HIGHEST)
+        norm = jnp.max(jnp.sum(jnp.abs(residual), axis=1))
+        inverse = inverse + jnp.dot(inverse, residual, precision=lax.Precision.HIGHEST)
+        return steps + 1, inverse, norm
+
+    _, inverse, _ = lax.while_loop(going, step, (jnp.int32(0), start, jnp.float32(2.0)))
+    return inverse
+
+
 def shards(slab_blocks, owner_column, block_row, block_col, factor_dst, factor_slab, factor_old):
     peers = lax.axis_size("dst")
     count = slab_blocks.shape[0]
@@ -95,13 +114,14 @@
     row_blocks = factor_old.shape[0] * peers // edge
     partial_sum = block_products(slab_blocks, received, places, block_row, factor_slab, row_blocks)
     partial_sum = partial_sum.reshape(row_blocks * edge, width)
+    partial_sum, gram_left = lax.optimization_barrier((partial_sum, gram_left))
     summed_rows = scatter_sum(partial_sum, peers)
 
     gram_right = jnp.dot(factor_slab.T, factor_slab, preferred_element_type=jnp.float32)
     gram = gram_left * gram_right + RIDGE * jnp.eye(width, dtype=jnp.float32)
-    lower = jnp.linalg.cholesky(gram)
+    inverse = ridge_inverse(gram)
     target = summed_rows + RIDGE * factor_old
-    return jax.scipy.linalg.cho_solve((lower, True), target.T).T
+    return jnp.dot(target, inverse, precision=lax.Precision.HIGHEST)
 
 
 def solution(mesh):

time: 120 us -> 93.9 us (0.78)
  other arithmetic: 57.6 us -> 8.67 us
  blocking collectives: 0 us -> 16.8 us
  starting transfers between devices: 22.5 us -> 15.2 us
  matrix products: 2.59 us -> 9.21 us
  loops' own time: 0.06 us -> 5.9 us
  waiting for transfers between devices: 16.4 us -> 21.9 us
  local copies, waits for them, and re-layouts: 7.63 us -> 3.21 us
    another operation x9 -> x0, other arithmetic: 53.7 us -> none  [the longest x6 34 us: shards(): lower = jnp.linalg.cholesky(gram)]
    all_to_all x1, waiting for transfers between devices: 0.01 us -> 21.9 us  [shards(): lax.all_to_all(outgoing, 'dst', split_axis=0, concat_axis=0, tiled=True)]
    all_to_all x0 -> x1, blocking collectives: none -> 16.8 us  [shards(): lax.all_to_all(first, 'dst', split_axis=0, concat_axis=0, tiled=True)]
    all_to_all x1 -> x0, waiting for transfers between devices: 9.8 us -> none  [shards(): lax.all_to_all(first, 'dst', split_axis=0, concat_axis=0, tiled=True)]
    dot_general x0 -> x19, matrix products: none -> 8.21 us  [the longest x9 3.87 us: step(): residual = eye - jnp.dot(gram, inverse, precision=lax.Precision.HIGHEST)]
    all_to_all x1 -> x0, starting transfers between devices: 7.15 us -> none  [shards(): lax.all_to_all(first, 'dst', split_axis=0, concat_axis=0, tiled=True)]
    all_to_all x1, waiting for transfers between devices: 6.58 us -> 0.01 us  [shards(): lax.all_to_all(spread, 'dst', split_axis=0, concat_axis=0, tiled=True)]
    reduce_max x0 -> x10, other arithmetic: none -> 6.13 us  [the longest x9 5.51 us: step(): norm = jnp.max(jnp.sum(jnp.abs(residual), axis=1))]
  transfers between devices with their start and end apart: 4 -> 3, of which waited for: 2 -> 1; matrix products, arithmetic and copies ran while one was open for 51% -> 15% of each run, Pallas kernels for 0% -> 12%
where the time goes in v4:
time: 93.9 us; the launch traced here: 92.8 us
  waiting for transfers between devices  21.9 us (23%)
  blocking collectives  16.8 us (18%)
  starting transfers between devices  15.2 us (16%)
  Pallas kernels  11.2 us (12%)
  matrix products  9.21 us (10%)
  other arithmetic  8.67 us (9%)
  loops' own time  5.9 us (6%)
  local copies, waits for them, and re-layouts  3.21 us (3%)
    all_to_all x1, waiting for transfers between devices, shards(): lax.all_to_all(outgoing, 'dst', split_axis=0, concat_axis=0, tiled=True)  21.9 us
    all_to_all x1, blocking collectives, shards(): lax.all_to_all(first, 'dst', split_axis=0, concat_axis=0, tiled=True)  16.8 us
    pallas_call x1, Pallas kernels, block_products(): pl.pallas_call(mttkrp_kernel, grid_spec=grid_spec, out_shape=jax.ShapeDty...  11.2 us
    all_to_all x1, starting transfers between devices, scatter_sum(): lax.all_to_all(pieces, 'dst', split_axis=0, concat_axis=0, tiled=True)  7.15 us
    another operation x1, loops' own time, ridge_inverse(): lax.while_loop(going, step, (jnp.int32(0), start, jnp.float32(2.0)))  5.9 us
    reduce_max x9, other arithmetic, step(): norm = jnp.max(jnp.sum(jnp.abs(residual), axis=1))  5.51 us
    all_to_all x1, starting transfers between devices, shards(): lax.all_to_all(outgoing, 'dst', split_axis=0, concat_axis=0, tiled=True)  4.52 us
    dot_general x9, matrix products, step(): residual = eye - jnp.dot(gram, inverse, precision=lax.Precision.HIGHEST)  3.87 us
  transfers between devices with their start and end apart: 3, of which 1 were waited for; matrix products, arithmetic and copies ran while one was open for 15% of the time, Pallas kernels for 12%

profile of v4, /device:TPU:0, one launch (start us, length us, event | category | flops | bytes accessed | tf_op | source)
XLA Modules:
  0.0 92.8 jit_solution(13359799294802681959)
XLA Ops:
  0.0 1.0 %convert_reduce_fusion = s32[12]{0:T(128)S(1)} fusion(s32[12]{0:T(128)} %bitcast.40), kind=kLoop, calls=%fused_computation.23 | loop fusion | flops 708 | bytes 96 | tf_op jit(solution)/shard_map/reduce_sum | solution.py:95
  1.0 0.7 multiply_add_fusion.places_ref
  1.7 0.7 select_reduce_fusion
  2.4 0.1 convert_element_type.34
  2.5 0.7 fusion.13
  3.3 16.8 %all_to_all.20 = f32[16,17,256]{2,1,0:T(8,128)S(1)} all-to-all(f32[16,17,256]{2,1,0:T(8,128)S(1)} %select_maximum_fusion), channel_id=1, replica_groups=mesh['src'=8,'dst'=16] {'dst'}, dimensions={0} | all-to-all | bytes 557056 | tf_op jit(solution)/shard_map/all_to_all | solution.py:103
  20.1 0.1 convert_element_type.36
  20.2 1.9 %gather_fusion = bf16[48,64,256]{2,1,0:T(8,128)(2,1)} fusion(bf16[64,64,256]{2,1,0:T(8,128)(2,1)S(1)} %bitcast.35, s32[1024]{0:T(1024)S(1)} %pad_clamp_fusion), kind=kCustom, calls=%fused_computation | custom fusion | bytes 3145920 | tf_op jit(solution)/shard_map/gather | solution.py:110
  22.1 4.5 %all-to-all-start.1 = ((bf16[16,3,64,256]{3,2,1,0:T(8,128)(2,1)}), bf16[16,3,64,256]{3,2,1,0:T(8,128)(2,1)}, u32[]{:S(2)}, u32[]{:S(2)}) async-start(bf16[16,3,64,256]{3,2,1,0:T(8,128)(2,1)} %bitcast.36), calls=%async_computation.1 | async-start | bytes 3145728 | tf_op jit(solution)/shard_map/all_to_all | solution.py:111
  26.6 21.9 %all-to-all-done.1 = bf16[16,3,64,256]{3,2,1,0:T(8,128)(2,1)} async-done(((bf16[16,3,64,256]{3,2,1,0:T(8,128)(2,1)}), bf16[16,3,64,256]{3,2,1,0:T(8,128)(2,1)}, u32[]{:S(2)}, u32[]{:S(2)}) %all-to-all-start.1) | async-done | bytes 1572896 | tf_op jit(solution)/shard_map/all_to_all | solution.py:111
  48.6 0.7 broadcast_in_dim.16
  49.3 3.5 %all-to-all-start.2 = ((f32[16,16,256]{2,1,0:T(8,128)}), f32[16,16,256]{2,1,0:T(8,128)S(1)}, u32[]{:S(2)}, u32[]{:S(2)}) async-start(f32[16,16,256]{2,1,0:T(8,128)} %broadcast_in_dim.16), calls=%async_computation.2 | async-start | bytes 524288 | tf_op jit(solution)/shard_map/all_to_all | solution.py:107
  52.9 11.2 %shard_map.73 = f32[4,64,256]{2,1,0:T(8,128)} custom-call(s32[12]{0:T(128)S(1)} %copy-done.2, s32[12]{0:T(128)S(1)} %multiply_add_fusion.places_ref, bf16[12,64,4096]{2,1,0:T(8,128)(2,1)} %x_ref.1, bf16[48,64,256]{2,1,0:T(8,128)(2,1)} %bitcast.5.left_ref, bf16[64,256]{1,0:T(8,128)(2,1)S(1)} %copy-done.1), custom_call_target="tpu_custom_call" | custom-call | flops 1610612736 | bytes 6946816 | tf_op jit(solution)/shard_map/pallas_call | solution.py:46
  64.0 7.2 %all-to-all-start.3 = ((f32[16,16,256]{2,1,0:T(8,128)}), f32[16,16,256]{2,1,0:T(8,128)S(1)}, u32[]{:S(2)}, u32[]{:S(2)}) async-start(f32[16,16,256]{2,1,0:T(8,128)} %bitcast.8), calls=%async_computation.3 | async-start | bytes 524288 | tf_op jit(solution)/shard_map/all_to_all | solution.py:63
  71.2 0.1 copy.17
  71.3 0.3 abs_reduce_fusion.1
  71.6 0.6 reduce_max.18
  72.8 0.1 copy.18
  73.0 0.0 copy-start.3
  73.0 18.9 %while.14 = (s32[]{:T(128)}, f32[256,256]{0,1:T(8,128)S(1)}, f32[]{:T(128)}, f32[256,256]{1,0:T(8,128)S(1)}, s32[]{:T(128)}, /*index=5*/f32[]{:T(128)}) while((s32[]{:T(128)}, f32[256,256]{0,1:T(8,128)S(1)}, f32[]{:T(128)}, f32[256,256]{1,0:T(8,128)S(1)}, s32[]{:T(128)}, /*index=5*/f32[]{:T(128)}) %tuple.35), condition=%wide.region_9.0_spmd.clone, body=%wide.region_6.9_spmd.clone.sunk | while | flops 403046400 | bytes 2099289 | solution.py:82
  73.0 0.4 abs_reduce_fusion.3
  73.5 0.6 reduce_max.21
  74.1 0.4 fusion.32
  75.1 0.4 abs_reduce_fusion.3
  75.6 0.6 reduce_max.21
  76.2 0.4 fusion.32
  77.2 0.4 abs_reduce_fusion.3
  77.7 0.6 reduce_max.21
  78.3 0.4 fusion.32
  79.3 0.4 abs_reduce_fusion.3
  79.8 0.6 reduce_max.21
  80.4 0.4 fusion.32
  81.4 0.4 abs_reduce_fusion.3
  81.8 0.6 reduce_max.21
  82.5 0.4 fusion.32
  83.5 0.4 abs_reduce_fusion.3
  83.9 0.6 reduce_max.21
  84.6 0.4 fusion.32
  85.6 0.4 abs_reduce_fusion.3
  86.0 0.6 reduce_max.21
  86.7 0.4 fusion.32
  87.7 0.4 abs_reduce_fusion.3
  88.1 0.6 reduce_max.21
  88.8 0.4 fusion.32
  89.8 0.4 abs_reduce_fusion.3
  90.2 0.6 reduce_max.21
  90.8 0.4 fusion.32
  91.9 0.9 %fusion.5 = f32[16,256]{1,0:T(8,128)} fusion(f32[256,256]{0,1:T(8,128)S(1)} %get-tuple-element.48, f32[16,256]{1,0:T(8,128)S(1)} %reduce_sum.57, f32[16,256]{1,0:T(8,128)S(1)} %copy-done.3), kind=kOutput, calls=%fused_computation.15 | convolution fusion | flops 12591104 | bytes 311296 | tf_op jit(solution)/shard_map/dot_general | solution.py:124
  (26 shorter events, 0.3 us)
Async XLA Ops:
  0.0 2.5 %copy-start = (bf16[4096,256]{1,0:T(8,128)(2,1)S(1)}, bf16[4096,256]{1,0:T(8,128)(2,1)}, u32[]{:S(2)}) copy-start(bf16[4096,256]{1,0:T(8,128)(2,1)} %param.15) | copy-start | bytes 6291460
  22.1 30.8 %copy-start.1 = (bf16[64,256]{1,0:T(8,128)(2,1)S(1)}, bf16[64,256]{1,0:T(8,128)(2,1)}, u32[]{:S(2)}) copy-start(bf16[64,256]{1,0:T(8,128)(2,1)} %slab_ref.1) | copy-start | bytes 98308
  22.1 30.8 %copy-start.2 = (s32[12]{0:T(128)S(1)}, s32[12]{0:T(128)}, u32[]{:S(2)}) copy-start(s32[12]{0:T(128)} %rows_ref.1) | copy-start | bytes 148
  22.1 26.5 %all-to-all-start.1 = ((bf16[16,3,64,256]{3,2,1,0:T(8,128)(2,1)}), bf16[16,3,64,256]{3,2,1,0:T(8,128)(2,1)}, u32[]{:S(2)}, u32[]{:S(2)}) async-start(bf16[16,3,64,256]{3,2,1,0:T(8,128)(2,1)} %bitcast.36), calls=%async_computation.1 | async-start | bytes 3145728 | tf_op jit(solution)/shard_map/all_to_all | solution.py:111
  49.3 14.7 %all-to-all-start.2 = ((f32[16,16,256]{2,1,0:T(8,128)}), f32[16,16,256]{2,1,0:T(8,128)S(1)}, u32[]{:S(2)}, u32[]{:S(2)}) async-start(f32[16,16,256]{2,1,0:T(8,128)} %broadcast_in_dim.16), calls=%async_computation.2 | async-start | bytes 524288 | tf_op jit(solution)/shard_map/all_to_all | solution.py:107
  64.0 27.8 %all-to-all-start.3 = ((f32[16,16,256]{2,1,0:T(8,128)}), f32[16,16,256]{2,1,0:T(8,128)S(1)}, u32[]{:S(2)}, u32[]{:S(2)}) async-start(f32[16,16,256]{2,1,0:T(8,128)} %bitcast.8), calls=%async_computation.3 | async-start | bytes 524288 | tf_op jit(solution)/shard_map/all_to_all | solution.py:63
  73.0 18.9 %copy-start.3 = (f32[16,256]{1,0:T(8,128)S(1)}, f32[16,256]{1,0:T(8,128)}, u32[]{:S(2)}) copy-start(f32[16,256]{1,0:T(8,128)} %param.17) | copy-start | bytes 49156

commit v5 on v4

--- a/solution.py
+++ b/solution.py
@@ -79,7 +79,12 @@
         inverse = inverse + jnp.dot(inverse, residual, precision=lax.Precision.HIGHEST)
         return steps + 1, inverse, norm
 
-    _, inverse, _ = lax.while_loop(going, step, (jnp.int32(0), start, jnp.float32(2.0)))
+    inverse = start
+    for _ in range(9):
+        inverse = inverse + jnp.dot(
+            inverse, eye - jnp.dot(gram, inverse, precision=lax.Precision.HIGHEST), precision=lax.Precision.HIGHEST
+        )
+    _, inverse, _ = lax.while_loop(going, step, (jnp.int32(0), inverse, jnp.float32(2.0)))
     return inverse
 
 

time: 93.9 us -> 84.3 us (0.90)
  loops' own time: 5.9 us -> 0.65 us
  other arithmetic: 8.67 us -> 3.74 us
    dot_general x0 -> x18, matrix products: none -> 7.07 us  [the longest x9 3.54 us: ridge_inverse(): jnp.dot(gram, inverse, precision=lax.Precision.HIGHEST)]
    another operation x1, loops' own time: 5.9 us -> 0.65 us  [ridge_inverse(): lax.while_loop(going, step, (jnp.int32(0), inverse, jnp.float32(2.0)))]
    reduce_max x9 -> x1, other arithmetic: 5.51 us -> 0.61 us  [step(): norm = jnp.max(jnp.sum(jnp.abs(residual), axis=1))]
    dot_general x9 -> x1, matrix products: 3.87 us -> 0.43 us  [step(): residual = eye - jnp.dot(gram, inverse, precision=lax.Precision.HIGHEST)]
    dot_general x9 -> x1, matrix products: 3.41 us -> 0.38 us  [step(): jnp.dot(inverse, residual, precision=lax.Precision.HIGHEST)]
  transfers between devices with their start and end apart: 3 -> 3, of which waited for: 1 -> 1; matrix products, arithmetic and copies ran while one was open for 15% -> 12% of each run, Pallas kernels for 12% -> 13%
where the time goes in v5:
time: 84.3 us; the launch traced here: 83.3 us
  waiting for transfers between devices  21.9 us (26%)
  blocking collectives  16.8 us (20%)
  starting transfers between devices  15.2 us (18%)
  Pallas kernels  11.2 us (13%)
  matrix products  9.81 us (12%)
  other arithmetic  3.74 us (4%)
  local copies, waits for them, and re-layouts  3.06 us (4%)
  between operations  0.92 us (1%)
    all_to_all x1, waiting for transfers between devices, shards(): lax.all_to_all(outgoing, 'dst', split_axis=0, concat_axis=0, tiled=True)  21.9 us
    all_to_all x1, blocking collectives, shards(): lax.all_to_all(first, 'dst', split_axis=0, concat_axis=0, tiled=True)  16.8 us
    pallas_call x1, Pallas kernels, block_products(): pl.pallas_call(mttkrp_kernel, grid_spec=grid_spec, out_shape=jax.ShapeDty...  11.2 us
    all_to_all x1, starting transfers between devices, scatter_sum(): lax.all_to_all(pieces, 'dst', split_axis=0, concat_axis=0, tiled=True)  7.15 us
    all_to_all x1, starting transfers between devices, shards(): lax.all_to_all(outgoing, 'dst', split_axis=0, concat_axis=0, tiled=True)  4.52 us
    dot_general x9, matrix products, ridge_inverse(): jnp.dot(gram, inverse, precision=lax.Precision.HIGHEST)  3.54 us
    all_to_all x1, starting transfers between devices, shards(): lax.all_to_all(spread, 'dst', split_axis=0, concat_axis=0, tiled=True)  3.53 us
    dot_general x9, matrix products, ridge_inverse(): jnp.dot(inverse, eye - jnp.dot(gram, inverse, precision=lax.Precision.HIG...  3.53 us
  transfers between devices with their start and end apart: 3, of which 1 were waited for; matrix products, arithmetic and copies ran while one was open for 12% of the time, Pallas kernels for 13%

profile of v5, /device:TPU:0, one launch (start us, length us, event | category | flops | bytes accessed | tf_op | source)
XLA Modules:
  0.0 83.3 jit_solution(1519444020810260280)
XLA Ops:
  0.0 0.0 copy-start
  0.0 1.0 %convert_reduce_fusion = s32[12]{0:T(128)S(1)} fusion(s32[12]{0:T(128)} %bitcast.74), kind=kLoop, calls=%fused_computation.46 | loop fusion | flops 708 | bytes 96 | tf_op jit(solution)/shard_map/reduce_sum | solution.py:100
  1.0 0.7 multiply_add_fusion.places_ref
  1.7 0.7 select_reduce_fusion
  2.4 0.1 convert_element_type.52
  2.5 0.0 copy-done
  2.5 0.7 fusion.20
  3.3 16.8 %all_to_all.20 = f32[16,17,256]{2,1,0:T(8,128)S(1)} all-to-all(f32[16,17,256]{2,1,0:T(8,128)S(1)} %select_maximum_fusion), channel_id=1, replica_groups=mesh['src'=8,'dst'=16] {'dst'}, dimensions={0} | all-to-all | bytes 557056 | tf_op jit(solution)/shard_map/all_to_all | solution.py:108
  20.1 0.1 convert_element_type.54
  20.2 1.9 %gather_fusion = bf16[48,64,256]{2,1,0:T(8,128)(2,1)} fusion(bf16[64,64,256]{2,1,0:T(8,128)(2,1)S(1)} %bitcast.69, s32[1024]{0:T(1024)S(1)} %pad_clamp_fusion), kind=kCustom, calls=%fused_computation | custom fusion | bytes 3145920 | tf_op jit(solution)/shard_map/gather | solution.py:115
  22.1 4.5 %all-to-all-start.1 = ((bf16[16,3,64,256]{3,2,1,0:T(8,128)(2,1)}), bf16[16,3,64,256]{3,2,1,0:T(8,128)(2,1)}, u32[]{:S(2)}, u32[]{:S(2)}) async-start(bf16[16,3,64,256]{3,2,1,0:T(8,128)(2,1)} %bitcast.70), calls=%async_computation.1 | async-start | bytes 3145728 | tf_op jit(solution)/shard_map/all_to_all | solution.py:116
  26.6 21.9 %all-to-all-done.1 = bf16[16,3,64,256]{3,2,1,0:T(8,128)(2,1)} async-done(((bf16[16,3,64,256]{3,2,1,0:T(8,128)(2,1)}), bf16[16,3,64,256]{3,2,1,0:T(8,128)(2,1)}, u32[]{:S(2)}, u32[]{:S(2)}) %all-to-all-start.1) | async-done | bytes 1572896 | tf_op jit(solution)/shard_map/all_to_all | solution.py:116
  48.6 0.7 broadcast_in_dim.16
  49.3 3.5 %all-to-all-start.2 = ((f32[16,16,256]{2,1,0:T(8,128)}), f32[16,16,256]{2,1,0:T(8,128)S(1)}, u32[]{:S(2)}, u32[]{:S(2)}) async-start(f32[16,16,256]{2,1,0:T(8,128)} %broadcast_in_dim.16), calls=%async_computation.2 | async-start | bytes 524288 | tf_op jit(solution)/shard_map/all_to_all | solution.py:112
  52.8 0.0 copy-done.1
  52.9 0.0 copy-done.2
  52.9 11.2 %shard_map.73 = f32[4,64,256]{2,1,0:T(8,128)} custom-call(s32[12]{0:T(128)S(1)} %copy-done.2, s32[12]{0:T(128)S(1)} %multiply_add_fusion.places_ref, bf16[12,64,4096]{2,1,0:T(8,128)(2,1)} %x_ref.1, bf16[48,64,256]{2,1,0:T(8,128)(2,1)} %bitcast.5.left_ref, bf16[64,256]{1,0:T(8,128)(2,1)S(1)} %copy-done.1), custom_call_target="tpu_custom_call" | custom-call | flops 1610612736 | bytes 6946816 | tf_op jit(solution)/shard_map/pallas_call | solution.py:46
  64.0 0.0 all-to-all-done.2
  64.0 7.2 %all-to-all-start.3 = ((f32[16,16,256]{2,1,0:T(8,128)}), f32[16,16,256]{2,1,0:T(8,128)S(1)}, u32[]{:S(2)}, u32[]{:S(2)}) async-start(f32[16,16,256]{2,1,0:T(8,128)} %bitcast.8), calls=%async_computation.3 | async-start | bytes 524288 | tf_op jit(solution)/shard_map/all_to_all | solution.py:63
  71.2 0.1 copy.51
  71.3 0.3 abs_reduce_fusion.1
  71.6 0.1 copy.70
  71.7 0.6 reduce_max.18
  73.0 0.4 convolution_subtract_fusion.9
  73.4 0.4 convolution_add_fusion.8
  73.7 0.4 convolution_subtract_fusion.8
  74.1 0.4 convolution_add_fusion.7
  74.5 0.4 convolution_subtract_fusion.7
  74.9 0.4 convolution_add_fusion.6
  75.3 0.4 convolution_subtract_fusion.6
  75.8 0.4 convolution_add_fusion.5
  76.2 0.4 convolution_subtract_fusion.5
  76.6 0.4 convolution_add_fusion.4
  77.0 0.4 convolution_subtract_fusion.4
  77.4 0.4 convolution_add_fusion.3
  77.8 0.4 convolution_subtract_fusion.3
  78.2 0.4 convolution_add_fusion.2
  78.6 0.4 convolution_subtract_fusion.2
  79.0 0.4 convolution_add_fusion.1
  79.4 0.4 convolution_subtract_fusion.1
  79.8 0.4 convolution_add_fusion
  80.2 0.0 copy-start.3
  80.2 2.1 %while.14 = (s32[]{:T(128)}, f32[256,256]{0,1:T(8,128)S(1)}, f32[]{:T(128)}, f32[256,256]{1,0:T(8,128)S(1)}, s32[]{:T(128)}, /*index=5*/f32[]{:T(128)}) while((s32[]{:T(128)}, f32[256,256]{0,1:T(8,128)S(1)}, f32[]{:T(128)}, f32[256,256]{1,0:T(8,128)S(1)}, s32[]{:T(128)}, /*index=5*/f32[]{:T(128)}) %tuple.35), condition=%wide.region_9.0_spmd.clone, body=%wide.region_6.9_spmd.clone.sunk | while | flops 403046400 | bytes 2099289 | solution.py:87
  80.2 0.4 abs_reduce_fusion.3
  80.6 0.6 reduce_max.21
  81.3 0.4 fusion.73
  82.3 0.0 all-to-all-done.3
  82.3 0.9 %fusion.10 = f32[16,256]{1,0:T(8,128)} fusion(f32[256,256]{0,1:T(8,128)S(1)} %get-tuple-element.48, f32[16,256]{1,0:T(8,128)S(1)} %reduce_sum.57, f32[16,256]{1,0:T(8,128)S(1)} %copy-done.3), kind=kOutput, calls=%fused_computation.38 | convolution fusion | flops 12591104 | bytes 311296 | tf_op jit(solution)/shard_map/dot_general | solution.py:129
  (11 shorter events, 0.1 us)
Async XLA Ops:
  0.0 2.5 %copy-start = (bf16[4096,256]{1,0:T(8,128)(2,1)S(1)}, bf16[4096,256]{1,0:T(8,128)(2,1)}, u32[]{:S(2)}) copy-start(bf16[4096,256]{1,0:T(8,128)(2,1)} %param.15) | copy-start | bytes 6291460
  22.1 30.8 %copy-start.1 = (bf16[64,256]{1,0:T(8,128)(2,1)S(1)}, bf16[64,256]{1,0:T(8,128)(2,1)}, u32[]{:S(2)}) copy-start(bf16[64,256]{1,0:T(8,128)(2,1)} %slab_ref.1) | copy-start | bytes 98308
  22.1 30.8 %copy-start.2 = (s32[12]{0:T(128)S(1)}, s32[12]{0:T(128)}, u32[]{:S(2)}) copy-start(s32[12]{0:T(128)} %rows_ref.1) | copy-start | bytes 148
  22.1 26.5 %all-to-all-start.1 = ((bf16[16,3,64,256]{3,2,1,0:T(8,128)(2,1)}), bf16[16,3,64,256]{3,2,1,0:T(8,128)(2,1)}, u32[]{:S(2)}, u32[]{:S(2)}) async-start(bf16[16,3,64,256]{3,2,1,0:T(8,128)(2,1)} %bitcast.70), calls=%async_computation.1 | async-start | bytes 3145728 | tf_op jit(solution)/shard_map/all_to_all | solution.py:116
  49.3 14.7 %all-to-all-start.2 = ((f32[16,16,256]{2,1,0:T(8,128)}), f32[16,16,256]{2,1,0:T(8,128)S(1)}, u32[]{:S(2)}, u32[]{:S(2)}) async-start(f32[16,16,256]{2,1,0:T(8,128)} %broadcast_in_dim.16), calls=%async_computation.2 | async-start | bytes 524288 | tf_op jit(solution)/shard_map/all_to_all | solution.py:112
  64.0 18.2 %all-to-all-start.3 = ((f32[16,16,256]{2,1,0:T(8,128)}), f32[16,16,256]{2,1,0:T(8,128)S(1)}, u32[]{:S(2)}, u32[]{:S(2)}) async-start(f32[16,16,256]{2,1,0:T(8,128)} %bitcast.8), calls=%async_computation.3 | async-start | bytes 524288 | tf_op jit(solution)/shard_map/all_to_all | solution.py:63
  80.2 2.2 %copy-start.3 = (f32[16,256]{1,0:T(8,128)S(1)}, f32[16,256]{1,0:T(8,128)}, u32[]{:S(2)}) copy-start(f32[16,256]{1,0:T(8,128)} %param.17) | copy-start | bytes 49156

commit v6 on v5

--- a/solution.py
+++ b/solution.py
@@ -17,8 +17,8 @@
     def _():
         out_ref[...] = jnp.zeros_like(out_ref)
 
-    left = left_ref[0].astype(jnp.float32)
-    slab = slab_ref[...].astype(jnp.float32)
+    left = left_ref[0]
+    slab = slab_ref[...]
     edge = left.shape[0]
     bins = slab.shape[0]
     for b in range(edge):

time: 84.3 us -> 84.3 us (level)
  no operation moved by 1% of the time
where the time goes in v6:
time: 84.3 us; the launch traced here: 83.3 us
  waiting for transfers between devices  21.9 us (26%)
  blocking collectives  16.8 us (20%)
  starting transfers between devices  15.2 us (18%)
  Pallas kernels  11.2 us (13%)
  matrix products  9.8 us (12%)
  other arithmetic  3.74 us (4%)
  local copies, waits for them, and re-layouts  3.06 us (4%)
  between operations  0.92 us (1%)
    all_to_all x1, waiting for transfers between devices, shards(): lax.all_to_all(outgoing, 'dst', split_axis=0, concat_axis=0, tiled=True)  21.9 us
    all_to_all x1, blocking collectives, shards(): lax.all_to_all(first, 'dst', split_axis=0, concat_axis=0, tiled=True)  16.8 us
    pallas_call x1, Pallas kernels, block_products(): pl.pallas_call(mttkrp_kernel, grid_spec=grid_spec, out_shape=jax.ShapeDty...  11.2 us
    all_to_all x1, starting transfers between devices, scatter_sum(): lax.all_to_all(pieces, 'dst', split_axis=0, concat_axis=0, tiled=True)  7.15 us
    all_to_all x1, starting transfers between devices, shards(): lax.all_to_all(outgoing, 'dst', split_axis=0, concat_axis=0, tiled=True)  4.52 us
    dot_general x9, matrix products, ridge_inverse(): jnp.dot(gram, inverse, precision=lax.Precision.HIGHEST)  3.53 us
    all_to_all x1, starting transfers between devices, shards(): lax.all_to_all(spread, 'dst', split_axis=0, concat_axis=0, tiled=True)  3.53 us
    dot_general x9, matrix products, ridge_inverse(): jnp.dot(inverse, eye - jnp.dot(gram, inverse, precision=lax.Precision.HIG...  3.53 us
  transfers between devices with their start and end apart: 3, of which 1 were waited for; matrix products, arithmetic and copies ran while one was open for 12% of the time, Pallas kernels for 13%

profile of v6, /device:TPU:0, one launch (start us, length us, event | category | flops | bytes accessed | tf_op | source)
XLA Modules:
  0.0 83.3 jit_solution(11782727452293725002)
XLA Ops:
  0.0 1.0 %convert_reduce_fusion = s32[12]{0:T(128)S(1)} fusion(s32[12]{0:T(128)} %bitcast.74), kind=kLoop, calls=%fused_computation.46 | loop fusion | flops 708 | bytes 96 | tf_op jit(solution)/shard_map/reduce_sum | solution.py:100
  1.0 0.7 multiply_add_fusion.places_ref
  1.7 0.7 select_reduce_fusion
  2.4 0.1 convert_element_type.52
  2.5 0.0 copy-done
  2.5 0.7 fusion.20
  3.3 16.8 %all_to_all.20 = f32[16,17,256]{2,1,0:T(8,128)S(1)} all-to-all(f32[16,17,256]{2,1,0:T(8,128)S(1)} %select_maximum_fusion), channel_id=1, replica_groups=mesh['src'=8,'dst'=16] {'dst'}, dimensions={0} | all-to-all | bytes 557056 | tf_op jit(solution)/shard_map/all_to_all | solution.py:108
  20.1 0.1 convert_element_type.54
  20.2 1.9 %gather_fusion = bf16[48,64,256]{2,1,0:T(8,128)(2,1)} fusion(bf16[64,64,256]{2,1,0:T(8,128)(2,1)S(1)} %bitcast.69, s32[1024]{0:T(1024)S(1)} %pad_clamp_fusion), kind=kCustom, calls=%fused_computation | custom fusion | bytes 3145920 | tf_op jit(solution)/shard_map/gather | solution.py:115
  22.1 4.5 %all-to-all-start.1 = ((bf16[16,3,64,256]{3,2,1,0:T(8,128)(2,1)}), bf16[16,3,64,256]{3,2,1,0:T(8,128)(2,1)}, u32[]{:S(2)}, u32[]{:S(2)}) async-start(bf16[16,3,64,256]{3,2,1,0:T(8,128)(2,1)} %bitcast.70), calls=%async_computation.1 | async-start | bytes 3145728 | tf_op jit(solution)/shard_map/all_to_all | solution.py:116
  26.6 21.9 %all-to-all-done.1 = bf16[16,3,64,256]{3,2,1,0:T(8,128)(2,1)} async-done(((bf16[16,3,64,256]{3,2,1,0:T(8,128)(2,1)}), bf16[16,3,64,256]{3,2,1,0:T(8,128)(2,1)}, u32[]{:S(2)}, u32[]{:S(2)}) %all-to-all-start.1) | async-done | bytes 1572896 | tf_op jit(solution)/shard_map/all_to_all | solution.py:116
  48.6 0.7 broadcast_in_dim.16
  49.3 3.5 %all-to-all-start.2 = ((f32[16,16,256]{2,1,0:T(8,128)}), f32[16,16,256]{2,1,0:T(8,128)S(1)}, u32[]{:S(2)}, u32[]{:S(2)}) async-start(f32[16,16,256]{2,1,0:T(8,128)} %broadcast_in_dim.16), calls=%async_computation.2 | async-start | bytes 524288 | tf_op jit(solution)/shard_map/all_to_all | solution.py:112
  52.8 0.0 copy-done.1
  52.9 0.0 copy-done.2
  52.9 11.2 %shard_map.73 = f32[4,64,256]{2,1,0:T(8,128)} custom-call(s32[12]{0:T(128)S(1)} %copy-done.2, s32[12]{0:T(128)S(1)} %multiply_add_fusion.places_ref, bf16[12,64,4096]{2,1,0:T(8,128)(2,1)} %x_ref.1, bf16[48,64,256]{2,1,0:T(8,128)(2,1)} %bitcast.5.left_ref, bf16[64,256]{1,0:T(8,128)(2,1)S(1)} %copy-done.1), custom_call_target="tpu_custom_call" | custom-call | flops 1610612736 | bytes 6946816 | tf_op jit(solution)/shard_map/pallas_call | solution.py:46
  64.1 0.0 all-to-all-done.2
  64.1 7.2 %all-to-all-start.3 = ((f32[16,16,256]{2,1,0:T(8,128)}), f32[16,16,256]{2,1,0:T(8,128)S(1)}, u32[]{:S(2)}, u32[]{:S(2)}) async-start(f32[16,16,256]{2,1,0:T(8,128)} %bitcast.8), calls=%async_computation.3 | async-start | bytes 524288 | tf_op jit(solution)/shard_map/all_to_all | solution.py:63
  71.2 0.1 copy.51
  71.4 0.3 abs_reduce_fusion.1
  71.6 0.1 copy.70
  71.8 0.6 reduce_max.18
  73.0 0.4 convolution_subtract_fusion.9
  73.4 0.4 convolution_add_fusion.8
  73.8 0.4 convolution_subtract_fusion.8
  74.2 0.4 convolution_add_fusion.7
  74.6 0.4 convolution_subtract_fusion.7
  75.0 0.4 convolution_add_fusion.6
  75.4 0.4 convolution_subtract_fusion.6
  75.8 0.4 convolution_add_fusion.5
  76.2 0.4 convolution_subtract_fusion.5
  76.6 0.4 convolution_add_fusion.4
  77.0 0.4 convolution_subtract_fusion.4
  77.4 0.4 convolution_add_fusion.3
  77.8 0.4 convolution_subtract_fusion.3
  78.2 0.4 convolution_add_fusion.2
  78.6 0.4 convolution_subtract_fusion.2
  79.0 0.4 convolution_add_fusion.1
  79.4 0.4 convolution_subtract_fusion.1
  79.8 0.4 convolution_add_fusion
  80.2 0.0 copy-start.3
  80.2 2.1 %while.14 = (s32[]{:T(128)}, f32[256,256]{0,1:T(8,128)S(1)}, f32[]{:T(128)}, f32[256,256]{1,0:T(8,128)S(1)}, s32[]{:T(128)}, /*index=5*/f32[]{:T(128)}) while((s32[]{:T(128)}, f32[256,256]{0,1:T(8,128)S(1)}, f32[]{:T(128)}, f32[256,256]{1,0:T(8,128)S(1)}, s32[]{:T(128)}, /*index=5*/f32[]{:T(128)}) %tuple.35), condition=%wide.region_9.0_spmd.clone, body=%wide.region_6.9_spmd.clone.sunk | while | flops 403046400 | bytes 2099289 | solution.py:87
  80.3 0.4 abs_reduce_fusion.3
  80.7 0.6 reduce_max.21
  81.3 0.4 fusion.73
  82.3 0.0 all-to-all-done.3
  82.4 0.0 copy-done.3
  82.4 0.9 %fusion.10 = f32[16,256]{1,0:T(8,128)} fusion(f32[256,256]{0,1:T(8,128)S(1)} %get-tuple-element.48, f32[16,256]{1,0:T(8,128)S(1)} %reduce_sum.57, f32[16,256]{1,0:T(8,128)S(1)} %copy-done.3), kind=kOutput, calls=%fused_computation.38 | convolution fusion | flops 12591104 | bytes 311296 | tf_op jit(solution)/shard_map/dot_general | solution.py:129
  (11 shorter events, 0.1 us)
Async XLA Ops:
  0.0 2.5 %copy-start = (bf16[4096,256]{1,0:T(8,128)(2,1)S(1)}, bf16[4096,256]{1,0:T(8,128)(2,1)}, u32[]{:S(2)}) copy-start(bf16[4096,256]{1,0:T(8,128)(2,1)} %param.15) | copy-start | bytes 6291460
  22.1 30.8 %copy-start.1 = (bf16[64,256]{1,0:T(8,128)(2,1)S(1)}, bf16[64,256]{1,0:T(8,128)(2,1)}, u32[]{:S(2)}) copy-start(bf16[64,256]{1,0:T(8,128)(2,1)} %slab_ref.1) | copy-start | bytes 98308
  22.1 30.8 %copy-start.2 = (s32[12]{0:T(128)S(1)}, s32[12]{0:T(128)}, u32[]{:S(2)}) copy-start(s32[12]{0:T(128)} %rows_ref.1) | copy-start | bytes 148
  22.1 26.5 %all-to-all-start.1 = ((bf16[16,3,64,256]{3,2,1,0:T(8,128)(2,1)}), bf16[16,3,64,256]{3,2,1,0:T(8,128)(2,1)}, u32[]{:S(2)}, u32[]{:S(2)}) async-start(bf16[16,3,64,256]{3,2,1,0:T(8,128)(2,1)} %bitcast.70), calls=%async_computation.1 | async-start | bytes 3145728 | tf_op jit(solution)/shard_map/all_to_all | solution.py:116
  49.3 14.8 %all-to-all-start.2 = ((f32[16,16,256]{2,1,0:T(8,128)}), f32[16,16,256]{2,1,0:T(8,128)S(1)}, u32[]{:S(2)}, u32[]{:S(2)}) async-start(f32[16,16,256]{2,1,0:T(8,128)} %broadcast_in_dim.16), calls=%async_computation.2 | async-start | bytes 524288 | tf_op jit(solution)/shard_map/all_to_all | solution.py:112
  64.1 18.2 %all-to-all-start.3 = ((f32[16,16,256]{2,1,0:T(8,128)}), f32[16,16,256]{2,1,0:T(8,128)S(1)}, u32[]{:S(2)}, u32[]{:S(2)}) async-start(f32[16,16,256]{2,1,0:T(8,128)} %bitcast.8), calls=%async_computation.3 | async-start | bytes 524288 | tf_op jit(solution)/shard_map/all_to_all | solution.py:63
  80.2 2.2 %copy-start.3 = (f32[16,256]{1,0:T(8,128)S(1)}, f32[16,256]{1,0:T(8,128)}, u32[]{:S(2)}) copy-start(f32[16,256]{1,0:T(8,128)} %param.17) | copy-start | bytes 49156

commit v7 on v6

--- a/solution.py
+++ b/solution.py
@@ -28,7 +28,7 @@
     out_ref[row] = out_ref[row] + prod
 
 
-def block_products(slab_blocks, received, places, block_row, factor_slab, row_blocks):
+def block_products(slab_blocks, received, places, block_row, factor_slab, row_blocks, depth):
     count, edge, depth_k = slab_blocks.shape
     width = received.shape[2]
     grid_spec = pltpu.PrefetchScalarGridSpec(
@@ -36,7 +36,7 @@
         grid=(count,),
         in_specs=[
             pl.BlockSpec((1, edge, depth_k), lambda i, rows, pl_: (i, 0, 0)),
-            pl.BlockSpec((1, received.shape[1], width), lambda i, rows, pl_: (pl_[i], 0, 0)),
+            pl.BlockSpec((1, edge, width), lambda i, rows, pl_: (pl_[i] // depth, pl_[i] % depth, 0)),
             pl.BlockSpec(factor_slab.shape, lambda i, rows, pl_: (0, 0)),
         ],
         out_specs=pl.BlockSpec((row_blocks, edge, width), lambda i, rows, pl_: (0, 0, 0)),
@@ -62,6 +62,14 @@
     pieces = rows.reshape(peers, rows.shape[0] // peers, rows.shape[1])
     arrived = lax.all_to_all(pieces, "dst", split_axis=0, concat_axis=0, tiled=True)
     return jnp.sum(arrived, axis=0)
+
+
+def split_bf16(values):
+    high = lax.reduce_precision(values, exponent_bits=8, mantissa_bits=7)
+    rest = values - high
+    middle = lax.reduce_precision(rest, exponent_bits=8, mantissa_bits=7)
+    low = rest - middle
+    return jnp.concatenate([high, middle, low], axis=0).astype(jnp.bfloat16)
 
 
 def ridge_inverse(gram):
@@ -108,16 +116,17 @@
     first = lax.all_to_all(first, "dst", split_axis=0, concat_axis=0, tiled=True)
     gram_rows = jnp.sum(first[:, :chunk, :], axis=0)
     asked = first[:, chunk, :depth].astype(jnp.int32)
-    spread = jnp.broadcast_to(gram_rows[None], (peers, chunk, width))
-    gram_left = lax.all_to_all(spread, "dst", split_axis=0, concat_axis=0, tiled=True)
-    gram_left = gram_left.reshape(peers * chunk, width)
+    parts = split_bf16(gram_rows)
+    spread = jnp.broadcast_to(parts[None], (peers,) + parts.shape)
     tiles_dst = factor_dst.reshape(factor_dst.shape[0] // edge, edge, width)
-    outgoing = tiles_dst[asked.reshape(peers * depth)].reshape(peers, depth, edge, width)
-    received = lax.all_to_all(outgoing, "dst", split_axis=0, concat_axis=0, tiled=True)
-    received = received.reshape(peers * depth, edge, width)
+    outgoing = tiles_dst[asked.reshape(peers * depth)].reshape(peers, depth * edge, width)
+    outgoing = jnp.concatenate([outgoing, spread], axis=1)
+    arrived = lax.all_to_all(outgoing, "dst", split_axis=0, concat_axis=0, tiled=True)
+    pieces = arrived[:, depth * edge :].astype(jnp.float32).reshape(peers, 3, chunk, width)
+    gram_left = (pieces[:, 0] + pieces[:, 1] + pieces[:, 2]).reshape(peers * chunk, width)
 
     row_blocks = factor_old.shape[0] * peers // edge
-    partial_sum = block_products(slab_blocks, received, places, block_row, factor_slab, row_blocks)
+    partial_sum = block_products(slab_blocks, arrived, places, block_row, factor_slab, row_blocks, depth)
     partial_sum = partial_sum.reshape(row_blocks * edge, width)
     partial_sum, gram_left = lax.optimization_barrier((partial_sum, gram_left))
     summed_rows = scatter_sum(partial_sum, peers)

time: 84.3 us -> 91.4 us (1.084)
  waiting for transfers between devices: 21.9 us -> 33 us
  starting transfers between devices: 15.2 us -> 7.96 us
  other arithmetic: 3.74 us -> 6.8 us
    all_to_all x1, waiting for transfers between devices: 0.01 us -> 6.3 us  [scatter_sum(): lax.all_to_all(pieces, 'dst', split_axis=0, concat_axis=0, tiled=True)]
    all_to_all x1, waiting for transfers between devices: 21.9 us -> 26.7 us  [shards(): lax.all_to_all(outgoing, 'dst', split_axis=0, concat_axis=0, tiled=True)]
    all_to_all x1, starting transfers between devices: 7.15 us -> 3.54 us  [scatter_sum(): lax.all_to_all(pieces, 'dst', split_axis=0, concat_axis=0, tiled=True)]
    all_to_all x1 -> x0, starting transfers between devices: 3.53 us -> none  [shards(): lax.all_to_all(spread, 'dst', split_axis=0, concat_axis=0, tiled=True)]
    concatenate x0 -> x2, other arithmetic: none -> 2.83 us  [the longest x1 2.82 us: shards(): outgoing = jnp.concatenate([outgoing, spread], axis=1)]
    slice x0 -> x1, local copies, waits for them, and re-layouts: none -> 1.02 us  [shards(): arrived[:, depth * edge:].astype(jnp.float32)]
  transfers between devices with their start and end apart: 3 -> 2, of which waited for: 1 -> 2; matrix products, arithmetic and copies ran while one was open for 12% -> 2% of each run, Pallas kernels for 13% -> 0%
where the time goes in v7:
time: 91.4 us; the launch traced here: 90.8 us
  waiting for transfers between devices  33 us (36%)
  blocking collectives  16.8 us (18%)
  Pallas kernels  11.3 us (12%)
  matrix products  9.81 us (11%)
  starting transfers between devices  7.96 us (9%)
  other arithmetic  6.8 us (7%)
  local copies, waits for them, and re-layouts  3.38 us (4%)
  between operations  1.05 us (1%)
    all_to_all x1, waiting for transfers between devices, shards(): lax.all_to_all(outgoing, 'dst', split_axis=0, concat_axis=0, tiled=True)  26.7 us
    all_to_all x1, blocking collectives, shards(): lax.all_to_all(first, 'dst', split_axis=0, concat_axis=0, tiled=True)  16.8 us
    pallas_call x1, Pallas kernels, block_products(): pl.pallas_call(mttkrp_kernel, grid_spec=grid_spec, out_shape=jax.ShapeDty...  11.3 us
    all_to_all x1, waiting for transfers between devices, scatter_sum(): lax.all_to_all(pieces, 'dst', split_axis=0, concat_axis=0, tiled=True)  6.3 us
    all_to_all x1, starting transfers between devices, shards(): lax.all_to_all(outgoing, 'dst', split_axis=0, concat_axis=0, tiled=True)  4.41 us
    all_to_all x1, starting transfers between devices, scatter_sum(): lax.all_to_all(pieces, 'dst', split_axis=0, concat_axis=0, tiled=True)  3.54 us
    dot_general x9, matrix products, ridge_inverse(): jnp.dot(gram, inverse, precision=lax.Precision.HIGHEST)  3.54 us
    dot_general x9, matrix products, ridge_inverse(): jnp.dot(inverse, eye - jnp.dot(gram, inverse, precision=lax.Precision.HIG...  3.53 us
  transfers between devices with their start and end apart: 2, of which 2 were waited for; matrix products, arithmetic and copies ran while one was open for 2% of the time, Pallas kernels for 0%

profile of v7, /device:TPU:0, one launch (start us, length us, event | category | flops | bytes accessed | tf_op | source)
XLA Modules:
  0.0 90.8 jit_solution(13644684090611985421)
XLA Ops:
  0.0 0.0 copy-start
  0.0 1.0 %convert_reduce_fusion = s32[12]{0:T(128)S(1)} fusion(s32[12]{0:T(128)} %bitcast.90), kind=kLoop, calls=%fused_computation.58 | loop fusion | flops 708 | bytes 96 | tf_op jit(solution)/shard_map/reduce_sum | solution.py:108
  1.0 0.7 multiply_add_fusion.places_ref
  1.7 0.7 select_reduce_fusion
  2.4 0.1 convert_element_type.58
  2.5 0.7 fusion.23
  3.3 16.8 %all_to_all.15 = f32[16,17,256]{2,1,0:T(8,128)S(1)} all-to-all(f32[16,17,256]{2,1,0:T(8,128)S(1)} %select_maximum_fusion), channel_id=1, replica_groups=mesh['src'=8,'dst'=16] {'dst'}, dimensions={0} | all-to-all | bytes 557056 | tf_op jit(solution)/shard_map/all_to_all | solution.py:116
  20.1 0.1 convert_element_type.60
  20.3 1.9 %gather_fusion = bf16[48,64,256]{2,1,0:T(8,128)(2,1)} fusion(bf16[64,64,256]{2,1,0:T(8,128)(2,1)S(1)} %bitcast.84, s32[1024]{0:T(1024)S(1)} %pad_clamp_fusion), kind=kCustom, calls=%fused_computation | custom fusion | bytes 3145920 | tf_op jit(solution)/shard_map/gather | solution.py:122
  22.2 2.8 %pad_maximum_fusion = bf16[16,240,256]{2,1,0:T(8,128)(2,1)} fusion(bf16[16,48,256]{2,1,0:T(8,128)(2,1)S(1)} %broadcast_in_dim.16, bf16[16,192,256]{2,1,0:T(8,128)(2,1)} %bitcast.85), kind=kLoop, calls=%fused_computation.7 | loop fusion | flops 3932160 | bytes 3932160 | tf_op jit(solution)/shard_map/concatenate | solution.py:123
  25.0 4.4 %all-to-all-start.1 = ((bf16[16,240,256]{2,1,0:T(8,128)(2,1)}), bf16[16,240,256]{2,1,0:T(8,128)(2,1)}, u32[]{:S(2)}, u32[]{:S(2)}) async-start(bf16[16,240,256]{2,1,0:T(8,128)(2,1)} %pad_maximum_fusion), calls=%async_computation.1 | async-start | bytes 3932160 | tf_op jit(solution)/shard_map/all_to_all | solution.py:124
  29.4 0.0 copy-start.1
  29.4 0.0 copy-start.2
  29.4 26.7 %all-to-all-done.1.left_ref = bf16[16,240,256]{2,1,0:T(8,128)(2,1)} async-done(((bf16[16,240,256]{2,1,0:T(8,128)(2,1)}), bf16[16,240,256]{2,1,0:T(8,128)(2,1)}, u32[]{:S(2)}, u32[]{:S(2)}) %all-to-all-start.1) | async-done | bytes 1966112 | tf_op jit(solution)/shard_map/all_to_all | solution.py:124
  56.1 1.0 %slice.51 = bf16[16,48,256]{2,1,0:T(8,128)(2,1)S(1)} slice(bf16[16,240,256]{2,1,0:T(8,128)(2,1)} %all-to-all-done.1.left_ref), slice={[0:16], [192:240], [0:256]} | slice | bytes 786432 | tf_op jit(solution)/shard_map/slice | solution.py:125
  57.2 0.1 convert.13
  57.3 0.1 fusion.6
  57.3 11.3 %shard_map.73 = f32[4,64,256]{2,1,0:T(8,128)} custom-call(s32[12]{0:T(128)S(1)} %copy-done.2, s32[12]{0:T(128)S(1)} %multiply_add_fusion.places_ref, bf16[12,64,4096]{2,1,0:T(8,128)(2,1)} %x_ref.1, bf16[16,240,256]{2,1,0:T(8,128)(2,1)} %all-to-all-done.1.left_ref, bf16[64,256]{1,0:T(8,128)(2,1)S(1)} %copy-done.1), custom_call_target="tpu_custom_call" | custom-call | flops 1610612736 | bytes 6946816 | tf_op jit(solution)/shard_map/pallas_call | solution.py:46
  68.7 0.1 copy.61
  68.8 0.3 abs_reduce_fusion.1
  69.1 0.1 copy.80
  69.2 0.7 reduce_max.18
  70.6 0.4 convolution_subtract_fusion.9
  71.0 0.4 convolution_add_fusion.8
  71.4 0.4 convolution_subtract_fusion.8
  71.8 0.4 convolution_add_fusion.7
  72.2 0.4 convolution_subtract_fusion.7
  72.6 0.4 convolution_add_fusion.6
  73.0 0.4 convolution_subtract_fusion.6
  73.4 0.4 convolution_add_fusion.5
  73.8 0.4 convolution_subtract_fusion.5
  74.2 0.4 convolution_add_fusion.4
  74.6 0.4 convolution_subtract_fusion.4
  75.0 0.4 convolution_add_fusion.3
  75.4 0.4 convolution_subtract_fusion.3
  75.8 0.4 convolution_add_fusion.2
  76.2 0.4 convolution_subtract_fusion.2
  76.6 0.4 convolution_add_fusion.1
  77.0 0.4 convolution_subtract_fusion.1
  77.4 0.4 convolution_add_fusion
  77.8 3.5 %all-to-all-start.2 = ((f32[16,16,256]{2,1,0:T(8,128)}), f32[16,16,256]{2,1,0:T(8,128)S(1)}, u32[]{:S(2)}, u32[]{:S(2)}) async-start(f32[16,16,256]{2,1,0:T(8,128)} %bitcast.9), calls=%async_computation.2 | async-start | bytes 524288 | tf_op jit(solution)/shard_map/all_to_all | solution.py:63
  81.4 0.0 copy-start.3
  81.4 2.1 %while.14 = (s32[]{:T(128)}, f32[256,256]{0,1:T(8,128)S(1)}, f32[]{:T(128)}, f32[256,256]{1,0:T(8,128)S(1)}, s32[]{:T(128)}, /*index=5*/f32[]{:T(128)}) while((s32[]{:T(128)}, f32[256,256]{0,1:T(8,128)S(1)}, f32[]{:T(128)}, f32[256,256]{1,0:T(8,128)S(1)}, s32[]{:T(128)}, /*index=5*/f32[]{:T(128)}) %tuple.37), condition=%wide.region_9.0_spmd.clone, body=%wide.region_6.9_spmd.clone.sunk | while | flops 403046400 | bytes 2099289 | solution.py:95
  81.4 0.4 abs_reduce_fusion.3
  81.8 0.4 fusion.76
  82.2 0.6 reduce_max.21
  83.5 6.3 %all-to-all-done.2 = f32[16,16,256]{2,1,0:T(8,128)S(1)} async-done(((f32[16,16,256]{2,1,0:T(8,128)}), f32[16,16,256]{2,1,0:T(8,128)S(1)}, u32[]{:S(2)}, u32[]{:S(2)}) %all-to-all-start.2) | async-done | bytes 262176 | tf_op jit(solution)/shard_map/all_to_all | solution.py:63
  89.8 0.9 %fusion.13 = f32[16,256]{1,0:T(8,128)} fusion(f32[256,256]{0,1:T(8,128)S(1)} %get-tuple-element.48, f32[16,256]{1,0:T(8,128)S(1)} %reduce_sum.57, f32[16,256]{1,0:T(8,128)S(1)} %copy-done.3), kind=kOutput, calls=%fused_computation.50 | convolution fusion | flops 12591104 | bytes 311296 | tf_op jit(solution)/shard_map/dot_general | solution.py:138
  (15 shorter events, 0.2 us)
Async XLA Ops:
  0.0 2.5 %copy-start = (bf16[4096,256]{1,0:T(8,128)(2,1)S(1)}, bf16[4096,256]{1,0:T(8,128)(2,1)}, u32[]{:S(2)}) copy-start(bf16[4096,256]{1,0:T(8,128)(2,1)} %param.15) | copy-start | bytes 6291460
  25.0 31.1 %all-to-all-start.1 = ((bf16[16,240,256]{2,1,0:T(8,128)(2,1)}), bf16[16,240,256]{2,1,0:T(8,128)(2,1)}, u32[]{:S(2)}, u32[]{:S(2)}) async-start(bf16[16,240,256]{2,1,0:T(8,128)(2,1)} %pad_maximum_fusion), calls=%async_computation.1 | async-start | bytes 3932160 | tf_op jit(solution)/shard_map/all_to_all | solution.py:124
  29.4 27.9 %copy-start.1 = (bf16[64,256]{1,0:T(8,128)(2,1)S(1)}, bf16[64,256]{1,0:T(8,128)(2,1)}, u32[]{:S(2)}) copy-start(bf16[64,256]{1,0:T(8,128)(2,1)} %slab_ref.1) | copy-start | bytes 98308
  29.4 27.9 %copy-start.2 = (s32[12]{0:T(128)S(1)}, s32[12]{0:T(128)}, u32[]{:S(2)}) copy-start(s32[12]{0:T(128)} %rows_ref.1) | copy-start | bytes 148
  77.8 12.0 %all-to-all-start.2 = ((f32[16,16,256]{2,1,0:T(8,128)}), f32[16,16,256]{2,1,0:T(8,128)S(1)}, u32[]{:S(2)}, u32[]{:S(2)}) async-start(f32[16,16,256]{2,1,0:T(8,128)} %bitcast.9), calls=%async_computation.2 | async-start | bytes 524288 | tf_op jit(solution)/shard_map/all_to_all | solution.py:63
  81.4 8.5 %copy-start.3 = (f32[16,256]{1,0:T(8,128)S(1)}, f32[16,256]{1,0:T(8,128)}, u32[]{:S(2)}) copy-start(f32[16,256]{1,0:T(8,128)} %param.17) | copy-start | bytes 49156

commit v8 on v6

--- a/solution.py
+++ b/solution.py
@@ -10,22 +10,22 @@
 RIDGE = 0.1
 
 
-def mttkrp_kernel(rows_ref, places_ref, x_ref, left_ref, slab_ref, out_ref, kr_ref):
+def mttkrp_kernel(rows_ref, places_ref, x_ref, left_a_ref, left_b_ref, slab_ref, out_ref, kr_ref):
     step = pl.program_id(0)
 
     @pl.when(step == 0)
     def _():
         out_ref[...] = jnp.zeros_like(out_ref)
 
-    left = left_ref[0]
     slab = slab_ref[...]
-    edge = left.shape[0]
     bins = slab.shape[0]
-    for b in range(edge):
-        kr_ref[pl.ds(b * bins, bins), :] = (left[b : b + 1, :] * slab).astype(kr_ref.dtype)
-    prod = jnp.dot(x_ref[0], kr_ref[...], preferred_element_type=jnp.float32)
-    row = rows_ref[step]
-    out_ref[row] = out_ref[row] + prod
+    for half, left_ref in enumerate((left_a_ref, left_b_ref)):
+        left = left_ref[0]
+        for b in range(left.shape[0]):
+            kr_ref[pl.ds(b * bins, bins), :] = (left[b : b + 1, :] * slab).astype(kr_ref.dtype)
+        prod = jnp.dot(x_ref[half], kr_ref[...], preferred_element_type=jnp.float32)
+        row = rows_ref[2 * step + half]
+        out_ref[row] = out_ref[row] + prod
 
 
 def block_products(slab_blocks, received, places, block_row, factor_slab, row_blocks):
@@ -33,10 +33,11 @@
     width = received.shape[2]
     grid_spec = pltpu.PrefetchScalarGridSpec(
         num_scalar_prefetch=2,
-        grid=(count,),
+        grid=(count // 2,),
         in_specs=[
-            pl.BlockSpec((1, edge, depth_k), lambda i, rows, pl_: (i, 0, 0)),
-            pl.BlockSpec((1, received.shape[1], width), lambda i, rows, pl_: (pl_[i], 0, 0)),
+            pl.BlockSpec((2, edge, depth_k), lambda i, rows, pl_: (i, 0, 0)),
+            pl.BlockSpec((1, received.shape[1], width), lambda i, rows, pl_: (pl_[2 * i], 0, 0)),
+            pl.BlockSpec((1, received.shape[1], width), lambda i, rows, pl_: (pl_[2 * i + 1], 0, 0)),
             pl.BlockSpec(factor_slab.shape, lambda i, rows, pl_: (0, 0)),
         ],
         out_specs=pl.BlockSpec((row_blocks, edge, width), lambda i, rows, pl_: (0, 0, 0)),
@@ -55,7 +56,7 @@
             bytes_accessed=slab_blocks.size * 2 + count * edge * width * 2 + row_blocks * edge * width * 4,
             transcendentals=0,
         ),
-    )(block_row, places, slab_blocks, received, factor_slab)
+    )(block_row, places, slab_blocks, received, received, factor_slab)
 
 
 def scatter_sum(rows, peers):

time: 84.3 us -> 81.7 us (0.969)
  Pallas kernels: 11.2 us -> 8.65 us
    pallas_call x1, Pallas kernels: 11.2 us -> 8.65 us  [block_products(): pl.pallas_call(mttkrp_kernel, grid_spec=grid_spec, out_shape=jax.ShapeDty...]
  transfers between devices with their start and end apart: 3 -> 3, of which waited for: 1 -> 1; matrix products, arithmetic and copies ran while one was open for 12% -> 12% of each run, Pallas kernels for 13% -> 11%
where the time goes in v8:
time: 81.7 us; the launch traced here: 80.7 us
  waiting for transfers between devices  21.9 us (27%)
  blocking collectives  16.8 us (21%)
  starting transfers between devices  15.2 us (19%)
  matrix products  9.81 us (12%)
  Pallas kernels  8.65 us (11%)
  other arithmetic  3.74 us (5%)
  local copies, waits for them, and re-layouts  3.06 us (4%)
  between operations  0.92 us (1%)
    all_to_all x1, waiting for transfers between devices, shards(): lax.all_to_all(outgoing, 'dst', split_axis=0, concat_axis=0, tiled=True)  21.9 us
    all_to_all x1, blocking collectives, shards(): lax.all_to_all(first, 'dst', split_axis=0, concat_axis=0, tiled=True)  16.8 us
    pallas_call x1, Pallas kernels, block_products(): pl.pallas_call(mttkrp_kernel, grid_spec=grid_spec, out_shape=jax.ShapeDty...  8.65 us
    all_to_all x1, starting transfers between devices, scatter_sum(): lax.all_to_all(pieces, 'dst', split_axis=0, concat_axis=0, tiled=True)  7.15 us
    all_to_all x1, starting transfers between devices, shards(): lax.all_to_all(outgoing, 'dst', split_axis=0, concat_axis=0, tiled=True)  4.52 us
    dot_general x9, matrix products, ridge_inverse(): jnp.dot(gram, inverse, precision=lax.Precision.HIGHEST)  3.54 us
    all_to_all x1, starting transfers between devices, shards(): lax.all_to_all(spread, 'dst', split_axis=0, concat_axis=0, tiled=True)  3.53 us
    dot_general x9, matrix products, ridge_inverse(): jnp.dot(inverse, eye - jnp.dot(gram, inverse, precision=lax.Precision.HIG...  3.53 us
  transfers between devices with their start and end apart: 3, of which 1 were waited for; matrix products, arithmetic and copies ran while one was open for 12% of the time, Pallas kernels for 11%

profile of v8, /device:TPU:0, one launch (start us, length us, event | category | flops | bytes accessed | tf_op | source)
XLA Modules:
  0.0 80.7 jit_solution(6257706649824058694)
XLA Ops:
  0.0 0.0 copy-start
  0.0 1.0 %convert_reduce_fusion = s32[12]{0:T(128)S(1)} fusion(s32[12]{0:T(128)} %bitcast.74), kind=kLoop, calls=%fused_computation.46 | loop fusion | flops 708 | bytes 96 | tf_op jit(solution)/shard_map/reduce_sum | solution.py:101
  1.0 0.7 multiply_add_fusion.places_ref
  1.7 0.7 select_reduce_fusion
  2.4 0.1 convert_element_type.52
  2.5 0.0 copy-done
  2.5 0.7 fusion.20
  3.3 16.8 %all_to_all.20 = f32[16,17,256]{2,1,0:T(8,128)S(1)} all-to-all(f32[16,17,256]{2,1,0:T(8,128)S(1)} %select_maximum_fusion), channel_id=1, replica_groups=mesh['src'=8,'dst'=16] {'dst'}, dimensions={0} | all-to-all | bytes 557056 | tf_op jit(solution)/shard_map/all_to_all | solution.py:109
  20.1 0.1 convert_element_type.54
  20.2 1.9 %gather_fusion = bf16[48,64,256]{2,1,0:T(8,128)(2,1)} fusion(bf16[64,64,256]{2,1,0:T(8,128)(2,1)S(1)} %bitcast.69, s32[1024]{0:T(1024)S(1)} %pad_clamp_fusion), kind=kCustom, calls=%fused_computation | custom fusion | bytes 3145920 | tf_op jit(solution)/shard_map/gather | solution.py:116
  22.1 4.5 %all-to-all-start.1 = ((bf16[16,3,64,256]{3,2,1,0:T(8,128)(2,1)}), bf16[16,3,64,256]{3,2,1,0:T(8,128)(2,1)}, u32[]{:S(2)}, u32[]{:S(2)}) async-start(bf16[16,3,64,256]{3,2,1,0:T(8,128)(2,1)} %bitcast.70), calls=%async_computation.1 | async-start | bytes 3145728 | tf_op jit(solution)/shard_map/all_to_all | solution.py:117
  26.6 21.9 %all-to-all-done.1 = bf16[16,3,64,256]{3,2,1,0:T(8,128)(2,1)} async-done(((bf16[16,3,64,256]{3,2,1,0:T(8,128)(2,1)}), bf16[16,3,64,256]{3,2,1,0:T(8,128)(2,1)}, u32[]{:S(2)}, u32[]{:S(2)}) %all-to-all-start.1) | async-done | bytes 1572896 | tf_op jit(solution)/shard_map/all_to_all | solution.py:117
  48.6 0.7 broadcast_in_dim.16
  49.3 3.5 %all-to-all-start.2 = ((f32[16,16,256]{2,1,0:T(8,128)}), f32[16,16,256]{2,1,0:T(8,128)S(1)}, u32[]{:S(2)}, u32[]{:S(2)}) async-start(f32[16,16,256]{2,1,0:T(8,128)} %broadcast_in_dim.16), calls=%async_computation.2 | async-start | bytes 524288 | tf_op jit(solution)/shard_map/all_to_all | solution.py:113
  52.8 0.0 copy-done.1
  52.9 0.0 copy-done.2
  52.9 8.7 %shard_map.73 = f32[4,64,256]{2,1,0:T(8,128)} custom-call(s32[12]{0:T(128)S(1)} %copy-done.2, s32[12]{0:T(128)S(1)} %multiply_add_fusion.places_ref, bf16[12,64,4096]{2,1,0:T(8,128)(2,1)} %x_ref.1, bf16[48,64,256]{2,1,0:T(8,128)(2,1)} %bitcast.5.left_a_ref.left_b_ref, bf16[48,64,256]{2,1,0:T(8,128)(2,1)} %bitcast.5.left_a_ref.left_b_ref, ...), custom_call_target="tpu_custom_call" | custom-call | flops 1610612736 | bytes 6946816 | tf_op jit(solution)/shard_map/pallas_call | solution.py:47
  61.5 0.0 all-to-all-done.2
  61.5 7.1 %all-to-all-start.3 = ((f32[16,16,256]{2,1,0:T(8,128)}), f32[16,16,256]{2,1,0:T(8,128)S(1)}, u32[]{:S(2)}, u32[]{:S(2)}) async-start(f32[16,16,256]{2,1,0:T(8,128)} %bitcast.8), calls=%async_computation.3 | async-start | bytes 524288 | tf_op jit(solution)/shard_map/all_to_all | solution.py:64
  68.7 0.1 copy.51
  68.8 0.3 abs_reduce_fusion.1
  69.1 0.1 copy.70
  69.2 0.6 reduce_max.18
  70.4 0.4 convolution_subtract_fusion.9
  70.8 0.4 convolution_add_fusion.8
  71.2 0.4 convolution_subtract_fusion.8
  71.6 0.4 convolution_add_fusion.7
  72.0 0.4 convolution_subtract_fusion.7
  72.4 0.4 convolution_add_fusion.6
  72.8 0.4 convolution_subtract_fusion.6
  73.2 0.4 convolution_add_fusion.5
  73.6 0.4 convolution_subtract_fusion.5
  74.0 0.4 convolution_add_fusion.4
  74.4 0.4 convolution_subtract_fusion.4
  74.8 0.4 convolution_add_fusion.3
  75.2 0.4 convolution_subtract_fusion.3
  75.6 0.4 convolution_add_fusion.2
  76.0 0.4 convolution_subtract_fusion.2
  76.4 0.4 convolution_add_fusion.1
  76.8 0.4 convolution_subtract_fusion.1
  77.2 0.4 convolution_add_fusion
  77.7 0.0 copy-start.3
  77.7 2.1 %while.14 = (s32[]{:T(128)}, f32[256,256]{0,1:T(8,128)S(1)}, f32[]{:T(128)}, f32[256,256]{1,0:T(8,128)S(1)}, s32[]{:T(128)}, /*index=5*/f32[]{:T(128)}) while((s32[]{:T(128)}, f32[256,256]{0,1:T(8,128)S(1)}, f32[]{:T(128)}, f32[256,256]{1,0:T(8,128)S(1)}, s32[]{:T(128)}, /*index=5*/f32[]{:T(128)}) %tuple.35), condition=%wide.region_9.0_spmd.clone, body=%wide.region_6.9_spmd.clone.sunk | while | flops 403046400 | bytes 2099289 | solution.py:88
  77.7 0.4 abs_reduce_fusion.3
  78.1 0.6 reduce_max.21
  78.7 0.4 fusion.73
  79.8 0.0 all-to-all-done.3
  79.8 0.9 %fusion.10 = f32[16,256]{1,0:T(8,128)} fusion(f32[256,256]{0,1:T(8,128)S(1)} %get-tuple-element.48, f32[16,256]{1,0:T(8,128)S(1)} %reduce_sum.57, f32[16,256]{1,0:T(8,128)S(1)} %copy-done.3), kind=kOutput, calls=%fused_computation.38 | convolution fusion | flops 12591104 | bytes 311296 | tf_op jit(solution)/shard_map/dot_general | solution.py:130
  (11 shorter events, 0.1 us)
Async XLA Ops:
  0.0 2.5 %copy-start = (bf16[4096,256]{1,0:T(8,128)(2,1)S(1)}, bf16[4096,256]{1,0:T(8,128)(2,1)}, u32[]{:S(2)}) copy-start(bf16[4096,256]{1,0:T(8,128)(2,1)} %param.15) | copy-start | bytes 6291460
  22.1 30.8 %copy-start.1 = (bf16[64,256]{1,0:T(8,128)(2,1)S(1)}, bf16[64,256]{1,0:T(8,128)(2,1)}, u32[]{:S(2)}) copy-start(bf16[64,256]{1,0:T(8,128)(2,1)} %slab_ref.1) | copy-start | bytes 98308
  22.1 30.8 %copy-start.2 = (s32[12]{0:T(128)S(1)}, s32[12]{0:T(128)}, u32[]{:S(2)}) copy-start(s32[12]{0:T(128)} %rows_ref.1) | copy-start | bytes 148
  22.1 26.5 %all-to-all-start.1 = ((bf16[16,3,64,256]{3,2,1,0:T(8,128)(2,1)}), bf16[16,3,64,256]{3,2,1,0:T(8,128)(2,1)}, u32[]{:S(2)}, u32[]{:S(2)}) async-start(bf16[16,3,64,256]{3,2,1,0:T(8,128)(2,1)} %bitcast.70), calls=%async_computation.1 | async-start | bytes 3145728 | tf_op jit(solution)/shard_map/all_to_all | solution.py:117
  49.3 12.2 %all-to-all-start.2 = ((f32[16,16,256]{2,1,0:T(8,128)}), f32[16,16,256]{2,1,0:T(8,128)S(1)}, u32[]{:S(2)}, u32[]{:S(2)}) async-start(f32[16,16,256]{2,1,0:T(8,128)} %broadcast_in_dim.16), calls=%async_computation.2 | async-start | bytes 524288 | tf_op jit(solution)/shard_map/all_to_all | solution.py:113
  61.5 18.2 %all-to-all-start.3 = ((f32[16,16,256]{2,1,0:T(8,128)}), f32[16,16,256]{2,1,0:T(8,128)S(1)}, u32[]{:S(2)}, u32[]{:S(2)}) async-start(f32[16,16,256]{2,1,0:T(8,128)} %bitcast.8), calls=%async_computation.3 | async-start | bytes 524288 | tf_op jit(solution)/shard_map/all_to_all | solution.py:64
  77.7 2.2 %copy-start.3 = (f32[16,256]{1,0:T(8,128)S(1)}, f32[16,256]{1,0:T(8,128)}, u32[]{:S(2)}) copy-start(f32[16,256]{1,0:T(8,128)} %param.17) | copy-start | bytes 49156

commit v9 on v8

--- a/solution.py
+++ b/solution.py
@@ -10,7 +10,11 @@
 RIDGE = 0.1
 
 
-def mttkrp_kernel(rows_ref, places_ref, x_ref, left_a_ref, left_b_ref, slab_ref, out_ref, kr_ref):
+GROUP = 4
+
+
+def mttkrp_kernel(rows_ref, places_ref, x_ref, *refs):
+    left_refs, (slab_ref, out_ref, kr_ref) = refs[:GROUP], refs[GROUP:]
     step = pl.program_id(0)
 
     @pl.when(step == 0)
@@ -19,13 +23,17 @@
 
     slab = slab_ref[...]
     bins = slab.shape[0]
-    for half, left_ref in enumerate((left_a_ref, left_b_ref)):
+    for part, left_ref in enumerate(left_refs):
         left = left_ref[0]
         for b in range(left.shape[0]):
             kr_ref[pl.ds(b * bins, bins), :] = (left[b : b + 1, :] * slab).astype(kr_ref.dtype)
-        prod = jnp.dot(x_ref[half], kr_ref[...], preferred_element_type=jnp.float32)
-        row = rows_ref[2 * step + half]
+        prod = jnp.dot(x_ref[part], kr_ref[...], preferred_element_type=jnp.float32)
+        row = rows_ref[GROUP * step + part]
         out_ref[row] = out_ref[row] + prod
+
+
+def left_spec(shape, part):
+    return pl.BlockSpec(shape, lambda i, rows, pl_: (pl_[GROUP * i + part], 0, 0))
 
 
 def block_products(slab_blocks, received, places, block_row, factor_slab, row_blocks):
@@ -33,13 +41,10 @@
     width = received.shape[2]
     grid_spec = pltpu.PrefetchScalarGridSpec(
         num_scalar_prefetch=2,
-        grid=(count // 2,),
-        in_specs=[
-            pl.BlockSpec((2, edge, depth_k), lambda i, rows, pl_: (i, 0, 0)),
-            pl.BlockSpec((1, received.shape[1], width), lambda i, rows, pl_: (pl_[2 * i], 0, 0)),
-            pl.BlockSpec((1, received.shape[1], width), lambda i, rows, pl_: (pl_[2 * i + 1], 0, 0)),
-            pl.BlockSpec(factor_slab.shape, lambda i, rows, pl_: (0, 0)),
-        ],
+        grid=(count // GROUP,),
+        in_specs=[pl.BlockSpec((GROUP, edge, depth_k), lambda i, rows, pl_: (i, 0, 0))]
+        + [left_spec((1, received.shape[1], width), part) for part in range(GROUP)]
+        + [pl.BlockSpec(factor_slab.shape, lambda i, rows, pl_: (0, 0))],
         out_specs=pl.BlockSpec((row_blocks, edge, width), lambda i, rows, pl_: (0, 0, 0)),
         scratch_shapes=[pltpu.VMEM((depth_k, width), jnp.bfloat16)],
     )
@@ -56,7 +61,7 @@
             bytes_accessed=slab_blocks.size * 2 + count * edge * width * 2 + row_blocks * edge * width * 4,
             transcendentals=0,
         ),
-    )(block_row, places, slab_blocks, received, received, factor_slab)
+    )(block_row, places, slab_blocks, *([received] * GROUP), factor_slab)
 
 
 def scatter_sum(rows, peers):

time: 81.7 us -> 80.7 us (0.988)
  Pallas kernels: 8.65 us -> 7.79 us
    pallas_call x1, Pallas kernels: 8.65 us -> 7.79 us  [block_products(): pl.pallas_call(mttkrp_kernel, grid_spec=grid_spec, out_shape=jax.ShapeDty...]
  transfers between devices with their start and end apart: 3 -> 3, of which waited for: 1 -> 2; matrix products, arithmetic and copies ran while one was open for 12% -> 12% of each run, Pallas kernels for 11% -> 10%
where the time goes in v9:
time: 80.7 us; the launch traced here: 79.9 us
  waiting for transfers between devices  22.6 us (28%)
  blocking collectives  16.8 us (21%)
  starting transfers between devices  14.6 us (18%)
  matrix products  9.81 us (12%)
  Pallas kernels  7.79 us (10%)
  other arithmetic  3.74 us (5%)
  local copies, waits for them, and re-layouts  3.06 us (4%)
  between operations  0.92 us (1%)
    all_to_all x1, waiting for transfers between devices, shards(): lax.all_to_all(outgoing, 'dst', split_axis=0, concat_axis=0, tiled=True)  21.9 us
    all_to_all x1, blocking collectives, shards(): lax.all_to_all(first, 'dst', split_axis=0, concat_axis=0, tiled=True)  16.8 us
    pallas_call x1, Pallas kernels, block_products(): pl.pallas_call(mttkrp_kernel, grid_spec=grid_spec, out_shape=jax.ShapeDty...  7.79 us
    all_to_all x1, starting transfers between devices, scatter_sum(): lax.all_to_all(pieces, 'dst', split_axis=0, concat_axis=0, tiled=True)  6.53 us
    all_to_all x1, starting transfers between devices, shards(): lax.all_to_all(outgoing, 'dst', split_axis=0, concat_axis=0, tiled=True)  4.52 us
    dot_general x9, matrix products, ridge_inverse(): jnp.dot(gram, inverse, precision=lax.Precision.HIGHEST)  3.53 us
    all_to_all x1, starting transfers between devices, shards(): lax.all_to_all(spread, 'dst', split_axis=0, concat_axis=0, tiled=True)  3.53 us
    dot_general x9, matrix products, ridge_inverse(): jnp.dot(inverse, eye - jnp.dot(gram, inverse, precision=lax.Precision.HIG...  3.53 us
  transfers between devices with their start and end apart: 3, of which 2 were waited for; matrix products, arithmetic and copies ran while one was open for 12% of the time, Pallas kernels for 10%

profile of v9, /device:TPU:0, one launch (start us, length us, event | category | flops | bytes accessed | tf_op | source)
XLA Modules:
  0.0 79.9 jit_solution(7817102983629315825)
XLA Ops:
  0.0 1.0 %convert_reduce_fusion = s32[12]{0:T(128)S(1)} fusion(s32[12]{0:T(128)} %bitcast.74), kind=kLoop, calls=%fused_computation.46 | loop fusion | flops 708 | bytes 96 | tf_op jit(solution)/shard_map/reduce_sum | solution.py:106
  1.0 0.7 multiply_add_fusion.places_ref
  1.7 0.7 select_reduce_fusion
  2.4 0.1 convert_element_type.52
  2.5 0.0 copy-done
  2.5 0.7 fusion.20
  3.3 16.8 %all_to_all.20 = f32[16,17,256]{2,1,0:T(8,128)S(1)} all-to-all(f32[16,17,256]{2,1,0:T(8,128)S(1)} %select_maximum_fusion), channel_id=1, replica_groups=mesh['src'=8,'dst'=16] {'dst'}, dimensions={0} | all-to-all | bytes 557056 | tf_op jit(solution)/shard_map/all_to_all | solution.py:114
  20.1 0.1 convert_element_type.54
  20.2 1.9 %gather_fusion = bf16[48,64,256]{2,1,0:T(8,128)(2,1)} fusion(bf16[64,64,256]{2,1,0:T(8,128)(2,1)S(1)} %bitcast.69, s32[1024]{0:T(1024)S(1)} %pad_clamp_fusion), kind=kCustom, calls=%fused_computation | custom fusion | bytes 3145920 | tf_op jit(solution)/shard_map/gather | solution.py:121
  22.1 4.5 %all-to-all-start.1 = ((bf16[16,3,64,256]{3,2,1,0:T(8,128)(2,1)}), bf16[16,3,64,256]{3,2,1,0:T(8,128)(2,1)}, u32[]{:S(2)}, u32[]{:S(2)}) async-start(bf16[16,3,64,256]{3,2,1,0:T(8,128)(2,1)} %bitcast.70), calls=%async_computation.1 | async-start | bytes 3145728 | tf_op jit(solution)/shard_map/all_to_all | solution.py:122
  26.6 21.9 %all-to-all-done.1 = bf16[16,3,64,256]{3,2,1,0:T(8,128)(2,1)} async-done(((bf16[16,3,64,256]{3,2,1,0:T(8,128)(2,1)}), bf16[16,3,64,256]{3,2,1,0:T(8,128)(2,1)}, u32[]{:S(2)}, u32[]{:S(2)}) %all-to-all-start.1) | async-done | bytes 1572896 | tf_op jit(solution)/shard_map/all_to_all | solution.py:122
  48.6 0.7 broadcast_in_dim.16
  49.3 3.5 %all-to-all-start.2 = ((f32[16,16,256]{2,1,0:T(8,128)}), f32[16,16,256]{2,1,0:T(8,128)S(1)}, u32[]{:S(2)}, u32[]{:S(2)}) async-start(f32[16,16,256]{2,1,0:T(8,128)} %broadcast_in_dim.16), calls=%async_computation.2 | async-start | bytes 524288 | tf_op jit(solution)/shard_map/all_to_all | solution.py:118
  52.8 0.0 copy-done.1
  52.9 0.0 copy-done.2
  52.9 7.8 %shard_map.73 = f32[4,64,256]{2,1,0:T(8,128)} custom-call(s32[12]{0:T(128)S(1)} %copy-done.2, s32[12]{0:T(128)S(1)} %multiply_add_fusion.places_ref, bf16[12,64,4096]{2,1,0:T(8,128)(2,1)} %x_ref.1, bf16[48,64,256]{2,1,0:T(8,128)(2,1)} %bitcast.5.refs_0_.refs_1_.refs_2_.refs_3_, bf16[48,64,256]{2,1,0:T(8,128)(2,1)} %bitcast.5.refs_0_.refs_1_.refs_2_.refs_3_, ...), custom_call_target="tpu_custom_call" | custom-call | flops 1610612736 | bytes 6946816 | tf_op jit(solution)/shard_map/pallas_call | solution.py:52
  60.7 0.6 all-to-all-done.2
  61.3 6.5 %all-to-all-start.3 = ((f32[16,16,256]{2,1,0:T(8,128)}), f32[16,16,256]{2,1,0:T(8,128)S(1)}, u32[]{:S(2)}, u32[]{:S(2)}) async-start(f32[16,16,256]{2,1,0:T(8,128)} %bitcast.8), calls=%async_computation.3 | async-start | bytes 524288 | tf_op jit(solution)/shard_map/all_to_all | solution.py:69
  67.8 0.1 copy.51
  68.0 0.3 abs_reduce_fusion.1
  68.2 0.1 copy.70
  68.4 0.6 reduce_max.18
  69.6 0.4 convolution_subtract_fusion.9
  70.0 0.4 convolution_add_fusion.8
  70.4 0.4 convolution_subtract_fusion.8
  70.8 0.4 convolution_add_fusion.7
  71.2 0.4 convolution_subtract_fusion.7
  71.6 0.4 convolution_add_fusion.6
  72.0 0.4 convolution_subtract_fusion.6
  72.4 0.4 convolution_add_fusion.5
  72.8 0.4 convolution_subtract_fusion.5
  73.2 0.4 convolution_add_fusion.4
  73.6 0.4 convolution_subtract_fusion.4
  74.0 0.4 convolution_add_fusion.3
  74.4 0.4 convolution_subtract_fusion.3
  74.8 0.4 convolution_add_fusion.2
  75.2 0.4 convolution_subtract_fusion.2
  75.6 0.4 convolution_add_fusion.1
  76.0 0.4 convolution_subtract_fusion.1
  76.4 0.4 convolution_add_fusion
  76.8 0.0 copy-start.3
  76.8 2.1 %while.14 = (s32[]{:T(128)}, f32[256,256]{0,1:T(8,128)S(1)}, f32[]{:T(128)}, f32[256,256]{1,0:T(8,128)S(1)}, s32[]{:T(128)}, /*index=5*/f32[]{:T(128)}) while((s32[]{:T(128)}, f32[256,256]{0,1:T(8,128)S(1)}, f32[]{:T(128)}, f32[256,256]{1,0:T(8,128)S(1)}, s32[]{:T(128)}, /*index=5*/f32[]{:T(128)}) %tuple.35), condition=%wide.region_9.0_spmd.clone, body=%wide.region_6.9_spmd.clone.sunk | while | flops 403046400 | bytes 2099289 | solution.py:93
  76.8 0.4 abs_reduce_fusion.3
  77.3 0.6 reduce_max.21
  77.9 0.4 fusion.73
  78.9 0.0 all-to-all-done.3
  78.9 0.0 copy-done.3
  79.0 0.9 %fusion.10 = f32[16,256]{1,0:T(8,128)} fusion(f32[256,256]{0,1:T(8,128)S(1)} %get-tuple-element.48, f32[16,256]{1,0:T(8,128)S(1)} %reduce_sum.57, f32[16,256]{1,0:T(8,128)S(1)} %copy-done.3), kind=kOutput, calls=%fused_computation.38 | convolution fusion | flops 12591104 | bytes 311296 | tf_op jit(solution)/shard_map/dot_general | solution.py:135
  (11 shorter events, 0.1 us)
Async XLA Ops:
  0.0 2.5 %copy-start = (bf16[4096,256]{1,0:T(8,128)(2,1)S(1)}, bf16[4096,256]{1,0:T(8,128)(2,1)}, u32[]{:S(2)}) copy-start(bf16[4096,256]{1,0:T(8,128)(2,1)} %param.15) | copy-start | bytes 6291460
  22.1 30.8 %copy-start.1 = (bf16[64,256]{1,0:T(8,128)(2,1)S(1)}, bf16[64,256]{1,0:T(8,128)(2,1)}, u32[]{:S(2)}) copy-start(bf16[64,256]{1,0:T(8,128)(2,1)} %refs_4_.1) | copy-start | bytes 98308
  22.1 30.8 %copy-start.2 = (s32[12]{0:T(128)S(1)}, s32[12]{0:T(128)}, u32[]{:S(2)}) copy-start(s32[12]{0:T(128)} %rows_ref.1) | copy-start | bytes 148
  22.1 26.5 %all-to-all-start.1 = ((bf16[16,3,64,256]{3,2,1,0:T(8,128)(2,1)}), bf16[16,3,64,256]{3,2,1,0:T(8,128)(2,1)}, u32[]{:S(2)}, u32[]{:S(2)}) async-start(bf16[16,3,64,256]{3,2,1,0:T(8,128)(2,1)} %bitcast.70), calls=%async_computation.1 | async-start | bytes 3145728 | tf_op jit(solution)/shard_map/all_to_all | solution.py:122
  49.3 12.0 %all-to-all-start.2 = ((f32[16,16,256]{2,1,0:T(8,128)}), f32[16,16,256]{2,1,0:T(8,128)S(1)}, u32[]{:S(2)}, u32[]{:S(2)}) async-start(f32[16,16,256]{2,1,0:T(8,128)} %broadcast_in_dim.16), calls=%async_computation.2 | async-start | bytes 524288 | tf_op jit(solution)/shard_map/all_to_all | solution.py:118
  61.3 17.6 %all-to-all-start.3 = ((f32[16,16,256]{2,1,0:T(8,128)}), f32[16,16,256]{2,1,0:T(8,128)S(1)}, u32[]{:S(2)}, u32[]{:S(2)}) async-start(f32[16,16,256]{2,1,0:T(8,128)} %bitcast.8), calls=%async_computation.3 | async-start | bytes 524288 | tf_op jit(solution)/shard_map/all_to_all | solution.py:69
  76.8 2.2 %copy-start.3 = (f32[16,256]{1,0:T(8,128)S(1)}, f32[16,256]{1,0:T(8,128)}, u32[]{:S(2)}) copy-start(f32[16,256]{1,0:T(8,128)} %param.17) | copy-start | bytes 49156

commit v10 on v9

--- a/solution.py
+++ b/solution.py
@@ -70,6 +70,19 @@
     return jnp.sum(arrived, axis=0)
 
 
+def gather_rows(rows, peers):
+    me = lax.axis_index("dst")
+    held = rows
+    distance = 1
+    while distance < peers:
+        pairs = [(i, i ^ distance) for i in range(peers)]
+        other = lax.ppermute(held, "dst", perm=pairs)
+        low = (me & distance) == 0
+        held = jnp.where(low, jnp.concatenate([held, other]), jnp.concatenate([other, held]))
+        distance *= 2
+    return held
+
+
 def ridge_inverse(gram):
     eye = jnp.eye(gram.shape[0], dtype=jnp.float32)
     start = eye / jnp.max(jnp.sum(jnp.abs(gram), axis=1))
@@ -114,18 +127,16 @@
     first = lax.all_to_all(first, "dst", split_axis=0, concat_axis=0, tiled=True)
     gram_rows = jnp.sum(first[:, :chunk, :], axis=0)
     asked = first[:, chunk, :depth].astype(jnp.int32)
-    spread = jnp.broadcast_to(gram_rows[None], (peers, chunk, width))
-    gram_left = lax.all_to_all(spread, "dst", split_axis=0, concat_axis=0, tiled=True)
-    gram_left = gram_left.reshape(peers * chunk, width)
     tiles_dst = factor_dst.reshape(factor_dst.shape[0] // edge, edge, width)
     outgoing = tiles_dst[asked.reshape(peers * depth)].reshape(peers, depth, edge, width)
     received = lax.all_to_all(outgoing, "dst", split_axis=0, concat_axis=0, tiled=True)
+    gram_rows, outgoing = lax.optimization_barrier((gram_rows, outgoing))
+    gram_left = gather_rows(gram_rows, peers)
     received = received.reshape(peers * depth, edge, width)
 
     row_blocks = factor_old.shape[0] * peers // edge
     partial_sum = block_products(slab_blocks, received, places, block_row, factor_slab, row_blocks)
     partial_sum = partial_sum.reshape(row_blocks * edge, width)
-    partial_sum, gram_left = lax.optimization_barrier((partial_sum, gram_left))
     summed_rows = scatter_sum(partial_sum, peers)
 
     gram_right = jnp.dot(factor_slab.T, factor_slab, preferred_element_type=jnp.float32)

time: 80.7 us -> 85 us (1.053)
  waiting for transfers between devices: 22.6 us -> 30.3 us
  starting transfers between devices: 14.6 us -> 11.9 us
    ppermute x0 -> x4, waiting for transfers between devices: none -> 16 us  [gather_rows(): other = lax.ppermute(held, 'dst', perm=pairs)]
    all_to_all x1, waiting for transfers between devices: 21.9 us -> 7.94 us  [shards(): lax.all_to_all(outgoing, 'dst', split_axis=0, concat_axis=0, tiled=True)]
    all_to_all x1, waiting for transfers between devices: 0.01 us -> 6.45 us  [scatter_sum(): lax.all_to_all(pieces, 'dst', split_axis=0, concat_axis=0, tiled=True)]
    ppermute x0 -> x4, starting transfers between devices: none -> 3.97 us  [gather_rows(): other = lax.ppermute(held, 'dst', perm=pairs)]
    all_to_all x1 -> x0, starting transfers between devices: 3.53 us -> none  [shards(): lax.all_to_all(spread, 'dst', split_axis=0, concat_axis=0, tiled=True)]
    all_to_all x1, starting transfers between devices: 6.53 us -> 3.53 us  [scatter_sum(): lax.all_to_all(pieces, 'dst', split_axis=0, concat_axis=0, tiled=True)]
  transfers between devices with their start and end apart: 3 -> 6, of which waited for: 2 -> 6; matrix products, arithmetic and copies ran while one was open for 12% -> 11% of each run, Pallas kernels for 10% -> 0%
where the time goes in v10:
time: 85 us; the launch traced here: 84.6 us
  waiting for transfers between devices  30.3 us (36%)
  blocking collectives  16.8 us (20%)
  starting transfers between devices  11.9 us (14%)
  matrix products  9.89 us (12%)
  Pallas kernels  7.79 us (9%)
  other arithmetic  4 us (5%)
  local copies, waits for them, and re-layouts  2.39 us (3%)
  between operations  0.96 us (1%)
    all_to_all x1, blocking collectives, shards(): lax.all_to_all(first, 'dst', split_axis=0, concat_axis=0, tiled=True)  16.8 us
    ppermute x4, waiting for transfers between devices, gather_rows(): other = lax.ppermute(held, 'dst', perm=pairs)  16 us
    all_to_all x1, waiting for transfers between devices, shards(): lax.all_to_all(outgoing, 'dst', split_axis=0, concat_axis=0, tiled=True)  7.94 us
    pallas_call x1, Pallas kernels, block_products(): pl.pallas_call(mttkrp_kernel, grid_spec=grid_spec, out_shape=jax.ShapeDty...  7.79 us
    all_to_all x1, waiting for transfers between devices, scatter_sum(): lax.all_to_all(pieces, 'dst', split_axis=0, concat_axis=0, tiled=True)  6.45 us
    all_to_all x1, starting transfers between devices, shards(): lax.all_to_all(outgoing, 'dst', split_axis=0, concat_axis=0, tiled=True)  4.39 us
    ppermute x4, starting transfers between devices, gather_rows(): other = lax.ppermute(held, 'dst', perm=pairs)  3.97 us
    dot_general x9, matrix products, ridge_inverse(): jnp.dot(gram, inverse, precision=lax.Precision.HIGHEST)  3.59 us
  transfers between devices with their start and end apart: 6, of which 6 were waited for; matrix products, arithmetic and copies ran while one was open for 11% of the time, Pallas kernels for 0%

profile of v10, /device:TPU:0, one launch (start us, length us, event | category | flops | bytes accessed | tf_op | source)
XLA Modules:
  0.0 84.6 jit_solution(4099488332122900948)
XLA Ops:
  0.0 1.0 %convert_reduce_fusion = s32[12]{0:T(128)S(1)} fusion(s32[12]{0:T(128)} %bitcast.71), kind=kLoop, calls=%fused_computation.52 | loop fusion | flops 708 | bytes 96 | tf_op jit(solution)/shard_map/reduce_sum | solution.py:119
  1.0 0.7 multiply_add_fusion.places_ref
  1.7 0.7 select_reduce_fusion
  2.5 0.7 fusion.22
  3.3 16.8 %all_to_all.15 = f32[16,17,256]{2,1,0:T(8,128)S(1)} all-to-all(f32[16,17,256]{2,1,0:T(8,128)S(1)} %select_maximum_fusion), channel_id=1, replica_groups=mesh['src'=8,'dst'=16] {'dst'}, dimensions={0} | all-to-all | bytes 557056 | tf_op jit(solution)/shard_map/all_to_all | solution.py:127
  20.2 1.9 %gather_fusion = bf16[48,64,256]{2,1,0:T(8,128)(2,1)} fusion(bf16[64,64,256]{2,1,0:T(8,128)(2,1)S(1)} %bitcast.67, s32[1024]{0:T(1024)S(1)} %pad_clamp_fusion), kind=kCustom, calls=%fused_computation | custom fusion | bytes 3145920 | tf_op jit(solution)/shard_map/gather | solution.py:131
  22.1 0.4 collective-permute-start
  22.5 3.4 %collective-permute-done = f32[16,256]{1,0:T(8,128)S(1)} collective-permute-done((f32[16,256]{1,0:T(8,128)S(1)}, f32[16,256]{1,0:T(8,128)S(1)}, u32[]{:S(2)}, u32[]{:S(2)}) %collective-permute-start) | collective-permute-done | bytes 16416 | tf_op jit(solution)/shard_map/ppermute | solution.py:79
  25.9 0.1 copy.54
  26.2 1.5 %collective-permute-start.1 = (f32[32,256]{0,1:T(8,128)S(1)}, f32[32,256]{0,1:T(8,128)S(1)}, u32[]{:S(2)}, u32[]{:S(2)}) collective-permute-start(f32[32,256]{0,1:T(8,128)S(1)} %broadcast_select_fusion), channel_id=1, source_target_pairs={{0,2},{1,3},{2,0},{3,1},{4,6},{5,7},{6,4},{7,5},{8,10},{9,11},{10,... | collective-permute-start | bytes 98312 | tf_op jit(solution)/shard_map/ppermute | solution.py:79
  27.7 5.0 %collective-permute-done.1 = f32[32,256]{0,1:T(8,128)S(1)} collective-permute-done((f32[32,256]{0,1:T(8,128)S(1)}, f32[32,256]{0,1:T(8,128)S(1)}, u32[]{:S(2)}, u32[]{:S(2)}) %collective-permute-start.1) | collective-permute-done | bytes 32800 | tf_op jit(solution)/shard_map/ppermute | solution.py:79
  32.7 0.1 maximum_select_fusion.1
  32.8 0.1 collective-permute-start.2
  33.0 5.8 %collective-permute-done.2 = f32[64,256]{0,1:T(8,128)S(1)} collective-permute-done((f32[64,256]{0,1:T(8,128)S(1)}, f32[64,256]{0,1:T(8,128)S(1)}, u32[]{:S(2)}, u32[]{:S(2)}) %collective-permute-start.2) | collective-permute-done | bytes 65568 | tf_op jit(solution)/shard_map/ppermute | solution.py:79
  38.8 0.1 maximum_select_fusion.2
  38.9 1.9 %collective-permute-start.3 = (f32[128,256]{0,1:T(8,128)S(1)}, f32[128,256]{0,1:T(8,128)S(1)}, u32[]{:S(2)}, u32[]{:S(2)}) collective-permute-start(f32[128,256]{0,1:T(8,128)S(1)} %maximum_select_fusion.2), channel_id=1, source_target_pairs={{0,8},{1,9},{2,10},{3,11},{4,12},{5,13},{6,14},{7,15},{8,0},{9,1},... | collective-permute-start | bytes 393224 | tf_op jit(solution)/shard_map/ppermute | solution.py:79
  40.8 4.4 %all-to-all-start.1 = ((bf16[16,3,64,256]{3,2,1,0:T(8,128)(2,1)}), bf16[16,3,64,256]{3,2,1,0:T(8,128)(2,1)}, u32[]{:S(2)}, u32[]{:S(2)}) async-start(bf16[16,3,64,256]{3,2,1,0:T(8,128)(2,1)} %bitcast.68), calls=%async_computation.1 | async-start | bytes 3145728 | tf_op jit(solution)/shard_map/all_to_all | solution.py:132
  45.2 1.7 %collective-permute-done.3 = f32[128,256]{0,1:T(8,128)S(1)} collective-permute-done((f32[128,256]{0,1:T(8,128)S(1)}, f32[128,256]{0,1:T(8,128)S(1)}, u32[]{:S(2)}, u32[]{:S(2)}) %collective-permute-start.3) | collective-permute-done | bytes 131104 | tf_op jit(solution)/shard_map/ppermute | solution.py:79
  46.9 0.3 abs_reduce_fusion.1
  47.2 0.6 reduce_max.18
  48.5 0.4 convolution_subtract_fusion.9
  48.9 0.4 convolution_add_fusion.8
  49.3 0.4 convolution_subtract_fusion.8
  49.7 0.4 convolution_add_fusion.7
  50.1 0.4 convolution_subtract_fusion.7
  50.5 0.4 convolution_add_fusion.6
  50.9 0.4 convolution_subtract_fusion.6
  51.3 0.4 convolution_add_fusion.5
  51.7 0.4 convolution_subtract_fusion.5
  52.1 0.4 convolution_add_fusion.4
  52.5 0.4 convolution_subtract_fusion.4
  52.9 0.4 convolution_add_fusion.3
  53.4 0.1 copy.73
  53.5 0.4 convolution_subtract_fusion.3
  53.9 0.4 convolution_add_fusion.2
  54.3 0.4 convolution_subtract_fusion.2
  54.7 0.4 convolution_add_fusion.1
  55.1 0.4 convolution_subtract_fusion.1
  55.5 0.4 convolution_add_fusion
  55.9 7.9 %all-to-all-done.1 = bf16[16,3,64,256]{3,2,1,0:T(8,128)(2,1)} async-done(((bf16[16,3,64,256]{3,2,1,0:T(8,128)(2,1)}), bf16[16,3,64,256]{3,2,1,0:T(8,128)(2,1)}, u32[]{:S(2)}, u32[]{:S(2)}) %all-to-all-start.1) | async-done | bytes 1572896 | tf_op jit(solution)/shard_map/all_to_all | solution.py:132
  63.9 7.8 %shard_map.73 = f32[4,64,256]{2,1,0:T(8,128)} custom-call(s32[12]{0:T(128)S(1)} %copy-done.2, s32[12]{0:T(128)S(1)} %multiply_add_fusion.places_ref, bf16[12,64,4096]{2,1,0:T(8,128)(2,1)} %x_ref.1, bf16[48,64,256]{2,1,0:T(8,128)(2,1)} %bitcast.5.refs_0_.refs_1_.refs_2_.refs_3_, bf16[48,64,256]{2,1,0:T(8,128)(2,1)} %bitcast.5.refs_0_.refs_1_.refs_2_.refs_3_, ...), custom_call_target="tpu_custom_call" | custom-call | flops 1610612736 | bytes 6946816 | tf_op jit(solution)/shard_map/pallas_call | solution.py:52
  71.7 3.5 %all-to-all-start.2 = ((f32[16,16,256]{2,1,0:T(8,128)}), f32[16,16,256]{2,1,0:T(8,128)S(1)}, u32[]{:S(2)}, u32[]{:S(2)}) async-start(f32[16,16,256]{2,1,0:T(8,128)} %bitcast.6), calls=%async_computation.2 | async-start | bytes 524288 | tf_op jit(solution)/shard_map/all_to_all | solution.py:69
  75.2 2.0 %while.14 = (s32[]{:T(128)}, f32[256,256]{0,1:T(8,128)S(1)}, f32[]{:T(128)}, f32[256,256]{1,0:T(8,128)S(1)}, s32[]{:T(128)}, /*index=5*/f32[]{:T(128)}) while((s32[]{:T(128)}, f32[256,256]{0,1:T(8,128)S(1)}, f32[]{:T(128)}, f32[256,256]{1,0:T(8,128)S(1)}, s32[]{:T(128)}, /*index=5*/f32[]{:T(128)}) %tuple.36), condition=%wide.region_9.10_spmd.clone, body=%wide.region_6.9_spmd.clone.sunk | while | flops 403046400 | bytes 2099289 | solution.py:106
  75.3 0.4 abs_reduce_fusion.3
  75.7 0.6 reduce_max.21
  76.3 0.4 fusion.75
  77.2 6.4 %all-to-all-done.2 = f32[16,16,256]{2,1,0:T(8,128)S(1)} async-done(((f32[16,16,256]{2,1,0:T(8,128)}), f32[16,16,256]{2,1,0:T(8,128)S(1)}, u32[]{:S(2)}, u32[]{:S(2)}) %all-to-all-start.2) | async-done | bytes 262176 | tf_op jit(solution)/shard_map/all_to_all | solution.py:69
  83.7 0.9 %fusion.11 = f32[16,256]{1,0:T(8,128)} fusion(f32[256,256]{0,1:T(8,128)S(1)} %get-tuple-element.46, f32[16,256]{1,0:T(8,128)S(1)} %reduce_sum.56, f32[16,256]{1,0:T(8,128)S(1)} %copy-done.3), kind=kOutput, calls=%fused_computation.44 | convolution fusion | flops 12591104 | bytes 311296 | tf_op jit(solution)/shard_map/dot_general | solution.py:146
  (21 shorter events, 0.4 us)
Async XLA Ops:
  0.0 2.5 %copy-start = (bf16[4096,256]{1,0:T(8,128)(2,1)S(1)}, bf16[4096,256]{1,0:T(8,128)(2,1)}, u32[]{:S(2)}) copy-start(bf16[4096,256]{1,0:T(8,128)(2,1)} %param.15) | copy-start | bytes 6291460
  22.1 3.8 %collective-permute-start = (f32[16,256]{1,0:T(8,128)S(1)}, f32[16,256]{1,0:T(8,128)S(1)}, u32[]{:S(2)}, u32[]{:S(2)}) collective-permute-start(f32[16,256]{1,0:T(8,128)S(1)} %slice_reduce_fusion), channel_id=1, source_target_pairs={{0,1},{1,0},{2,3},{3,2},{4,5},{5,4},{6,7},{7,6},{8,9},{9,8},{10,11... | collective-permute-start | bytes 49160 | tf_op jit(solution)/shard_map/ppermute | solution.py:79
  26.1 20.8 %copy-start.1 = (bf16[64,256]{1,0:T(8,128)(2,1)S(1)}, bf16[64,256]{1,0:T(8,128)(2,1)}, u32[]{:S(2)}) copy-start(bf16[64,256]{1,0:T(8,128)(2,1)} %refs_4_.1) | copy-start | bytes 98308
  26.2 6.6 %collective-permute-start.1 = (f32[32,256]{0,1:T(8,128)S(1)}, f32[32,256]{0,1:T(8,128)S(1)}, u32[]{:S(2)}, u32[]{:S(2)}) collective-permute-start(f32[32,256]{0,1:T(8,128)S(1)} %broadcast_select_fusion), channel_id=1, source_target_pairs={{0,2},{1,3},{2,0},{3,1},{4,6},{5,7},{6,4},{7,5},{8,10},{9,11},{10,... | collective-permute-start | bytes 98312 | tf_op jit(solution)/shard_map/ppermute | solution.py:79
  32.8 5.9 %collective-permute-start.2 = (f32[64,256]{0,1:T(8,128)S(1)}, f32[64,256]{0,1:T(8,128)S(1)}, u32[]{:S(2)}, u32[]{:S(2)}) collective-permute-start(f32[64,256]{0,1:T(8,128)S(1)} %maximum_select_fusion.1), channel_id=1, source_target_pairs={{0,4},{1,5},{2,6},{3,7},{4,0},{5,1},{6,2},{7,3},{8,12},{9,13},{10,... | collective-permute-start | bytes 196616 | tf_op jit(solution)/shard_map/ppermute | solution.py:79
  38.9 8.1 %collective-permute-start.3 = (f32[128,256]{0,1:T(8,128)S(1)}, f32[128,256]{0,1:T(8,128)S(1)}, u32[]{:S(2)}, u32[]{:S(2)}) collective-permute-start(f32[128,256]{0,1:T(8,128)S(1)} %maximum_select_fusion.2), channel_id=1, source_target_pairs={{0,8},{1,9},{2,10},{3,11},{4,12},{5,13},{6,14},{7,15},{8,0},{9,1},... | collective-permute-start | bytes 393224 | tf_op jit(solution)/shard_map/ppermute | solution.py:79
  40.8 23.1 %all-to-all-start.1 = ((bf16[16,3,64,256]{3,2,1,0:T(8,128)(2,1)}), bf16[16,3,64,256]{3,2,1,0:T(8,128)(2,1)}, u32[]{:S(2)}, u32[]{:S(2)}) async-start(bf16[16,3,64,256]{3,2,1,0:T(8,128)(2,1)} %bitcast.68), calls=%async_computation.1 | async-start | bytes 3145728 | tf_op jit(solution)/shard_map/all_to_all | solution.py:132
  53.9 10.0 %copy-start.2 = (s32[12]{0:T(128)S(1)}, s32[12]{0:T(128)}, u32[]{:S(2)}) copy-start(s32[12]{0:T(128)} %rows_ref.1) | copy-start | bytes 148
  71.7 12.0 %all-to-all-start.2 = ((f32[16,16,256]{2,1,0:T(8,128)}), f32[16,16,256]{2,1,0:T(8,128)S(1)}, u32[]{:S(2)}, u32[]{:S(2)}) async-start(f32[16,16,256]{2,1,0:T(8,128)} %bitcast.6), calls=%async_computation.2 | async-start | bytes 524288 | tf_op jit(solution)/shard_map/all_to_all | solution.py:69
  75.2 8.5 %copy-start.3 = (f32[16,256]{1,0:T(8,128)S(1)}, f32[16,256]{1,0:T(8,128)}, u32[]{:S(2)}) copy-start(f32[16,256]{1,0:T(8,128)} %param.17) | copy-start | bytes 49156

commit v11 on v9

--- a/solution.py
+++ b/solution.py
@@ -86,10 +86,9 @@
         return steps + 1, inverse, norm
 
     inverse = start
-    for _ in range(9):
-        inverse = inverse + jnp.dot(
-            inverse, eye - jnp.dot(gram, inverse, precision=lax.Precision.HIGHEST), precision=lax.Precision.HIGHEST
-        )
+    for count in range(9):
+        level = lax.Precision.HIGH if count < 6 else lax.Precision.HIGHEST
+        inverse = inverse + jnp.dot(inverse, eye - jnp.dot(gram, inverse, precision=level), precision=level)
     _, inverse, _ = lax.while_loop(going, step, (jnp.int32(0), inverse, jnp.float32(2.0)))
     return inverse
 

time: 80.7 us -> 79.4 us (0.984)
  matrix products: 9.81 us -> 8.48 us
    dot_general x18, matrix products: 7.07 us -> 5.74 us  [the longest x9 2.87 us: ridge_inverse(): jnp.dot(inverse, eye - jnp.dot(gram, inverse, precision=level), precision...]
  transfers between devices with their start and end apart: 3 -> 3, of which waited for: 2 -> 2; matrix products, arithmetic and copies ran while one was open for 12% -> 11% of each run, Pallas kernels for 10% -> 10%
where the time goes in v11:
time: 79.4 us; the launch traced here: 78.6 us
  waiting for transfers between devices  22.6 us (28%)
  blocking collectives  16.8 us (21%)
  starting transfers between devices  14.6 us (18%)
  matrix products  8.48 us (11%)
  Pallas kernels  7.8 us (10%)
  other arithmetic  3.74 us (5%)
  local copies, waits for them, and re-layouts  3.06 us (4%)
  between operations  0.92 us (1%)
    all_to_all x1, waiting for transfers between devices, shards(): lax.all_to_all(outgoing, 'dst', split_axis=0, concat_axis=0, tiled=True)  21.9 us
    all_to_all x1, blocking collectives, shards(): lax.all_to_all(first, 'dst', split_axis=0, concat_axis=0, tiled=True)  16.8 us
    pallas_call x1, Pallas kernels, block_products(): pl.pallas_call(mttkrp_kernel, grid_spec=grid_spec, out_shape=jax.ShapeDty...  7.8 us
    all_to_all x1, starting transfers between devices, scatter_sum(): lax.all_to_all(pieces, 'dst', split_axis=0, concat_axis=0, tiled=True)  6.53 us
    all_to_all x1, starting transfers between devices, shards(): lax.all_to_all(outgoing, 'dst', split_axis=0, concat_axis=0, tiled=True)  4.52 us
    all_to_all x1, starting transfers between devices, shards(): lax.all_to_all(spread, 'dst', split_axis=0, concat_axis=0, tiled=True)  3.53 us
    dot_general x9, matrix products, ridge_inverse(): jnp.dot(inverse, eye - jnp.dot(gram, inverse, precision=level), precision...  2.87 us
    dot_general x9, matrix products, ridge_inverse(): jnp.dot(gram, inverse, precision=level)  2.87 us
  transfers between devices with their start and end apart: 3, of which 2 were waited for; matrix products, arithmetic and copies ran while one was open for 11% of the time, Pallas kernels for 10%

profile of v11, /device:TPU:0, one launch (start us, length us, event | category | flops | bytes accessed | tf_op | source)
XLA Modules:
  0.0 78.6 jit_solution(4414623321356724235)
XLA Ops:
  0.0 0.0 copy-start
  0.0 1.0 %convert_reduce_fusion = s32[12]{0:T(128)S(1)} fusion(s32[12]{0:T(128)} %bitcast.74), kind=kLoop, calls=%fused_computation.46 | loop fusion | flops 708 | bytes 96 | tf_op jit(solution)/shard_map/reduce_sum | solution.py:105
  1.0 0.7 multiply_add_fusion.places_ref
  1.7 0.7 select_reduce_fusion
  2.4 0.1 convert_element_type.52
  2.5 0.0 copy-done
  2.5 0.7 fusion.20
  3.3 16.8 %all_to_all.20 = f32[16,17,256]{2,1,0:T(8,128)S(1)} all-to-all(f32[16,17,256]{2,1,0:T(8,128)S(1)} %select_maximum_fusion), channel_id=1, replica_groups=mesh['src'=8,'dst'=16] {'dst'}, dimensions={0} | all-to-all | bytes 557056 | tf_op jit(solution)/shard_map/all_to_all | solution.py:113
  20.1 0.1 convert_element_type.54
  20.2 1.9 %gather_fusion = bf16[48,64,256]{2,1,0:T(8,128)(2,1)} fusion(bf16[64,64,256]{2,1,0:T(8,128)(2,1)S(1)} %bitcast.69, s32[1024]{0:T(1024)S(1)} %pad_clamp_fusion), kind=kCustom, calls=%fused_computation | custom fusion | bytes 3145920 | tf_op jit(solution)/shard_map/gather | solution.py:120
  22.1 4.5 %all-to-all-start.1 = ((bf16[16,3,64,256]{3,2,1,0:T(8,128)(2,1)}), bf16[16,3,64,256]{3,2,1,0:T(8,128)(2,1)}, u32[]{:S(2)}, u32[]{:S(2)}) async-start(bf16[16,3,64,256]{3,2,1,0:T(8,128)(2,1)} %bitcast.70), calls=%async_computation.1 | async-start | bytes 3145728 | tf_op jit(solution)/shard_map/all_to_all | solution.py:121
  26.6 21.9 %all-to-all-done.1 = bf16[16,3,64,256]{3,2,1,0:T(8,128)(2,1)} async-done(((bf16[16,3,64,256]{3,2,1,0:T(8,128)(2,1)}), bf16[16,3,64,256]{3,2,1,0:T(8,128)(2,1)}, u32[]{:S(2)}, u32[]{:S(2)}) %all-to-all-start.1) | async-done | bytes 1572896 | tf_op jit(solution)/shard_map/all_to_all | solution.py:121
  48.6 0.7 broadcast_in_dim.16
  49.3 3.5 %all-to-all-start.2 = ((f32[16,16,256]{2,1,0:T(8,128)}), f32[16,16,256]{2,1,0:T(8,128)S(1)}, u32[]{:S(2)}, u32[]{:S(2)}) async-start(f32[16,16,256]{2,1,0:T(8,128)} %broadcast_in_dim.16), calls=%async_computation.2 | async-start | bytes 524288 | tf_op jit(solution)/shard_map/all_to_all | solution.py:117
  52.8 0.0 copy-done.1
  52.9 0.0 copy-done.2
  52.9 7.8 %shard_map.73 = f32[4,64,256]{2,1,0:T(8,128)} custom-call(s32[12]{0:T(128)S(1)} %copy-done.2, s32[12]{0:T(128)S(1)} %multiply_add_fusion.places_ref, bf16[12,64,4096]{2,1,0:T(8,128)(2,1)} %x_ref.1, bf16[48,64,256]{2,1,0:T(8,128)(2,1)} %bitcast.5.refs_0_.refs_1_.refs_2_.refs_3_, bf16[48,64,256]{2,1,0:T(8,128)(2,1)} %bitcast.5.refs_0_.refs_1_.refs_2_.refs_3_, ...), custom_call_target="tpu_custom_call" | custom-call | flops 1610612736 | bytes 6946816 | tf_op jit(solution)/shard_map/pallas_call | solution.py:52
  60.7 0.6 all-to-all-done.2
  61.3 6.5 %all-to-all-start.3 = ((f32[16,16,256]{2,1,0:T(8,128)}), f32[16,16,256]{2,1,0:T(8,128)S(1)}, u32[]{:S(2)}, u32[]{:S(2)}) async-start(f32[16,16,256]{2,1,0:T(8,128)} %bitcast.8), calls=%async_computation.3 | async-start | bytes 524288 | tf_op jit(solution)/shard_map/all_to_all | solution.py:69
  67.8 0.1 copy.51
  68.0 0.3 abs_reduce_fusion.1
  68.2 0.1 copy.70
  68.4 0.6 reduce_max.18
  69.6 0.3 convolution_subtract_fusion.9
  69.9 0.3 convolution_add_fusion.8
  70.2 0.3 convolution_subtract_fusion.8
  70.5 0.3 convolution_add_fusion.7
  70.7 0.3 convolution_subtract_fusion.7
  71.0 0.3 convolution_add_fusion.6
  71.3 0.3 convolution_subtract_fusion.6
  71.6 0.3 convolution_add_fusion.5
  71.9 0.3 convolution_subtract_fusion.5
  72.2 0.3 convolution_add_fusion.4
  72.5 0.3 convolution_subtract_fusion.4
  72.8 0.3 convolution_add_fusion.3
  73.1 0.4 convolution_subtract_fusion.3
  73.5 0.4 convolution_add_fusion.2
  73.9 0.4 convolution_subtract_fusion.2
  74.3 0.4 convolution_add_fusion.1
  74.7 0.4 convolution_subtract_fusion.1
  75.1 0.4 convolution_add_fusion
  75.5 0.0 copy-start.3
  75.5 2.1 %while.14 = (s32[]{:T(128)}, f32[256,256]{0,1:T(8,128)S(1)}, f32[]{:T(128)}, f32[256,256]{1,0:T(8,128)S(1)}, s32[]{:T(128)}, /*index=5*/f32[]{:T(128)}) while((s32[]{:T(128)}, f32[256,256]{0,1:T(8,128)S(1)}, f32[]{:T(128)}, f32[256,256]{1,0:T(8,128)S(1)}, s32[]{:T(128)}, /*index=5*/f32[]{:T(128)}) %tuple.35), condition=%wide.region_9.0_spmd.clone, body=%wide.region_6.9_spmd.clone.sunk | while | flops 403046400 | bytes 2099289 | solution.py:92
  75.5 0.4 abs_reduce_fusion.3
  76.0 0.6 reduce_max.21
  76.6 0.4 fusion.73
  77.6 0.0 all-to-all-done.3
  77.6 0.9 %fusion.10 = f32[16,256]{1,0:T(8,128)} fusion(f32[256,256]{0,1:T(8,128)S(1)} %get-tuple-element.48, f32[16,256]{1,0:T(8,128)S(1)} %reduce_sum.57, f32[16,256]{1,0:T(8,128)S(1)} %copy-done.3), kind=kOutput, calls=%fused_computation.38 | convolution fusion | flops 12591104 | bytes 311296 | tf_op jit(solution)/shard_map/dot_general | solution.py:134
  (11 shorter events, 0.1 us)
Async XLA Ops:
  0.0 2.5 %copy-start = (bf16[4096,256]{1,0:T(8,128)(2,1)S(1)}, bf16[4096,256]{1,0:T(8,128)(2,1)}, u32[]{:S(2)}) copy-start(bf16[4096,256]{1,0:T(8,128)(2,1)} %param.15) | copy-start | bytes 6291460
  22.1 30.8 %copy-start.1 = (bf16[64,256]{1,0:T(8,128)(2,1)S(1)}, bf16[64,256]{1,0:T(8,128)(2,1)}, u32[]{:S(2)}) copy-start(bf16[64,256]{1,0:T(8,128)(2,1)} %refs_4_.1) | copy-start | bytes 98308
  22.1 30.8 %copy-start.2 = (s32[12]{0:T(128)S(1)}, s32[12]{0:T(128)}, u32[]{:S(2)}) copy-start(s32[12]{0:T(128)} %rows_ref.1) | copy-start | bytes 148
  22.1 26.5 %all-to-all-start.1 = ((bf16[16,3,64,256]{3,2,1,0:T(8,128)(2,1)}), bf16[16,3,64,256]{3,2,1,0:T(8,128)(2,1)}, u32[]{:S(2)}, u32[]{:S(2)}) async-start(bf16[16,3,64,256]{3,2,1,0:T(8,128)(2,1)} %bitcast.70), calls=%async_computation.1 | async-start | bytes 3145728 | tf_op jit(solution)/shard_map/all_to_all | solution.py:121
  49.3 12.0 %all-to-all-start.2 = ((f32[16,16,256]{2,1,0:T(8,128)}), f32[16,16,256]{2,1,0:T(8,128)S(1)}, u32[]{:S(2)}, u32[]{:S(2)}) async-start(f32[16,16,256]{2,1,0:T(8,128)} %broadcast_in_dim.16), calls=%async_computation.2 | async-start | bytes 524288 | tf_op jit(solution)/shard_map/all_to_all | solution.py:117
  61.3 16.3 %all-to-all-start.3 = ((f32[16,16,256]{2,1,0:T(8,128)}), f32[16,16,256]{2,1,0:T(8,128)S(1)}, u32[]{:S(2)}, u32[]{:S(2)}) async-start(f32[16,16,256]{2,1,0:T(8,128)} %bitcast.8), calls=%async_computation.3 | async-start | bytes 524288 | tf_op jit(solution)/shard_map/all_to_all | solution.py:69
  75.5 2.2 %copy-start.3 = (f32[16,256]{1,0:T(8,128)S(1)}, f32[16,256]{1,0:T(8,128)}, u32[]{:S(2)}) copy-start(f32[16,256]{1,0:T(8,128)} %param.17) | copy-start | bytes 49156

commit v12 on v11

--- a/solution.py
+++ b/solution.py
@@ -87,7 +87,7 @@
 
     inverse = start
     for count in range(9):
-        level = lax.Precision.HIGH if count < 6 else lax.Precision.HIGHEST
+        level = lax.Precision.DEFAULT if count < 6 else lax.Precision.HIGHEST
         inverse = inverse + jnp.dot(inverse, eye - jnp.dot(gram, inverse, precision=level), precision=level)
     _, inverse, _ = lax.while_loop(going, step, (jnp.int32(0), inverse, jnp.float32(2.0)))
     return inverse

time: 79.4 us -> 77.9 us (0.981)
  matrix products: 8.48 us -> 7.08 us
    dot_general x9 -> x3, matrix products: 2.87 us -> 1.18 us  [ridge_inverse(): jnp.dot(gram, inverse, precision=level)]
  transfers between devices with their start and end apart: 3 -> 3, of which waited for: 2 -> 3; matrix products, arithmetic and copies ran while one was open for 11% -> 9% of each run, Pallas kernels for 10% -> 10%
where the time goes in v12:
time: 77.9 us; the launch traced here: 77.3 us
  waiting for transfers between devices  22.7 us (29%)
  blocking collectives  16.8 us (22%)
  starting transfers between devices  14.6 us (19%)
  Pallas kernels  7.8 us (10%)
  matrix products  7.08 us (9%)
  other arithmetic  3.74 us (5%)
  local copies, waits for them, and re-layouts  3.06 us (4%)
  between operations  0.86 us (1%)
    all_to_all x1, waiting for transfers between devices, shards(): lax.all_to_all(outgoing, 'dst', split_axis=0, concat_axis=0, tiled=True)  21.9 us
    all_to_all x1, blocking collectives, shards(): lax.all_to_all(first, 'dst', split_axis=0, concat_axis=0, tiled=True)  16.8 us
    pallas_call x1, Pallas kernels, block_products(): pl.pallas_call(mttkrp_kernel, grid_spec=grid_spec, out_shape=jax.ShapeDty...  7.8 us
    all_to_all x1, starting transfers between devices, scatter_sum(): lax.all_to_all(pieces, 'dst', split_axis=0, concat_axis=0, tiled=True)  6.53 us
    all_to_all x1, starting transfers between devices, shards(): lax.all_to_all(outgoing, 'dst', split_axis=0, concat_axis=0, tiled=True)  4.52 us
    all_to_all x1, starting transfers between devices, shards(): lax.all_to_all(spread, 'dst', split_axis=0, concat_axis=0, tiled=True)  3.53 us
    dot_general x9, matrix products, ridge_inverse(): jnp.dot(inverse, eye - jnp.dot(gram, inverse, precision=level), precision...  3.16 us
    gather x1, local copies, waits for them, and re-layouts, shards(): tiles_dst[asked.reshape(peers * depth)].reshape(peers, depth, edge, width)  1.86 us
  transfers between devices with their start and end apart: 3, of which 3 were waited for; matrix products, arithmetic and copies ran while one was open for 9% of the time, Pallas kernels for 10%

profile of v12, /device:TPU:0, one launch (start us, length us, event | category | flops | bytes accessed | tf_op | source)
XLA Modules:
  0.0 77.3 jit_solution(7171994320233821900)
XLA Ops:
  0.0 0.0 copy-start
  0.0 1.0 %convert_reduce_fusion = s32[12]{0:T(128)S(1)} fusion(s32[12]{0:T(128)} %bitcast.68), kind=kLoop, calls=%fused_computation.49 | loop fusion | flops 708 | bytes 96 | tf_op jit(solution)/shard_map/reduce_sum | solution.py:105
  1.0 0.7 multiply_add_fusion.places_ref
  1.7 0.7 select_reduce_fusion
  2.4 0.1 convert_element_type.52
  2.5 0.0 copy-done
  2.5 0.7 fusion.26
  3.3 16.8 %all_to_all.20 = f32[16,17,256]{2,1,0:T(8,128)S(1)} all-to-all(f32[16,17,256]{2,1,0:T(8,128)S(1)} %select_maximum_fusion), channel_id=1, replica_groups=mesh['src'=8,'dst'=16] {'dst'}, dimensions={0} | all-to-all | bytes 557056 | tf_op jit(solution)/shard_map/all_to_all | solution.py:113
  20.1 0.1 convert_element_type.54
  20.2 1.9 %gather_fusion = bf16[48,64,256]{2,1,0:T(8,128)(2,1)} fusion(bf16[64,64,256]{2,1,0:T(8,128)(2,1)S(1)} %bitcast.63, s32[1024]{0:T(1024)S(1)} %pad_clamp_fusion), kind=kCustom, calls=%fused_computation | custom fusion | bytes 3145920 | tf_op jit(solution)/shard_map/gather | solution.py:120
  22.1 0.0 copy-start.1
  22.1 0.0 copy-start.2
  22.1 4.5 %all-to-all-start.1 = ((bf16[16,3,64,256]{3,2,1,0:T(8,128)(2,1)}), bf16[16,3,64,256]{3,2,1,0:T(8,128)(2,1)}, u32[]{:S(2)}, u32[]{:S(2)}) async-start(bf16[16,3,64,256]{3,2,1,0:T(8,128)(2,1)} %bitcast.64), calls=%async_computation.1 | async-start | bytes 3145728 | tf_op jit(solution)/shard_map/all_to_all | solution.py:121
  26.6 21.9 %all-to-all-done.1 = bf16[16,3,64,256]{3,2,1,0:T(8,128)(2,1)} async-done(((bf16[16,3,64,256]{3,2,1,0:T(8,128)(2,1)}), bf16[16,3,64,256]{3,2,1,0:T(8,128)(2,1)}, u32[]{:S(2)}, u32[]{:S(2)}) %all-to-all-start.1) | async-done | bytes 1572896 | tf_op jit(solution)/shard_map/all_to_all | solution.py:121
  48.6 0.7 broadcast_in_dim.16
  49.3 3.5 %all-to-all-start.2 = ((f32[16,16,256]{2,1,0:T(8,128)}), f32[16,16,256]{2,1,0:T(8,128)S(1)}, u32[]{:S(2)}, u32[]{:S(2)}) async-start(f32[16,16,256]{2,1,0:T(8,128)} %broadcast_in_dim.16), calls=%async_computation.2 | async-start | bytes 524288 | tf_op jit(solution)/shard_map/all_to_all | solution.py:117
  52.8 0.0 copy-done.1
  52.9 0.0 copy-done.2
  52.9 7.8 %shard_map.73 = f32[4,64,256]{2,1,0:T(8,128)} custom-call(s32[12]{0:T(128)S(1)} %copy-done.2, s32[12]{0:T(128)S(1)} %multiply_add_fusion.places_ref, bf16[12,64,4096]{2,1,0:T(8,128)(2,1)} %x_ref.1, bf16[48,64,256]{2,1,0:T(8,128)(2,1)} %bitcast.5.refs_0_.refs_1_.refs_2_.refs_3_, bf16[48,64,256]{2,1,0:T(8,128)(2,1)} %bitcast.5.refs_0_.refs_1_.refs_2_.refs_3_, ...), custom_call_target="tpu_custom_call" | custom-call | flops 1610612736 | bytes 6946816 | tf_op jit(solution)/shard_map/pallas_call | solution.py:52
  60.7 0.6 all-to-all-done.2
  61.3 6.5 %all-to-all-start.3 = ((f32[16,16,256]{2,1,0:T(8,128)}), f32[16,16,256]{2,1,0:T(8,128)S(1)}, u32[]{:S(2)}, u32[]{:S(2)}) async-start(f32[16,16,256]{2,1,0:T(8,128)} %bitcast.8), calls=%async_computation.3 | async-start | bytes 524288 | tf_op jit(solution)/shard_map/all_to_all | solution.py:69
  67.8 0.1 copy.51
  68.0 0.3 abs_reduce_fusion.1
  68.2 0.1 copy.70
  68.4 0.6 reduce_max.18
  69.6 0.3 convolution_add_fusion.8
  69.9 0.3 convolution_add_fusion.7
  70.3 0.3 convolution_add_fusion.6
  70.6 0.3 convolution_add_fusion.5
  70.9 0.3 convolution_add_fusion.4
  71.3 0.3 convolution_add_fusion.3
  71.6 0.4 convolution_subtract_fusion.3
  72.0 0.4 convolution_add_fusion.2
  72.4 0.4 convolution_subtract_fusion.2
  72.8 0.4 convolution_add_fusion.1
  73.2 0.4 convolution_subtract_fusion.1
  73.6 0.4 convolution_add_fusion
  74.0 0.0 copy-start.3
  74.0 2.1 %while.14 = (s32[]{:T(128)}, f32[256,256]{0,1:T(8,128)S(1)}, f32[]{:T(128)}, f32[256,256]{1,0:T(8,128)S(1)}, s32[]{:T(128)}, /*index=5*/f32[]{:T(128)}) while((s32[]{:T(128)}, f32[256,256]{0,1:T(8,128)S(1)}, f32[]{:T(128)}, f32[256,256]{1,0:T(8,128)S(1)}, s32[]{:T(128)}, /*index=5*/f32[]{:T(128)}) %tuple.35), condition=%wide.region_9.0_spmd.clone, body=%wide.region_6.9_spmd.clone.sunk | while | flops 403046400 | bytes 2099289 | solution.py:92
  74.1 0.4 abs_reduce_fusion.3
  74.5 0.6 reduce_max.21
  75.1 0.4 fusion.73
  76.1 0.2 all-to-all-done.3
  76.3 0.0 copy-done.3
  76.3 0.9 %fusion.16 = f32[16,256]{1,0:T(8,128)} fusion(f32[256,256]{0,1:T(8,128)S(1)} %get-tuple-element.48, f32[16,256]{1,0:T(8,128)S(1)} %reduce_sum.57, f32[16,256]{1,0:T(8,128)S(1)} %copy-done.3), kind=kOutput, calls=%fused_computation.41 | convolution fusion | flops 12591104 | bytes 311296 | tf_op jit(solution)/shard_map/dot_general | solution.py:134
  (8 shorter events, 0.1 us)
Async XLA Ops:
  0.0 2.5 %copy-start = (bf16[4096,256]{1,0:T(8,128)(2,1)S(1)}, bf16[4096,256]{1,0:T(8,128)(2,1)}, u32[]{:S(2)}) copy-start(bf16[4096,256]{1,0:T(8,128)(2,1)} %param.15) | copy-start | bytes 6291460
  22.1 30.8 %copy-start.1 = (bf16[64,256]{1,0:T(8,128)(2,1)S(1)}, bf16[64,256]{1,0:T(8,128)(2,1)}, u32[]{:S(2)}) copy-start(bf16[64,256]{1,0:T(8,128)(2,1)} %refs_4_.1) | copy-start | bytes 98308
  22.1 30.8 %copy-start.2 = (s32[12]{0:T(128)S(1)}, s32[12]{0:T(128)}, u32[]{:S(2)}) copy-start(s32[12]{0:T(128)} %rows_ref.1) | copy-start | bytes 148
  22.1 26.5 %all-to-all-start.1 = ((bf16[16,3,64,256]{3,2,1,0:T(8,128)(2,1)}), bf16[16,3,64,256]{3,2,1,0:T(8,128)(2,1)}, u32[]{:S(2)}, u32[]{:S(2)}) async-start(bf16[16,3,64,256]{3,2,1,0:T(8,128)(2,1)} %bitcast.64), calls=%async_computation.1 | async-start | bytes 3145728 | tf_op jit(solution)/shard_map/all_to_all | solution.py:121
  49.3 12.0 %all-to-all-start.2 = ((f32[16,16,256]{2,1,0:T(8,128)}), f32[16,16,256]{2,1,0:T(8,128)S(1)}, u32[]{:S(2)}, u32[]{:S(2)}) async-start(f32[16,16,256]{2,1,0:T(8,128)} %broadcast_in_dim.16), calls=%async_computation.2 | async-start | bytes 524288 | tf_op jit(solution)/shard_map/all_to_all | solution.py:117
  61.3 15.0 %all-to-all-start.3 = ((f32[16,16,256]{2,1,0:T(8,128)}), f32[16,16,256]{2,1,0:T(8,128)S(1)}, u32[]{:S(2)}, u32[]{:S(2)}) async-start(f32[16,16,256]{2,1,0:T(8,128)} %bitcast.8), calls=%async_computation.3 | async-start | bytes 524288 | tf_op jit(solution)/shard_map/all_to_all | solution.py:69
  74.0 2.3 %copy-start.3 = (f32[16,256]{1,0:T(8,128)S(1)}, f32[16,256]{1,0:T(8,128)}, u32[]{:S(2)}) copy-start(f32[16,256]{1,0:T(8,128)} %param.17) | copy-start | bytes 49156

commit v13 on v12

--- a/solution.py
+++ b/solution.py
@@ -10,7 +10,7 @@
 RIDGE = 0.1
 
 
-GROUP = 4
+GROUP = 6
 
 
 def mttkrp_kernel(rows_ref, places_ref, x_ref, *refs):

time: 77.9 us -> 78.1 us (level)
  no operation moved by 1% of the time
where the time goes in v13:
time: 78.1 us; the launch traced here: 77.4 us
  waiting for transfers between devices  22.6 us (29%)
  blocking collectives  16.8 us (22%)
  starting transfers between devices  14.8 us (19%)
  Pallas kernels  7.97 us (10%)
  matrix products  7.09 us (9%)
  other arithmetic  3.74 us (5%)
  local copies, waits for them, and re-layouts  3.06 us (4%)
  between operations  0.86 us (1%)
    all_to_all x1, waiting for transfers between devices, shards(): lax.all_to_all(outgoing, 'dst', split_axis=0, concat_axis=0, tiled=True)  21.9 us
    all_to_all x1, blocking collectives, shards(): lax.all_to_all(first, 'dst', split_axis=0, concat_axis=0, tiled=True)  16.8 us
    pallas_call x1, Pallas kernels, block_products(): pl.pallas_call(mttkrp_kernel, grid_spec=grid_spec, out_shape=jax.ShapeDty...  7.97 us
    all_to_all x1, starting transfers between devices, scatter_sum(): lax.all_to_all(pieces, 'dst', split_axis=0, concat_axis=0, tiled=True)  6.71 us
    all_to_all x1, starting transfers between devices, shards(): lax.all_to_all(outgoing, 'dst', split_axis=0, concat_axis=0, tiled=True)  4.52 us
    all_to_all x1, starting transfers between devices, shards(): lax.all_to_all(spread, 'dst', split_axis=0, concat_axis=0, tiled=True)  3.53 us
    dot_general x9, matrix products, ridge_inverse(): jnp.dot(inverse, eye - jnp.dot(gram, inverse, precision=level), precision...  3.16 us
    gather x1, local copies, waits for them, and re-layouts, shards(): tiles_dst[asked.reshape(peers * depth)].reshape(peers, depth, edge, width)  1.86 us
  transfers between devices with their start and end apart: 3, of which 3 were waited for; matrix products, arithmetic and copies ran while one was open for 9% of the time, Pallas kernels for 10%

profile of v13, /device:TPU:0, one launch (start us, length us, event | category | flops | bytes accessed | tf_op | source)
XLA Modules:
  0.0 77.4 jit_solution(14817215351748699442)
XLA Ops:
  0.0 0.0 copy-start
  0.0 1.0 %convert_reduce_fusion = s32[12]{0:T(128)S(1)} fusion(s32[12]{0:T(128)} %bitcast.68), kind=kLoop, calls=%fused_computation.49 | loop fusion | flops 708 | bytes 96 | tf_op jit(solution)/shard_map/reduce_sum | solution.py:105
  1.0 0.7 multiply_add_fusion.places_ref
  1.7 0.7 select_reduce_fusion
  2.4 0.1 convert_element_type.52
  2.5 0.0 copy-done
  2.5 0.7 fusion.26
  3.3 16.8 %all_to_all.20 = f32[16,17,256]{2,1,0:T(8,128)S(1)} all-to-all(f32[16,17,256]{2,1,0:T(8,128)S(1)} %select_maximum_fusion), channel_id=1, replica_groups=mesh['src'=8,'dst'=16] {'dst'}, dimensions={0} | all-to-all | bytes 557056 | tf_op jit(solution)/shard_map/all_to_all | solution.py:113
  20.1 0.1 convert_element_type.54
  20.2 1.9 %gather_fusion = bf16[48,64,256]{2,1,0:T(8,128)(2,1)} fusion(bf16[64,64,256]{2,1,0:T(8,128)(2,1)S(1)} %bitcast.63, s32[1024]{0:T(1024)S(1)} %pad_clamp_fusion), kind=kCustom, calls=%fused_computation | custom fusion | bytes 3145920 | tf_op jit(solution)/shard_map/gather | solution.py:120
  22.1 0.0 copy-start.1
  22.1 0.0 copy-start.2
  22.1 4.5 %all-to-all-start.1 = ((bf16[16,3,64,256]{3,2,1,0:T(8,128)(2,1)}), bf16[16,3,64,256]{3,2,1,0:T(8,128)(2,1)}, u32[]{:S(2)}, u32[]{:S(2)}) async-start(bf16[16,3,64,256]{3,2,1,0:T(8,128)(2,1)} %bitcast.64), calls=%async_computation.1 | async-start | bytes 3145728 | tf_op jit(solution)/shard_map/all_to_all | solution.py:121
  26.6 21.9 %all-to-all-done.1 = bf16[16,3,64,256]{3,2,1,0:T(8,128)(2,1)} async-done(((bf16[16,3,64,256]{3,2,1,0:T(8,128)(2,1)}), bf16[16,3,64,256]{3,2,1,0:T(8,128)(2,1)}, u32[]{:S(2)}, u32[]{:S(2)}) %all-to-all-start.1) | async-done | bytes 1572896 | tf_op jit(solution)/shard_map/all_to_all | solution.py:121
  48.6 0.7 broadcast_in_dim.16
  49.3 3.5 %all-to-all-start.2 = ((f32[16,16,256]{2,1,0:T(8,128)}), f32[16,16,256]{2,1,0:T(8,128)S(1)}, u32[]{:S(2)}, u32[]{:S(2)}) async-start(f32[16,16,256]{2,1,0:T(8,128)} %broadcast_in_dim.16), calls=%async_computation.2 | async-start | bytes 524288 | tf_op jit(solution)/shard_map/all_to_all | solution.py:117
  52.8 0.0 copy-done.1
  52.9 0.0 copy-done.2
  52.9 8.0 %shard_map.73 = f32[4,64,256]{2,1,0:T(8,128)} custom-call(s32[12]{0:T(128)S(1)} %copy-done.2, s32[12]{0:T(128)S(1)} %multiply_add_fusion.places_ref, bf16[12,64,4096]{2,1,0:T(8,128)(2,1)} %x_ref.1, bf16[48,64,256]{2,1,0:T(8,128)(2,1)} %bitcast.5.refs_0_.refs_1_.refs_2_.refs_3_.refs_4_.refs_5_, ...), custom_call_target="tpu_custom_call" | custom-call | flops 1610612736 | bytes 6946816 | tf_op jit(solution)/shard_map/pallas_call | solution.py:52
  60.8 0.5 all-to-all-done.2
  61.3 6.7 %all-to-all-start.3 = ((f32[16,16,256]{2,1,0:T(8,128)}), f32[16,16,256]{2,1,0:T(8,128)S(1)}, u32[]{:S(2)}, u32[]{:S(2)}) async-start(f32[16,16,256]{2,1,0:T(8,128)} %bitcast.8), calls=%async_computation.3 | async-start | bytes 524288 | tf_op jit(solution)/shard_map/all_to_all | solution.py:69
  68.0 0.1 copy.51
  68.1 0.3 abs_reduce_fusion.1
  68.4 0.1 copy.70
  68.5 0.6 reduce_max.18
  69.8 0.3 convolution_add_fusion.8
  70.1 0.3 convolution_add_fusion.7
  70.4 0.3 convolution_add_fusion.6
  70.8 0.3 convolution_add_fusion.5
  71.1 0.3 convolution_add_fusion.4
  71.5 0.3 convolution_add_fusion.3
  71.8 0.4 convolution_subtract_fusion.3
  72.2 0.4 convolution_add_fusion.2
  72.6 0.4 convolution_subtract_fusion.2
  73.0 0.4 convolution_add_fusion.1
  73.4 0.4 convolution_subtract_fusion.1
  73.8 0.4 convolution_add_fusion
  74.2 0.0 copy-start.3
  74.2 2.1 %while.14 = (s32[]{:T(128)}, f32[256,256]{0,1:T(8,128)S(1)}, f32[]{:T(128)}, f32[256,256]{1,0:T(8,128)S(1)}, s32[]{:T(128)}, /*index=5*/f32[]{:T(128)}) while((s32[]{:T(128)}, f32[256,256]{0,1:T(8,128)S(1)}, f32[]{:T(128)}, f32[256,256]{1,0:T(8,128)S(1)}, s32[]{:T(128)}, /*index=5*/f32[]{:T(128)}) %tuple.35), condition=%wide.region_9.0_spmd.clone, body=%wide.region_6.9_spmd.clone.sunk | while | flops 403046400 | bytes 2099289 | solution.py:92
  74.3 0.4 abs_reduce_fusion.3
  74.7 0.6 reduce_max.21
  75.3 0.4 fusion.73
  76.3 0.2 all-to-all-done.3
  76.5 0.0 copy-done.3
  76.5 0.9 %fusion.16 = f32[16,256]{1,0:T(8,128)} fusion(f32[256,256]{0,1:T(8,128)S(1)} %get-tuple-element.48, f32[16,256]{1,0:T(8,128)S(1)} %reduce_sum.57, f32[16,256]{1,0:T(8,128)S(1)} %copy-done.3), kind=kOutput, calls=%fused_computation.41 | convolution fusion | flops 12591104 | bytes 311296 | tf_op jit(solution)/shard_map/dot_general | solution.py:134
  (8 shorter events, 0.1 us)
Async XLA Ops:
  0.0 2.5 %copy-start = (bf16[4096,256]{1,0:T(8,128)(2,1)S(1)}, bf16[4096,256]{1,0:T(8,128)(2,1)}, u32[]{:S(2)}) copy-start(bf16[4096,256]{1,0:T(8,128)(2,1)} %param.15) | copy-start | bytes 6291460
  22.1 30.8 %copy-start.1 = (bf16[64,256]{1,0:T(8,128)(2,1)S(1)}, bf16[64,256]{1,0:T(8,128)(2,1)}, u32[]{:S(2)}) copy-start(bf16[64,256]{1,0:T(8,128)(2,1)} %refs_6_.1) | copy-start | bytes 98308
  22.1 30.8 %copy-start.2 = (s32[12]{0:T(128)S(1)}, s32[12]{0:T(128)}, u32[]{:S(2)}) copy-start(s32[12]{0:T(128)} %rows_ref.1) | copy-start | bytes 148
  22.1 26.5 %all-to-all-start.1 = ((bf16[16,3,64,256]{3,2,1,0:T(8,128)(2,1)}), bf16[16,3,64,256]{3,2,1,0:T(8,128)(2,1)}, u32[]{:S(2)}, u32[]{:S(2)}) async-start(bf16[16,3,64,256]{3,2,1,0:T(8,128)(2,1)} %bitcast.64), calls=%async_computation.1 | async-start | bytes 3145728 | tf_op jit(solution)/shard_map/all_to_all | solution.py:121
  49.3 12.0 %all-to-all-start.2 = ((f32[16,16,256]{2,1,0:T(8,128)}), f32[16,16,256]{2,1,0:T(8,128)S(1)}, u32[]{:S(2)}, u32[]{:S(2)}) async-start(f32[16,16,256]{2,1,0:T(8,128)} %broadcast_in_dim.16), calls=%async_computation.2 | async-start | bytes 524288 | tf_op jit(solution)/shard_map/all_to_all | solution.py:117
  61.3 15.2 %all-to-all-start.3 = ((f32[16,16,256]{2,1,0:T(8,128)}), f32[16,16,256]{2,1,0:T(8,128)S(1)}, u32[]{:S(2)}, u32[]{:S(2)}) async-start(f32[16,16,256]{2,1,0:T(8,128)} %bitcast.8), calls=%async_computation.3 | async-start | bytes 524288 | tf_op jit(solution)/shard_map/all_to_all | solution.py:69
  74.2 2.3 %copy-start.3 = (f32[16,256]{1,0:T(8,128)S(1)}, f32[16,256]{1,0:T(8,128)}, u32[]{:S(2)}) copy-start(f32[16,256]{1,0:T(8,128)} %param.17) | copy-start | bytes 49156

commit v14 on v12

--- a/solution.py
+++ b/solution.py
@@ -86,8 +86,8 @@
         return steps + 1, inverse, norm
 
     inverse = start
-    for count in range(9):
-        level = lax.Precision.DEFAULT if count < 6 else lax.Precision.HIGHEST
+    for _ in range(9):
+        level = lax.Precision.HIGH
         inverse = inverse + jnp.dot(inverse, eye - jnp.dot(gram, inverse, precision=level), precision=level)
     _, inverse, _ = lax.while_loop(going, step, (jnp.int32(0), inverse, jnp.float32(2.0)))
     return inverse

time: 77.9 us -> 78.7 us (1.010)
    dot_general x3 -> x9, matrix products: 1.18 us -> 2.54 us  [ridge_inverse(): jnp.dot(gram, inverse, precision=level)]
  transfers between devices with their start and end apart: 3 -> 3, of which waited for: 3 -> 2; matrix products, arithmetic and copies ran while one was open for 9% -> 10% of each run, Pallas kernels for 10% -> 10%
where the time goes in v14:
time: 78.7 us; the launch traced here: 77.9 us
  waiting for transfers between devices  22.6 us (29%)
  blocking collectives  16.8 us (21%)
  starting transfers between devices  14.6 us (19%)
  matrix products  7.82 us (10%)
  Pallas kernels  7.8 us (10%)
  other arithmetic  3.74 us (5%)
  local copies, waits for them, and re-layouts  3.06 us (4%)
  between operations  0.92 us (1%)
    all_to_all x1, waiting for transfers between devices, shards(): lax.all_to_all(outgoing, 'dst', split_axis=0, concat_axis=0, tiled=True)  21.9 us
    all_to_all x1, blocking collectives, shards(): lax.all_to_all(first, 'dst', split_axis=0, concat_axis=0, tiled=True)  16.8 us
    pallas_call x1, Pallas kernels, block_products(): pl.pallas_call(mttkrp_kernel, grid_spec=grid_spec, out_shape=jax.ShapeDty...  7.8 us
    all_to_all x1, starting transfers between devices, scatter_sum(): lax.all_to_all(pieces, 'dst', split_axis=0, concat_axis=0, tiled=True)  6.53 us
    all_to_all x1, starting transfers between devices, shards(): lax.all_to_all(outgoing, 'dst', split_axis=0, concat_axis=0, tiled=True)  4.52 us
    all_to_all x1, starting transfers between devices, shards(): lax.all_to_all(spread, 'dst', split_axis=0, concat_axis=0, tiled=True)  3.53 us
    dot_general x9, matrix products, ridge_inverse(): jnp.dot(gram, inverse, precision=level)  2.54 us
    dot_general x9, matrix products, ridge_inverse(): jnp.dot(inverse, eye - jnp.dot(gram, inverse, precision=level), precision...  2.53 us
  transfers between devices with their start and end apart: 3, of which 2 were waited for; matrix products, arithmetic and copies ran while one was open for 10% of the time, Pallas kernels for 10%

profile of v14, /device:TPU:0, one launch (start us, length us, event | category | flops | bytes accessed | tf_op | source)
XLA Modules:
  0.0 77.9 jit_solution(13377358279074239076)
XLA Ops:
  0.0 1.0 %convert_reduce_fusion = s32[12]{0:T(128)S(1)} fusion(s32[12]{0:T(128)} %bitcast.74), kind=kLoop, calls=%fused_computation.46 | loop fusion | flops 708 | bytes 96 | tf_op jit(solution)/shard_map/reduce_sum | solution.py:105
  1.0 0.7 multiply_add_fusion.places_ref
  1.7 0.7 select_reduce_fusion
  2.4 0.1 convert_element_type.52
  2.5 0.0 copy-done
  2.5 0.7 fusion.20
  3.3 16.8 %all_to_all.20 = f32[16,17,256]{2,1,0:T(8,128)S(1)} all-to-all(f32[16,17,256]{2,1,0:T(8,128)S(1)} %select_maximum_fusion), channel_id=1, replica_groups=mesh['src'=8,'dst'=16] {'dst'}, dimensions={0} | all-to-all | bytes 557056 | tf_op jit(solution)/shard_map/all_to_all | solution.py:113
  20.1 0.1 convert_element_type.54
  20.2 1.9 %gather_fusion = bf16[48,64,256]{2,1,0:T(8,128)(2,1)} fusion(bf16[64,64,256]{2,1,0:T(8,128)(2,1)S(1)} %bitcast.69, s32[1024]{0:T(1024)S(1)} %pad_clamp_fusion), kind=kCustom, calls=%fused_computation | custom fusion | bytes 3145920 | tf_op jit(solution)/shard_map/gather | solution.py:120
  22.1 4.5 %all-to-all-start.1 = ((bf16[16,3,64,256]{3,2,1,0:T(8,128)(2,1)}), bf16[16,3,64,256]{3,2,1,0:T(8,128)(2,1)}, u32[]{:S(2)}, u32[]{:S(2)}) async-start(bf16[16,3,64,256]{3,2,1,0:T(8,128)(2,1)} %bitcast.70), calls=%async_computation.1 | async-start | bytes 3145728 | tf_op jit(solution)/shard_map/all_to_all | solution.py:121
  26.6 21.9 %all-to-all-done.1 = bf16[16,3,64,256]{3,2,1,0:T(8,128)(2,1)} async-done(((bf16[16,3,64,256]{3,2,1,0:T(8,128)(2,1)}), bf16[16,3,64,256]{3,2,1,0:T(8,128)(2,1)}, u32[]{:S(2)}, u32[]{:S(2)}) %all-to-all-start.1) | async-done | bytes 1572896 | tf_op jit(solution)/shard_map/all_to_all | solution.py:121
  48.6 0.7 broadcast_in_dim.16
  49.3 3.5 %all-to-all-start.2 = ((f32[16,16,256]{2,1,0:T(8,128)}), f32[16,16,256]{2,1,0:T(8,128)S(1)}, u32[]{:S(2)}, u32[]{:S(2)}) async-start(f32[16,16,256]{2,1,0:T(8,128)} %broadcast_in_dim.16), calls=%async_computation.2 | async-start | bytes 524288 | tf_op jit(solution)/shard_map/all_to_all | solution.py:117
  52.8 0.0 copy-done.1
  52.9 0.0 copy-done.2
  52.9 7.8 %shard_map.73 = f32[4,64,256]{2,1,0:T(8,128)} custom-call(s32[12]{0:T(128)S(1)} %copy-done.2, s32[12]{0:T(128)S(1)} %multiply_add_fusion.places_ref, bf16[12,64,4096]{2,1,0:T(8,128)(2,1)} %x_ref.1, bf16[48,64,256]{2,1,0:T(8,128)(2,1)} %bitcast.5.refs_0_.refs_1_.refs_2_.refs_3_, bf16[48,64,256]{2,1,0:T(8,128)(2,1)} %bitcast.5.refs_0_.refs_1_.refs_2_.refs_3_, ...), custom_call_target="tpu_custom_call" | custom-call | flops 1610612736 | bytes 6946816 | tf_op jit(solution)/shard_map/pallas_call | solution.py:52
  60.7 0.6 all-to-all-done.2
  61.3 6.5 %all-to-all-start.3 = ((f32[16,16,256]{2,1,0:T(8,128)}), f32[16,16,256]{2,1,0:T(8,128)S(1)}, u32[]{:S(2)}, u32[]{:S(2)}) async-start(f32[16,16,256]{2,1,0:T(8,128)} %bitcast.8), calls=%async_computation.3 | async-start | bytes 524288 | tf_op jit(solution)/shard_map/all_to_all | solution.py:69
  67.8 0.1 copy.51
  68.0 0.3 abs_reduce_fusion.1
  68.2 0.1 copy.70
  68.4 0.6 reduce_max.18
  69.6 0.3 convolution_subtract_fusion.9
  69.9 0.3 convolution_add_fusion.8
  70.2 0.3 convolution_subtract_fusion.8
  70.5 0.3 convolution_add_fusion.7
  70.7 0.3 convolution_subtract_fusion.7
  71.0 0.3 convolution_add_fusion.6
  71.3 0.3 convolution_subtract_fusion.6
  71.6 0.3 convolution_add_fusion.5
  71.9 0.3 convolution_subtract_fusion.5
  72.2 0.3 convolution_add_fusion.4
  72.5 0.3 convolution_subtract_fusion.4
  72.8 0.3 convolution_add_fusion.3
  73.1 0.3 convolution_subtract_fusion.3
  73.4 0.3 convolution_add_fusion.2
  73.6 0.3 convolution_subtract_fusion.2
  73.9 0.3 convolution_add_fusion.1
  74.2 0.3 convolution_subtract_fusion.1
  74.5 0.3 convolution_add_fusion
  74.8 0.0 copy-start.3
  74.8 2.1 %while.14 = (s32[]{:T(128)}, f32[256,256]{0,1:T(8,128)S(1)}, f32[]{:T(128)}, f32[256,256]{1,0:T(8,128)S(1)}, s32[]{:T(128)}, /*index=5*/f32[]{:T(128)}) while((s32[]{:T(128)}, f32[256,256]{0,1:T(8,128)S(1)}, f32[]{:T(128)}, f32[256,256]{1,0:T(8,128)S(1)}, s32[]{:T(128)}, /*index=5*/f32[]{:T(128)}) %tuple.35), condition=%wide.region_9.0_spmd.clone, body=%wide.region_6.9_spmd.clone.sunk | while | flops 403046400 | bytes 2099289 | solution.py:92
  74.9 0.4 abs_reduce_fusion.3
  75.3 0.6 reduce_max.21
  75.9 0.4 fusion.73
  76.9 0.0 all-to-all-done.3
  77.0 0.0 copy-done.3
  77.0 0.9 %fusion.10 = f32[16,256]{1,0:T(8,128)} fusion(f32[256,256]{0,1:T(8,128)S(1)} %get-tuple-element.48, f32[16,256]{1,0:T(8,128)S(1)} %reduce_sum.57, f32[16,256]{1,0:T(8,128)S(1)} %copy-done.3), kind=kOutput, calls=%fused_computation.38 | convolution fusion | flops 12591104 | bytes 311296 | tf_op jit(solution)/shard_map/dot_general | solution.py:134
  (11 shorter events, 0.1 us)
Async XLA Ops:
  0.0 2.5 %copy-start = (bf16[4096,256]{1,0:T(8,128)(2,1)S(1)}, bf16[4096,256]{1,0:T(8,128)(2,1)}, u32[]{:S(2)}) copy-start(bf16[4096,256]{1,0:T(8,128)(2,1)} %param.15) | copy-start | bytes 6291460
  22.1 30.8 %copy-start.1 = (bf16[64,256]{1,0:T(8,128)(2,1)S(1)}, bf16[64,256]{1,0:T(8,128)(2,1)}, u32[]{:S(2)}) copy-start(bf16[64,256]{1,0:T(8,128)(2,1)} %refs_4_.1) | copy-start | bytes 98308
  22.1 30.8 %copy-start.2 = (s32[12]{0:T(128)S(1)}, s32[12]{0:T(128)}, u32[]{:S(2)}) copy-start(s32[12]{0:T(128)} %rows_ref.1) | copy-start | bytes 148
  22.1 26.5 %all-to-all-start.1 = ((bf16[16,3,64,256]{3,2,1,0:T(8,128)(2,1)}), bf16[16,3,64,256]{3,2,1,0:T(8,128)(2,1)}, u32[]{:S(2)}, u32[]{:S(2)}) async-start(bf16[16,3,64,256]{3,2,1,0:T(8,128)(2,1)} %bitcast.70), calls=%async_computation.1 | async-start | bytes 3145728 | tf_op jit(solution)/shard_map/all_to_all | solution.py:121
  49.3 12.0 %all-to-all-start.2 = ((f32[16,16,256]{2,1,0:T(8,128)}), f32[16,16,256]{2,1,0:T(8,128)S(1)}, u32[]{:S(2)}, u32[]{:S(2)}) async-start(f32[16,16,256]{2,1,0:T(8,128)} %broadcast_in_dim.16), calls=%async_computation.2 | async-start | bytes 524288 | tf_op jit(solution)/shard_map/all_to_all | solution.py:117
  61.3 15.6 %all-to-all-start.3 = ((f32[16,16,256]{2,1,0:T(8,128)}), f32[16,16,256]{2,1,0:T(8,128)S(1)}, u32[]{:S(2)}, u32[]{:S(2)}) async-start(f32[16,16,256]{2,1,0:T(8,128)} %bitcast.8), calls=%async_computation.3 | async-start | bytes 524288 | tf_op jit(solution)/shard_map/all_to_all | solution.py:69
  74.8 2.2 %copy-start.3 = (f32[16,256]{1,0:T(8,128)S(1)}, f32[16,256]{1,0:T(8,128)}, u32[]{:S(2)}) copy-start(f32[16,256]{1,0:T(8,128)} %param.17) | copy-start | bytes 49156

commit v15 on v14

--- a/solution.py
+++ b/solution.py
@@ -70,6 +70,17 @@
     return jnp.sum(arrived, axis=0)
 
 
+def exchange(pieces, peers):
+    me = lax.axis_index("dst")
+    got = [pieces[me][None]]
+    for shift in range(1, peers):
+        outgoing = lax.dynamic_index_in_dim(pieces, (me + shift) % peers, axis=0, keepdims=True)
+        pairs = [(i, (i + shift) % peers) for i in range(peers)]
+        got.append(lax.ppermute(outgoing, "dst", perm=pairs))
+    by_shift = jnp.concatenate(got, axis=0)
+    return jnp.take(by_shift, (me - jnp.arange(peers)) % peers, axis=0)
+
+
 def ridge_inverse(gram):
     eye = jnp.eye(gram.shape[0], dtype=jnp.float32)
     start = eye / jnp.max(jnp.sum(jnp.abs(gram), axis=1))
@@ -110,7 +121,7 @@
     chunk = local_gram.shape[0] // peers
     asked_row = jnp.zeros((peers, 1, width), jnp.float32).at[:, 0, :depth].set(requests.astype(jnp.float32))
     first = jnp.concatenate([local_gram.reshape(peers, chunk, width), asked_row], axis=1)
-    first = lax.all_to_all(first, "dst", split_axis=0, concat_axis=0, tiled=True)
+    first = exchange(first, peers)
     gram_rows = jnp.sum(first[:, :chunk, :], axis=0)
     asked = first[:, chunk, :depth].astype(jnp.int32)
     spread = jnp.broadcast_to(gram_rows[None], (peers, chunk, width))

time: 78.7 us -> 138 us (1.75)
  waiting for transfers between devices: 22.6 us -> 85.7 us
  blocking collectives: 16.8 us -> 0 us
  starting transfers between devices: 14.6 us -> 26.4 us
    ppermute x0 -> x15, waiting for transfers between devices: none -> 67.3 us  [exchange(): got.append(lax.ppermute(outgoing, 'dst', perm=pairs))]
    all_to_all x1 -> x0, blocking collectives: 16.8 us -> none  [shards(): lax.all_to_all(first, 'dst', split_axis=0, concat_axis=0, tiled=True)]
    ppermute x0 -> x15, starting transfers between devices: none -> 10.1 us  [exchange(): got.append(lax.ppermute(outgoing, 'dst', perm=pairs))]
    all_to_all x1, waiting for transfers between devices: 21.9 us -> 17.7 us  [shards(): lax.all_to_all(outgoing, 'dst', split_axis=0, concat_axis=0, tiled=True)]
    all_to_all x1, starting transfers between devices: 4.52 us -> 6.25 us  [shards(): lax.all_to_all(outgoing, 'dst', split_axis=0, concat_axis=0, tiled=True)]
  transfers between devices with their start and end apart: 3 -> 18, of which waited for: 2 -> 13; matrix products, arithmetic and copies ran while one was open for 10% -> 6% of each run, Pallas kernels for 10% -> 6%
where the time goes in v15:
time: 138 us; the launch traced here: 137 us
  waiting for transfers between devices  85.7 us (62%)
  starting transfers between devices  26.4 us (19%)
  matrix products  7.82 us (6%)
  Pallas kernels  7.79 us (6%)
  other arithmetic  3.88 us (3%)
  local copies, waits for them, and re-layouts  3.77 us (3%)
    ppermute x15, waiting for transfers between devices, exchange(): got.append(lax.ppermute(outgoing, 'dst', perm=pairs))  67.3 us
    all_to_all x1, waiting for transfers between devices, shards(): lax.all_to_all(outgoing, 'dst', split_axis=0, concat_axis=0, tiled=True)  17.7 us
    ppermute x15, starting transfers between devices, exchange(): got.append(lax.ppermute(outgoing, 'dst', perm=pairs))  10.1 us
    pallas_call x1, Pallas kernels, block_products(): pl.pallas_call(mttkrp_kernel, grid_spec=grid_spec, out_shape=jax.ShapeDty...  7.79 us
    all_to_all x1, starting transfers between devices, scatter_sum(): lax.all_to_all(pieces, 'dst', split_axis=0, concat_axis=0, tiled=True)  6.54 us
    all_to_all x1, starting transfers between devices, shards(): lax.all_to_all(outgoing, 'dst', split_axis=0, concat_axis=0, tiled=True)  6.25 us
    all_to_all x1, starting transfers between devices, shards(): lax.all_to_all(spread, 'dst', split_axis=0, concat_axis=0, tiled=True)  3.53 us
  transfers between devices with their start and end apart: 18, of which 13 were waited for; matrix products, arithmetic and copies ran while one was open for 6% of the time, Pallas kernels for 6%

profile of v15, /device:TPU:0, one launch (start us, length us, event | category | flops | bytes accessed | tf_op | source)
XLA Modules:
  0.0 137.1 jit_solution(10198524131143290798)
XLA Ops:
  0.0 1.0 convert_reduce_fusion
  1.0 0.7 multiply_add_fusion.places_ref
  1.7 0.7 select_reduce_fusion
  2.5 0.7 fusion.23
  3.5 5.4 %collective-permute-start.14 = (f32[1,17,256]{2,1,0:T(8,128)S(1)}, f32[1,17,256]{2,1,0:T(8,128)S(1)}, u32[]{:S(2)}, u32[]{:S(2)}) collective-permute-start(f32[1,17,256]{2,1,0:T(8,128)S(1)} %get-tuple-element.81), channel_id=1, source_target_pairs={{0,15},{1,0},{2,1},{3,2},{4,3},{5,4},{6,5},{7,6},{8,7},{9,8},{10,9... | collective-permute-start | bytes 52232 | tf_op jit(solution)/shard_map/ppermute | solution.py:79
  8.9 0.6 collective-permute-start.13
  9.5 1.2 collective-permute-start.12
  10.7 0.5 collective-permute-start.11
  11.3 1.9 %collective-permute-start = (f32[1,17,256]{2,1,0:T(8,128)S(1)}, f32[1,17,256]{2,1,0:T(8,128)S(1)}, u32[]{:S(2)}, u32[]{:S(2)}) collective-permute-start(f32[1,17,256]{2,1,0:T(8,128)S(1)} %get-tuple-element.95), channel_id=1, source_target_pairs={{0,1},{1,2},{2,3},{3,4},{4,5},{5,6},{6,7},{7,8},{8,9},{9,10},{10,1... | collective-permute-start | bytes 52232 | tf_op jit(solution)/shard_map/ppermute | solution.py:79
  13.2 5.2 %collective-permute-done = f32[1,17,256]{2,1,0:T(8,128)S(1)} collective-permute-done((f32[1,17,256]{2,1,0:T(8,128)S(1)}, f32[1,17,256]{2,1,0:T(8,128)S(1)}, u32[]{:S(2)}, u32[]{:S(2)}) %collective-permute-start) | collective-permute-done | bytes 17440 | tf_op jit(solution)/shard_map/ppermute | solution.py:79
  18.4 7.7 %collective-permute-done.1 = f32[1,17,256]{2,1,0:T(8,128)S(1)} collective-permute-done((f32[1,17,256]{2,1,0:T(8,128)S(1)}, f32[1,17,256]{2,1,0:T(8,128)S(1)}, u32[]{:S(2)}, u32[]{:S(2)}) %collective-permute-start.1) | collective-permute-done | bytes 17440 | tf_op jit(solution)/shard_map/ppermute | solution.py:79
  26.1 5.9 %collective-permute-done.2 = f32[1,17,256]{2,1,0:T(8,128)S(1)} collective-permute-done((f32[1,17,256]{2,1,0:T(8,128)S(1)}, f32[1,17,256]{2,1,0:T(8,128)S(1)}, u32[]{:S(2)}, u32[]{:S(2)}) %collective-permute-start.2) | collective-permute-done | bytes 17440 | tf_op jit(solution)/shard_map/ppermute | solution.py:79
  32.1 5.0 %collective-permute-done.3 = f32[1,17,256]{2,1,0:T(8,128)S(1)} collective-permute-done((f32[1,17,256]{2,1,0:T(8,128)S(1)}, f32[1,17,256]{2,1,0:T(8,128)S(1)}, u32[]{:S(2)}, u32[]{:S(2)}) %collective-permute-start.3) | collective-permute-done | bytes 17440 | tf_op jit(solution)/shard_map/ppermute | solution.py:79
  37.1 7.4 %collective-permute-done.4 = f32[1,17,256]{2,1,0:T(8,128)S(1)} collective-permute-done((f32[1,17,256]{2,1,0:T(8,128)S(1)}, f32[1,17,256]{2,1,0:T(8,128)S(1)}, u32[]{:S(2)}, u32[]{:S(2)}) %collective-permute-start.4) | collective-permute-done | bytes 17440 | tf_op jit(solution)/shard_map/ppermute | solution.py:79
  44.5 7.7 %collective-permute-done.5 = f32[1,17,256]{2,1,0:T(8,128)S(1)} collective-permute-done((f32[1,17,256]{2,1,0:T(8,128)S(1)}, f32[1,17,256]{2,1,0:T(8,128)S(1)}, u32[]{:S(2)}, u32[]{:S(2)}) %collective-permute-start.5) | collective-permute-done | bytes 17440 | tf_op jit(solution)/shard_map/ppermute | solution.py:79
  52.3 6.2 %collective-permute-done.6 = f32[1,17,256]{2,1,0:T(8,128)S(1)} collective-permute-done((f32[1,17,256]{2,1,0:T(8,128)S(1)}, f32[1,17,256]{2,1,0:T(8,128)S(1)}, u32[]{:S(2)}, u32[]{:S(2)}) %collective-permute-start.6) | collective-permute-done | bytes 17440 | tf_op jit(solution)/shard_map/ppermute | solution.py:79
  58.5 5.3 %collective-permute-done.7 = f32[1,17,256]{2,1,0:T(8,128)S(1)} collective-permute-done((f32[1,17,256]{2,1,0:T(8,128)S(1)}, f32[1,17,256]{2,1,0:T(8,128)S(1)}, u32[]{:S(2)}, u32[]{:S(2)}) %collective-permute-start.7) | collective-permute-done | bytes 17440 | tf_op jit(solution)/shard_map/ppermute | solution.py:79
  63.8 5.9 %collective-permute-done.8 = f32[1,17,256]{2,1,0:T(8,128)S(1)} collective-permute-done((f32[1,17,256]{2,1,0:T(8,128)S(1)}, f32[1,17,256]{2,1,0:T(8,128)S(1)}, u32[]{:S(2)}, u32[]{:S(2)}) %collective-permute-start.8) | collective-permute-done | bytes 17440 | tf_op jit(solution)/shard_map/ppermute | solution.py:79
  69.8 6.2 %collective-permute-done.9 = f32[1,17,256]{2,1,0:T(8,128)S(1)} collective-permute-done((f32[1,17,256]{2,1,0:T(8,128)S(1)}, f32[1,17,256]{2,1,0:T(8,128)S(1)}, u32[]{:S(2)}, u32[]{:S(2)}) %collective-permute-start.9) | collective-permute-done | bytes 17440 | tf_op jit(solution)/shard_map/ppermute | solution.py:79
  76.0 0.4 collective-permute-start.10
  76.4 4.6 %collective-permute-done.10 = f32[1,17,256]{2,1,0:T(8,128)S(1)} collective-permute-done((f32[1,17,256]{2,1,0:T(8,128)S(1)}, f32[1,17,256]{2,1,0:T(8,128)S(1)}, u32[]{:S(2)}, u32[]{:S(2)}) %collective-permute-start.10) | collective-permute-done | bytes 17440 | tf_op jit(solution)/shard_map/ppermute | solution.py:79
  81.1 0.6 gather_fusion
  81.9 1.9 %gather_fusion.1 = bf16[48,64,256]{2,1,0:T(8,128)(2,1)} fusion(bf16[64,64,256]{2,1,0:T(8,128)(2,1)S(1)} %bitcast.71, s32[1024]{0:T(1024)S(1)} %pad_clamp_fusion), kind=kCustom, calls=%fused_computation.1 | custom fusion | bytes 3145920 | tf_op jit(solution)/shard_map/gather | solution.py:131
  83.8 6.2 %all-to-all-start = ((bf16[16,3,64,256]{3,2,1,0:T(8,128)(2,1)}), bf16[16,3,64,256]{3,2,1,0:T(8,128)(2,1)}, u32[]{:S(2)}, u32[]{:S(2)}) async-start(bf16[16,3,64,256]{3,2,1,0:T(8,128)(2,1)} %bitcast.72), calls=%async_computation | async-start | bytes 3145728 | tf_op jit(solution)/shard_map/all_to_all | solution.py:132
  90.1 17.7 %all-to-all-done = bf16[16,3,64,256]{3,2,1,0:T(8,128)(2,1)} async-done(((bf16[16,3,64,256]{3,2,1,0:T(8,128)(2,1)}), bf16[16,3,64,256]{3,2,1,0:T(8,128)(2,1)}, u32[]{:S(2)}, u32[]{:S(2)}) %all-to-all-start) | async-done | bytes 1572896 | tf_op jit(solution)/shard_map/all_to_all | solution.py:132
  107.8 0.7 broadcast_in_dim.39
  108.5 3.5 %all-to-all-start.1 = ((f32[16,16,256]{2,1,0:T(8,128)}), f32[16,16,256]{2,1,0:T(8,128)S(1)}, u32[]{:S(2)}, u32[]{:S(2)}) async-start(f32[16,16,256]{2,1,0:T(8,128)} %broadcast_in_dim.39), calls=%async_computation.1 | async-start | bytes 524288 | tf_op jit(solution)/shard_map/all_to_all | solution.py:128
  112.1 7.8 %shard_map.73 = f32[4,64,256]{2,1,0:T(8,128)} custom-call(s32[12]{0:T(128)S(1)} %copy-done.2, s32[12]{0:T(128)S(1)} %multiply_add_fusion.places_ref, bf16[12,64,4096]{2,1,0:T(8,128)(2,1)} %x_ref.1, bf16[48,64,256]{2,1,0:T(8,128)(2,1)} %bitcast.7.refs_0_.refs_1_.refs_2_.refs_3_, bf16[48,64,256]{2,1,0:T(8,128)(2,1)} %bitcast.7.refs_0_.refs_1_.refs_2_.refs_3_, ...), custom_call_target="tpu_custom_call" | custom-call | flops 1610612736 | bytes 6946816 | tf_op jit(solution)/shard_map/pallas_call | solution.py:52
  119.9 0.6 all-to-all-done.1
  120.5 6.5 %all-to-all-start.2 = ((f32[16,16,256]{2,1,0:T(8,128)}), f32[16,16,256]{2,1,0:T(8,128)S(1)}, u32[]{:S(2)}, u32[]{:S(2)}) async-start(f32[16,16,256]{2,1,0:T(8,128)} %bitcast.10), calls=%async_computation.2 | async-start | bytes 524288 | tf_op jit(solution)/shard_map/all_to_all | solution.py:69
  127.6 0.7 reduce_max.18
  128.9 0.3 convolution_subtract_fusion.9
  129.2 0.3 convolution_add_fusion.8
  129.5 0.3 convolution_subtract_fusion.8
  129.8 0.3 convolution_add_fusion.7
  130.6 0.3 convolution_subtract_fusion.6
  130.9 0.3 convolution_add_fusion.5
  131.2 0.3 convolution_subtract_fusion.5
  132.1 0.3 convolution_add_fusion.3
  132.4 0.3 convolution_subtract_fusion.3
  132.7 0.3 convolution_add_fusion.2
  133.5 0.3 convolution_subtract_fusion.1
  133.8 0.3 convolution_add_fusion
  134.1 2.0 %while.14 = (s32[]{:T(128)}, f32[256,256]{0,1:T(8,128)S(1)}, f32[]{:T(128)}, f32[256,256]{1,0:T(8,128)S(1)}, s32[]{:T(128)}, /*index=5*/f32[]{:T(128)}) while((s32[]{:T(128)}, f32[256,256]{0,1:T(8,128)S(1)}, f32[]{:T(128)}, f32[256,256]{1,0:T(8,128)S(1)}, s32[]{:T(128)}, /*index=5*/f32[]{:T(128)}) %tuple.49), condition=%wide.region_9.10_spmd.clone, body=%wide.region_6.9_spmd.clone.sunk | while | flops 403046400 | bytes 2099289 | solution.py:103
  134.2 0.4 abs_reduce_fusion.3
  134.6 0.6 reduce_max.21
  135.2 0.4 fusion.76
  136.2 0.9 fusion.10
  (61 shorter events, 2.8 us)
Async XLA Ops:
  0.0 2.5 %copy-start = (bf16[4096,256]{1,0:T(8,128)(2,1)S(1)}, bf16[4096,256]{1,0:T(8,128)(2,1)}, u32[]{:S(2)}) copy-start(bf16[4096,256]{1,0:T(8,128)(2,1)} %param.15) | copy-start | bytes 6291460
  3.5 77.6 %collective-permute-start.14 = (f32[1,17,256]{2,1,0:T(8,128)S(1)}, f32[1,17,256]{2,1,0:T(8,128)S(1)}, u32[]{:S(2)}, u32[]{:S(2)}) collective-permute-start(f32[1,17,256]{2,1,0:T(8,128)S(1)} %get-tuple-element.81), channel_id=1, source_target_pairs={{0,15},{1,0},{2,1},{3,2},{4,3},{5,4},{6,5},{7,6},{8,7},{9,8},{10,9... | collective-permute-start | bytes 52232 | tf_op jit(solution)/shard_map/ppermute | solution.py:79
  8.9 72.2 %collective-permute-start.13 = (f32[1,17,256]{2,1,0:T(8,128)S(1)}, f32[1,17,256]{2,1,0:T(8,128)S(1)}, u32[]{:S(2)}, u32[]{:S(2)}) collective-permute-start(f32[1,17,256]{2,1,0:T(8,128)S(1)} %get-tuple-element.82), channel_id=1, source_target_pairs={{0,14},{1,15},{2,0},{3,1},{4,2},{5,3},{6,4},{7,5},{8,6},{9,7},{10,... | collective-permute-start | bytes 52232 | tf_op jit(solution)/shard_map/ppermute | solution.py:79
  9.5 71.5 %collective-permute-start.12 = (f32[1,17,256]{2,1,0:T(8,128)S(1)}, f32[1,17,256]{2,1,0:T(8,128)S(1)}, u32[]{:S(2)}, u32[]{:S(2)}) collective-permute-start(f32[1,17,256]{2,1,0:T(8,128)S(1)} %get-tuple-element.83), channel_id=1, source_target_pairs={{0,13},{1,14},{2,15},{3,0},{4,1},{5,2},{6,3},{7,4},{8,5},{9,6},{10... | collective-permute-start | bytes 52232 | tf_op jit(solution)/shard_map/ppermute | solution.py:79
  10.7 70.3 %collective-permute-start.11 = (f32[1,17,256]{2,1,0:T(8,128)S(1)}, f32[1,17,256]{2,1,0:T(8,128)S(1)}, u32[]{:S(2)}, u32[]{:S(2)}) collective-permute-start(f32[1,17,256]{2,1,0:T(8,128)S(1)} %get-tuple-element.84), channel_id=1, source_target_pairs={{0,12},{1,13},{2,14},{3,15},{4,0},{5,1},{6,2},{7,3},{8,4},{9,5},{1... | collective-permute-start | bytes 52232 | tf_op jit(solution)/shard_map/ppermute | solution.py:79
  11.3 7.1 %collective-permute-start = (f32[1,17,256]{2,1,0:T(8,128)S(1)}, f32[1,17,256]{2,1,0:T(8,128)S(1)}, u32[]{:S(2)}, u32[]{:S(2)}) collective-permute-start(f32[1,17,256]{2,1,0:T(8,128)S(1)} %get-tuple-element.95), channel_id=1, source_target_pairs={{0,1},{1,2},{2,3},{3,4},{4,5},{5,6},{6,7},{7,8},{8,9},{9,10},{10,1... | collective-permute-start | bytes 52232 | tf_op jit(solution)/shard_map/ppermute | solution.py:79
  18.4 7.7 %collective-permute-start.1 = (f32[1,17,256]{2,1,0:T(8,128)S(1)}, f32[1,17,256]{2,1,0:T(8,128)S(1)}, u32[]{:S(2)}, u32[]{:S(2)}) collective-permute-start(f32[1,17,256]{2,1,0:T(8,128)S(1)} %get-tuple-element.94), channel_id=1, source_target_pairs={{0,2},{1,3},{2,4},{3,5},{4,6},{5,7},{6,8},{7,9},{8,10},{9,11},{10,... | collective-permute-start | bytes 52232 | tf_op jit(solution)/shard_map/ppermute | solution.py:79
  26.1 5.9 %collective-permute-start.2 = (f32[1,17,256]{2,1,0:T(8,128)S(1)}, f32[1,17,256]{2,1,0:T(8,128)S(1)}, u32[]{:S(2)}, u32[]{:S(2)}) collective-permute-start(f32[1,17,256]{2,1,0:T(8,128)S(1)} %get-tuple-element.93), channel_id=1, source_target_pairs={{0,3},{1,4},{2,5},{3,6},{4,7},{5,8},{6,9},{7,10},{8,11},{9,12},{10... | collective-permute-start | bytes 52232 | tf_op jit(solution)/shard_map/ppermute | solution.py:79
  32.1 5.0 %collective-permute-start.3 = (f32[1,17,256]{2,1,0:T(8,128)S(1)}, f32[1,17,256]{2,1,0:T(8,128)S(1)}, u32[]{:S(2)}, u32[]{:S(2)}) collective-permute-start(f32[1,17,256]{2,1,0:T(8,128)S(1)} %get-tuple-element.92), channel_id=1, source_target_pairs={{0,4},{1,5},{2,6},{3,7},{4,8},{5,9},{6,10},{7,11},{8,12},{9,13},{1... | collective-permute-start | bytes 52232 | tf_op jit(solution)/shard_map/ppermute | solution.py:79
  37.1 7.4 %collective-permute-start.4 = (f32[1,17,256]{2,1,0:T(8,128)S(1)}, f32[1,17,256]{2,1,0:T(8,128)S(1)}, u32[]{:S(2)}, u32[]{:S(2)}) collective-permute-start(f32[1,17,256]{2,1,0:T(8,128)S(1)} %get-tuple-element.91), channel_id=1, source_target_pairs={{0,5},{1,6},{2,7},{3,8},{4,9},{5,10},{6,11},{7,12},{8,13},{9,14},{... | collective-permute-start | bytes 52232 | tf_op jit(solution)/shard_map/ppermute | solution.py:79
  44.5 7.7 %collective-permute-start.5 = (f32[1,17,256]{2,1,0:T(8,128)S(1)}, f32[1,17,256]{2,1,0:T(8,128)S(1)}, u32[]{:S(2)}, u32[]{:S(2)}) collective-permute-start(f32[1,17,256]{2,1,0:T(8,128)S(1)} %get-tuple-element.90), channel_id=1, source_target_pairs={{0,6},{1,7},{2,8},{3,9},{4,10},{5,11},{6,12},{7,13},{8,14},{9,15},... | collective-permute-start | bytes 52232 | tf_op jit(solution)/shard_map/ppermute | solution.py:79
  52.3 6.2 %collective-permute-start.6 = (f32[1,17,256]{2,1,0:T(8,128)S(1)}, f32[1,17,256]{2,1,0:T(8,128)S(1)}, u32[]{:S(2)}, u32[]{:S(2)}) collective-permute-start(f32[1,17,256]{2,1,0:T(8,128)S(1)} %get-tuple-element.89), channel_id=1, source_target_pairs={{0,7},{1,8},{2,9},{3,10},{4,11},{5,12},{6,13},{7,14},{8,15},{9,0},... | collective-permute-start | bytes 52232 | tf_op jit(solution)/shard_map/ppermute | solution.py:79
  58.5 5.3 %collective-permute-start.7 = (f32[1,17,256]{2,1,0:T(8,128)S(1)}, f32[1,17,256]{2,1,0:T(8,128)S(1)}, u32[]{:S(2)}, u32[]{:S(2)}) collective-permute-start(f32[1,17,256]{2,1,0:T(8,128)S(1)} %get-tuple-element.88), channel_id=1, source_target_pairs={{0,8},{1,9},{2,10},{3,11},{4,12},{5,13},{6,14},{7,15},{8,0},{9,1},... | collective-permute-start | bytes 52232 | tf_op jit(solution)/shard_map/ppermute | solution.py:79
  63.8 5.9 %collective-permute-start.8 = (f32[1,17,256]{2,1,0:T(8,128)S(1)}, f32[1,17,256]{2,1,0:T(8,128)S(1)}, u32[]{:S(2)}, u32[]{:S(2)}) collective-permute-start(f32[1,17,256]{2,1,0:T(8,128)S(1)} %get-tuple-element.87), channel_id=1, source_target_pairs={{0,9},{1,10},{2,11},{3,12},{4,13},{5,14},{6,15},{7,0},{8,1},{9,2},... | collective-permute-start | bytes 52232 | tf_op jit(solution)/shard_map/ppermute | solution.py:79
  69.8 6.2 %collective-permute-start.9 = (f32[1,17,256]{2,1,0:T(8,128)S(1)}, f32[1,17,256]{2,1,0:T(8,128)S(1)}, u32[]{:S(2)}, u32[]{:S(2)}) collective-permute-start(f32[1,17,256]{2,1,0:T(8,128)S(1)} %get-tuple-element.86), channel_id=1, source_target_pairs={{0,10},{1,11},{2,12},{3,13},{4,14},{5,15},{6,0},{7,1},{8,2},{9,3},... | collective-permute-start | bytes 52232 | tf_op jit(solution)/shard_map/ppermute | solution.py:79
  76.0 5.0 %collective-permute-start.10 = (f32[1,17,256]{2,1,0:T(8,128)S(1)}, f32[1,17,256]{2,1,0:T(8,128)S(1)}, u32[]{:S(2)}, u32[]{:S(2)}) collective-permute-start(f32[1,17,256]{2,1,0:T(8,128)S(1)} %get-tuple-element.85), channel_id=1, source_target_pairs={{0,11},{1,12},{2,13},{3,14},{4,15},{5,0},{6,1},{7,2},{8,3},{9,4},{... | collective-permute-start | bytes 52232 | tf_op jit(solution)/shard_map/ppermute | solution.py:79
  83.8 28.3 %copy-start.1 = (bf16[64,256]{1,0:T(8,128)(2,1)S(1)}, bf16[64,256]{1,0:T(8,128)(2,1)}, u32[]{:S(2)}) copy-start(bf16[64,256]{1,0:T(8,128)(2,1)} %refs_4_.1) | copy-start | bytes 98308
  83.8 28.3 %copy-start.2 = (s32[12]{0:T(128)S(1)}, s32[12]{0:T(128)}, u32[]{:S(2)}) copy-start(s32[12]{0:T(128)} %rows_ref.1) | copy-start | bytes 148
  83.8 24.0 %all-to-all-start = ((bf16[16,3,64,256]{3,2,1,0:T(8,128)(2,1)}), bf16[16,3,64,256]{3,2,1,0:T(8,128)(2,1)}, u32[]{:S(2)}, u32[]{:S(2)}) async-start(bf16[16,3,64,256]{3,2,1,0:T(8,128)(2,1)} %bitcast.72), calls=%async_computation | async-start | bytes 3145728 | tf_op jit(solution)/shard_map/all_to_all | solution.py:132
  108.5 12.0 %all-to-all-start.1 = ((f32[16,16,256]{2,1,0:T(8,128)}), f32[16,16,256]{2,1,0:T(8,128)S(1)}, u32[]{:S(2)}, u32[]{:S(2)}) async-start(f32[16,16,256]{2,1,0:T(8,128)} %broadcast_in_dim.39), calls=%async_computation.1 | async-start | bytes 524288 | tf_op jit(solution)/shard_map/all_to_all | solution.py:128
  120.5 15.6 %all-to-all-start.2 = ((f32[16,16,256]{2,1,0:T(8,128)}), f32[16,16,256]{2,1,0:T(8,128)S(1)}, u32[]{:S(2)}, u32[]{:S(2)}) async-start(f32[16,16,256]{2,1,0:T(8,128)} %bitcast.10), calls=%async_computation.2 | async-start | bytes 524288 | tf_op jit(solution)/shard_map/all_to_all | solution.py:69
  134.1 2.0 %copy-start.3 = (f32[16,256]{1,0:T(8,128)S(1)}, f32[16,256]{1,0:T(8,128)}, u32[]{:S(2)}) copy-start(f32[16,256]{1,0:T(8,128)} %param.17) | copy-start | bytes 49156
